TPU v7x, 32 devices: a whole 2x2x4 slice. The times are simulated.
32 devices in a mesh: vert: 16 (over z, y, x), eig: 2 (over core).
Axes of the slice: x: 2, y: 2, z: 4, core: 2. Of those that a mesh axis runs over, the one named last changes fastest.
Arguments:
- eig_table: bfloat16 [32768, 2048], P('vert', 'eig'), may hold values from -0.1875 to 0.1875
- obs_ids: int32 [49152], P('vert'), may hold values from 0 to 2047
- counts: int32 [16], P('vert'), may hold values from 512 to 3072, as said below
- noise_var: float32 [49152], P('vert'), may hold values from 0.05 to 0.5
- eigenvalues: float32 [2048], P('eig'), may hold values from 0.01 to 4
- rhs: float32 [256, 49152], P('eig', 'vert'), may hold values from -6 to 6
Outputs:
- solution: float32 [256, 49152], P('eig', 'vert')
- residual: float32 [256, 49152], P('eig', 'vert')
Inputs may be any that keep to these rules, and one draw needn't show every extreme that they name: `counts`: slots of a shard are filled from its first slot on; the busiest shard fills all 3072.
All inputs are finite; a program needn't handle non-finite values.
Results may differ from a plain program's by a relative error of at most 0.039.
Values may be sent and summed in bfloat16 or wider, within the bound.
No kernel may reach another device: no remote copies, remote signals or barrier semaphores. Data moves between devices by JAX's collectives and lax.ppermute only.
A program may use at most 64 MiB of HBM per device.

v0:
```python
import jax
import jax.numpy as jnp
from jax import lax
from jax.sharding import PartitionSpec as P

ITERS = 2


def shards(eig_table, obs_ids, counts, noise_var, eigenvalues, rhs):
    capacity = obs_ids.shape[0]
    filled = jnp.arange(capacity, dtype=jnp.int32) < counts[0]
    features = jnp.where(
        filled[:, None], jnp.take(eig_table, obs_ids, axis=0), jnp.zeros((), jnp.bfloat16)
    )
    spectrum = 5.0 * jnp.power(3.0 + eigenvalues, -1.5)

    def project(shard_rows):
        return jnp.dot(shard_rows, features, preferred_element_type=jnp.float32)

    def operate(vector):
        lowered = vector.astype(jnp.bfloat16)
        coeff = project(lax.all_gather(lowered, "eig", axis=0, tiled=True))
        summed = lax.psum(coeff, "vert")
        weights = (summed * spectrum[None, :]).astype(jnp.bfloat16)
        applied = lax.psum_scatter(
            lax.dot_general(
                weights, features, (((1,), (1,)), ((), ())), preferred_element_type=jnp.float32
            ).astype(jnp.bfloat16),
            "eig",
            scatter_dimension=0,
            tiled=True,
        ).astype(jnp.float32)
        return applied + noise_var[None, :] * vector

    def two_products(vector, applied):
        return lax.psum(
            (jnp.sum(vector * vector, axis=1), jnp.sum(vector * applied, axis=1)), "vert"
        )

    residual = jnp.where(filled[None, :], rhs, jnp.zeros((), jnp.float32))
    solution = jnp.zeros_like(residual)
    applied = operate(residual)
    norm_now, product = two_products(residual, applied)
    step_size = norm_now / product
    direction, along = (residual, applied)
    for iteration in range(ITERS):
        solution = solution + step_size[:, None] * direction
        residual = residual - step_size[:, None] * along
        if iteration + 1 < ITERS:
            applied = operate(residual)
            norm_next, product = two_products(residual, applied)
            beta_ratio = norm_next / norm_now
            step_size = norm_next / (product - beta_ratio * norm_next / step_size)
            direction = residual + beta_ratio[:, None] * direction
            along = applied + beta_ratio[:, None] * along
            norm_now = norm_next
    return (solution, residual)


def solution(mesh):
    return jax.shard_map(
        shards,
        mesh=mesh,
        in_specs=(P("vert", "eig"), P("vert"), P("vert"), P("vert"), P("eig"), P("eig", "vert")),
        out_specs=(P("eig", "vert"), P("eig", "vert")),
        check_vma=False,
    )
```

profile of v0, /device:TPU:0, one launch (start us, length us, event | category | flops | bytes accessed | tf_op | source)
XLA Modules:
  0.0 410.4 jit_solution(9690774962889516691)
XLA Ops:
  7.2 0.0 all-gather.3.cloned.1.call-start
  7.9 0.0 copy-start.4
  7.9 2.4 select_convert_fusion
  10.3 0.0 all-gather.3.cloned.1.call-update
  10.3 0.0 all-reduce.5.cloned.1.call-start
  10.4 0.0 copy-done.4
  10.4 18.7 %gather_fusion = bf16[3072,1024]{1,0:T(8,128)(2,1)} fusion(bf16[2048,1024]{1,0:T(8,128)(2,1)} %param.6, s32[3072]{0:T(1024)S(1)} %fusion.2), kind=kCustom, calls=%fused_computation | custom fusion | bytes 12595200 | tf_op jit(solution)/shard_map/jit(_take)/gather | solution.py:13
  29.1 6.8 %select_select_fusion = bf16[3072,1024]{1,0:T(8,128)(2,1)} fusion(bf16[3072,1024]{1,0:T(8,128)(2,1)} %gather_fusion, pred[3072]{0:T(1024)(128)(4,1)S(1)} %compare_and_fusion, pred[3072]{0:T(1024)(128)(4,1)S(1)} %iota_compare_fusion), kind=kLoop, calls=%fused_computation.1 | loop fusion | flops 6291456 | bytes 12589056 | tf_op jit(solution)/shard_map/jit(_where)/select_n | solution.py:12
  35.9 0.0 copy-start.5
  35.9 0.0 all-gather.3.cloned.1.call-done
  35.9 6.0 %fusion.4 = f32[256,1024]{1,0:T(8,128)} fusion(bf16[256,3072]{1,0:T(8,128)(2,1)} %all-gather.3.cloned.1.call-done, bf16[3072,1024]{1,0:T(8,128)(2,1)} %select_select_fusion), kind=kOutput, calls=%fused_computation.25 | convolution fusion | flops 1610612736 | bytes 8912896 | tf_op jit(solution)/shard_map/dot_general | solution.py:18
  42.0 0.0 all-reduce.5.cloned.1.call-update
  42.0 0.0 reduce-scatter.3.cloned.1.call-start
  42.0 0.0 copy-done.5
  42.1 115.3 %all-reduce.5.cloned.1.call-done = f32[256,1024]{1,0:T(8,128)} async-done(((f32[256,1024]{1,0:T(8,128)}), f32[256,1024]{1,0:T(8,128)}) %all-reduce.5.cloned.1.call-update) | async-done | bytes 1048592 | tf_op jit(solution)/shard_map/psum | solution.py:23
  157.3 0.0 copy-start.3
  157.3 6.1 %convolution_convert_fusion.1 = bf16[256,3072]{1,0:T(8,128)(2,1)} fusion(bf16[3072,1024]{1,0:T(8,128)(2,1)} %select_select_fusion, f32[256,1024]{1,0:T(8,128)} %all-reduce.5.cloned.1.call-done, f32[1024]{0:T(1024)S(1)} %power_multiply_fusion), kind=kOutput, calls=%fused_computation.3 | convolution fusion | flops 1611923456 | bytes 8916992 | tf_op jit(solution)/shard_map/dot_general | solution.py:26
  163.4 0.0 copy-start
  163.5 0.0 reduce-scatter.3.cloned.1.call-update
  163.5 0.0 all-gather.5.cloned.1.call-start
  163.5 8.2 %reduce-scatter.3.cloned.1.call-done = bf16[128,3072]{1,0:T(8,128)(2,1)} async-done(((bf16[256,3072]{1,0:T(8,128)(2,1)}), bf16[128,3072]{1,0:T(8,128)(2,1)}) %reduce-scatter.3.cloned.1.call-update) | async-done | bytes 786448 | tf_op jit(solution)/shard_map/reduce_scatter | solution.py:25
  171.8 0.0 copy-done.3
  171.8 0.0 copy-done
  171.8 0.0 copy-start.1
  171.8 1.7 multiply_reduce_fusion.2
  173.5 42.1 %all-reduce.1 = (f32[128]{0:T(128)S(1)}, f32[128]{0:T(128)S(1)}) all-reduce(f32[128]{0:T(128)S(1)} %get-tuple-element.5, f32[128]{0:T(128)S(1)} %get-tuple-element.4), channel_id=1, replica_groups=mesh['vert'=16,'eig'=2] {'vert'}, use_global_device_ids=true, to_apply=%region_1.2 | all-reduce | flops 256 | bytes 2048 | tf_op jit(solution)/shard_map/psum | solution.py:36
  215.6 0.0 copy-done.1
  215.6 1.2 fusion.3
  216.8 0.0 all-gather.5.cloned.1.call-update
  216.9 0.0 all-reduce.7.cloned.1.call-start
  216.9 5.8 %all-gather.5.cloned.1.call-done = bf16[256,3072]{1,0:T(8,128)(2,1)} async-done(((bf16[128,3072]{1,0:T(8,128)(2,1)}), bf16[256,3072]{1,0:T(8,128)(2,1)}) %all-gather.5.cloned.1.call-update) | async-done | bytes 1572880 | tf_op jit(solution)/shard_map/all_gather | solution.py:22
  222.7 6.0 %fusion.5 = f32[256,1024]{1,0:T(8,128)} fusion(bf16[256,3072]{1,0:T(8,128)(2,1)} %all-gather.5.cloned.1.call-done, bf16[3072,1024]{1,0:T(8,128)(2,1)} %select_select_fusion), kind=kOutput, calls=%fused_computation.26 | convolution fusion | flops 1610612736 | bytes 8912896 | tf_op jit(solution)/shard_map/dot_general | solution.py:18
  228.7 0.0 all-reduce.7.cloned.1.call-update
  228.7 0.0 reduce-scatter.5.cloned.1.call-start
  228.8 113.6 %all-reduce.7.cloned.1.call-done = f32[256,1024]{1,0:T(8,128)} async-done(((f32[256,1024]{1,0:T(8,128)}), f32[256,1024]{1,0:T(8,128)}) %all-reduce.7.cloned.1.call-update) | async-done | bytes 1048592 | tf_op jit(solution)/shard_map/psum | solution.py:23
  342.4 6.1 %convolution_convert_fusion = bf16[256,3072]{1,0:T(8,128)(2,1)} fusion(bf16[3072,1024]{1,0:T(8,128)(2,1)} %select_select_fusion, f32[256,1024]{1,0:T(8,128)} %all-reduce.7.cloned.1.call-done, f32[1024]{0:T(1024)S(1)} %power_multiply_fusion), kind=kOutput, calls=%fused_computation.2 | convolution fusion | flops 1611923456 | bytes 8916992 | tf_op jit(solution)/shard_map/dot_general | solution.py:26
  348.5 0.0 reduce-scatter.5.cloned.1.call-update
  348.5 8.3 %reduce-scatter.5.cloned.1.call-done = bf16[128,3072]{1,0:T(8,128)(2,1)} async-done(((bf16[256,3072]{1,0:T(8,128)(2,1)}), bf16[128,3072]{1,0:T(8,128)(2,1)}) %reduce-scatter.5.cloned.1.call-update) | async-done | bytes 786448 | tf_op jit(solution)/shard_map/reduce_scatter | solution.py:25
  356.8 0.0 copy-start.2
  356.8 2.0 multiply_reduce_fusion
  358.8 42.1 %all-reduce = (f32[128]{0:T(128)S(1)}, f32[128]{0:T(128)S(1)}) all-reduce(f32[128]{0:T(128)S(1)} %get-tuple-element.3, f32[128]{0:T(128)S(1)} %get-tuple-element.2), channel_id=1, replica_groups=mesh['vert'=16,'eig'=2] {'vert'}, use_global_device_ids=true, to_apply=%region_7.8 | all-reduce | flops 256 | bytes 2048 | tf_op jit(solution)/shard_map/psum | solution.py:36
  400.9 0.0 copy-done.2
  400.9 2.7 multiply_subtract_fusion
  (6 shorter events, 0.1 us)
Async XLA Ops:
  7.2 28.8 %all-gather.3.cloned.1.call-start = ((), (), s32[]{:S(2)}) async-start(), calls=%async_computation.2 | async-start | bytes 2359296 | tf_op jit(solution)/shard_map/all_gather | solution.py:22
  7.9 2.5 copy-start.4
  10.3 147.0 %all-reduce.5.cloned.1.call-start = ((), (), s32[]{:S(2)}) async-start(), calls=%async_computation.3 | async-start | bytes 2097152 | tf_op jit(solution)/shard_map/psum | solution.py:23
  35.9 6.1 %copy-start.5 = (f32[1024]{0:T(1024)S(1)}, f32[1024]{0:T(1024)}, u32[]{:S(2)}) copy-start(f32[1024]{0:T(1024)} %param.10) | copy-start | bytes 12292
  42.0 129.8 %reduce-scatter.3.cloned.1.call-start = ((), (), s32[]{:S(2)}) async-start(), calls=%async_computation.4 | async-start | bytes 2359296 | tf_op jit(solution)/shard_map/reduce_scatter | solution.py:25
  157.3 14.4 %copy-start.3 = (f32[3072]{0:T(1024)S(1)}, f32[3072]{0:T(1024)}, u32[]{:S(2)}) copy-start(f32[3072]{0:T(1024)} %param.9) | copy-start | bytes 36868
  163.4 8.3 %copy-start = (f32[128,3072]{1,0:T(8,128)S(1)}, f32[128,3072]{1,0:T(8,128)}, u32[]{:S(2)}) copy-start(f32[128,3072]{1,0:T(8,128)} %param.11) | copy-start | bytes 4718596
  163.5 59.2 %all-gather.5.cloned.1.call-start = ((), (), s32[]{:S(2)}) async-start(), calls=%async_computation.5 | async-start | bytes 2359296 | tf_op jit(solution)/shard_map/all_gather | solution.py:22
  171.8 43.8 %copy-start.1 = (bf16[128,3072]{1,0:T(8,128)(2,1)S(1)}, bf16[128,3072]{1,0:T(8,128)(2,1)}, u32[]{:S(2)}) copy-start(bf16[128,3072]{1,0:T(8,128)(2,1)} %reduce-scatter.3.cloned.1.call-done) | copy-start | bytes 2359300
  216.9 125.5 %all-reduce.7.cloned.1.call-start = ((), (), s32[]{:S(2)}) async-start(), calls=%async_computation.6 | async-start | bytes 2097152 | tf_op jit(solution)/shard_map/psum | solution.py:23
  228.7 128.0 %reduce-scatter.5.cloned.1.call-start = ((), (), s32[]{:S(2)}) async-start(), calls=%async_computation.7 | async-start | bytes 2359296 | tf_op jit(solution)/shard_map/reduce_scatter | solution.py:25
  356.8 44.1 %copy-start.2 = (bf16[128,3072]{1,0:T(8,128)(2,1)S(1)}, bf16[128,3072]{1,0:T(8,128)(2,1)}, u32[]{:S(2)}) copy-start(bf16[128,3072]{1,0:T(8,128)(2,1)} %reduce-scatter.5.cloned.1.call-done) | copy-start | bytes 2359300
Sparse Core Ops, SparseCore 0:
  10.4 12.5 all-gather.2
  42.1 115.1 all-reduce.4
  163.6 8.1 reduce-scatter.2
  217.0 5.6 all-gather.4
  228.8 113.4 all-reduce.6
  348.6 8.0 reduce-scatter.4
where the time goes:
time: 411 us; the launch traced here: 410 us
  waiting for transfers between devices  251 us (61%)
  blocking collectives  84.1 us (20%)
  matrix products  24.3 us (6%)
  local copies, waits for them, and re-layouts  18.7 us (5%)
  other arithmetic  17 us (4%)
  between operations  14.8 us (4%)
    psum x2, waiting for transfers between devices, operate(): summed = lax.psum(coeff, 'vert')  229 us
    psum x2, blocking collectives, two_products(): lax.psum((jnp.sum(vector * vector, axis=1), jnp.sum(vector * applied, axi...  84.1 us
    gather x1, local copies, waits for them, and re-layouts, shards(): jnp.take(eig_table, obs_ids, axis=0)  18.7 us
    reduce_scatter x2, waiting for transfers between devices, operate(): lax.psum_scatter(lax.dot_general(weights, features, (((1,), (1,)), ((), (...  16.5 us
    dot_general x2, matrix products, operate(): lax.dot_general(weights, features, (((1,), (1,)), ((), ())), preferred_el...  12.2 us
    dot_general x2, matrix products, project(): return jnp.dot(shard_rows, features, preferred_element_type=jnp.float32)  12.1 us
  transfers between devices with their start and end apart: 6, of which 5 were waited for; matrix products, arithmetic and copies ran while one was open for 6% of the time, Pallas kernels for 0%

commit v1 on v0

v1 whole, which is shorter than its diff:
```python
import jax
import jax.numpy as jnp
from jax import lax
from jax.sharding import PartitionSpec as P

ITERS = 2


def butterfly(x, n_vert, finish):
    bits = n_vert.bit_length() - 1
    me = lax.axis_index("vert")
    cur = x
    for b in range(bits):
        half = cur.shape[1] // 2
        perm = [(i, i ^ (1 << b)) for i in range(n_vert)]
        upper = (me >> b) & 1
        keep = lax.dynamic_slice_in_dim(cur, upper * half, half, axis=1)
        send = lax.dynamic_slice_in_dim(cur, (1 - upper) * half, half, axis=1)
        cur = keep + lax.ppermute(send, "vert", perm)
    cur = finish(cur)
    for b in reversed(range(bits)):
        perm = [(i, i ^ (1 << b)) for i in range(n_vert)]
        upper = (me >> b) & 1
        got = lax.ppermute(cur, "vert", perm)
        cur = jnp.where(upper == 0, jnp.concatenate([cur, got], 1), jnp.concatenate([got, cur], 1))
    return cur


def make_shards(n_vert, n_eig):
    def shards(eig_table, obs_ids, counts, noise_var, eigenvalues, rhs):
        capacity = obs_ids.shape[0]
        own = rhs.shape[0]
        samples = own * n_eig
        group = eig_table.shape[1]
        filled = jnp.arange(capacity, dtype=jnp.int32) < counts[0]
        features = jnp.where(
            filled[:, None], jnp.take(eig_table, obs_ids, axis=0), jnp.zeros((), jnp.bfloat16)
        )
        spectrum = 5.0 * jnp.power(3.0 + eigenvalues, -1.5)
        me_eig = lax.axis_index("eig")

        def finish(piece):
            weights = piece[:samples].astype(jnp.bfloat16)
            sums = piece[samples:]
            high = sums.astype(jnp.bfloat16)
            low = (sums - high.astype(jnp.float32)).astype(jnp.bfloat16)
            return jnp.concatenate([weights, high, low], 0)

        def operate(vector):
            lowered = vector.astype(jnp.bfloat16)
            coeff = jnp.dot(
                lax.all_gather(lowered, "eig", axis=0, tiled=True),
                features,
                preferred_element_type=jnp.float32,
            )
            sums = jnp.zeros((8, group), jnp.float32)
            sums = sums.at[0, :own].set(jnp.sum(vector * vector, axis=1))
            sums = sums.at[1, :own].set(jnp.sum(noise_var[None, :] * vector * vector, axis=1))
            gathered = butterfly(
                jnp.concatenate([coeff * spectrum[None, :], sums], 0), n_vert, finish
            )
            weights = gathered[:samples]
            sums = gathered[samples : samples + 8].astype(jnp.float32) + gathered[
                samples + 8 : samples + 16
            ].astype(jnp.float32)
            wide = weights.astype(jnp.float32)
            energy = jnp.sum(wide * wide / spectrum[None, :], axis=1)
            if n_eig == 2:
                mine = lax.dynamic_slice_in_dim(energy, me_eig * own, own)
                theirs = lax.dynamic_slice_in_dim(energy, (1 - me_eig) * own, own)
                energy = mine + lax.ppermute(theirs, "eig", [(0, 1), (1, 0)])
            else:
                energy = lax.psum_scatter(energy, "eig", scatter_dimension=0, tiled=True)
            applied = lax.psum_scatter(
                lax.dot_general(
                    weights, features, (((1,), (1,)), ((), ())), preferred_element_type=jnp.float32
                ).astype(jnp.bfloat16),
                "eig",
                scatter_dimension=0,
                tiled=True,
            ).astype(jnp.float32)
            norm = sums[0, :own]
            product = sums[1, :own] + energy
            return applied + noise_var[None, :] * vector, norm, product

        residual = jnp.where(filled[None, :], rhs, jnp.zeros((), jnp.float32))
        solution = jnp.zeros_like(residual)
        applied, norm_now, product = operate(residual)
        step_size = norm_now / product
        direction, along = (residual, applied)
        for iteration in range(ITERS):
            solution = solution + step_size[:, None] * direction
            residual = residual - step_size[:, None] * along
            if iteration + 1 < ITERS:
                applied, norm_next, product = operate(residual)
                beta_ratio = norm_next / norm_now
                step_size = norm_next / (product - beta_ratio * norm_next / step_size)
                direction = residual + beta_ratio[:, None] * direction
                along = applied + beta_ratio[:, None] * along
                norm_now = norm_next
        return (solution, residual)

    return shards


def solution(mesh):
    return jax.shard_map(
        make_shards(mesh.shape["vert"], mesh.shape["eig"]),
        mesh=mesh,
        in_specs=(P("vert", "eig"), P("vert"), P("vert"), P("vert"), P("eig"), P("eig", "vert")),
        out_specs=(P("eig", "vert"), P("eig", "vert")),
        check_vma=False,
    )
```

time: 411 us -> 223 us (0.54)
  waiting for transfers between devices: 251 us -> 114 us
  blocking collectives: 84.1 us -> 0 us
  starting transfers between devices: 0.25 us -> 33.3 us
    psum x2 -> x0, waiting for transfers between devices: 229 us -> none  [operate(): summed = lax.psum(coeff, 'vert')]
    ppermute x0 -> x18, waiting for transfers between devices: none -> 84.2 us  [the longest x8 53.1 us: butterfly(): cur = keep + lax.ppermute(send, 'vert', perm)]
    psum x2 -> x0, blocking collectives: 84.1 us -> none  [two_products(): lax.psum((jnp.sum(vector * vector, axis=1), jnp.sum(vector * applied, axi...]
    ppermute x0 -> x18, starting transfers between devices: none -> 32.9 us  [the longest x8 17.6 us: butterfly(): cur = keep + lax.ppermute(send, 'vert', perm)]
    all_gather x2, waiting for transfers between devices: 5.77 us -> 10.8 us  [operate(): lax.all_gather(lowered, 'eig', axis=0, tiled=True)]
  transfers between devices with their start and end apart: 6 -> 22, of which waited for: 5 -> 21; matrix products, arithmetic and copies ran while one was open for 6% -> 12% of each run, Pallas kernels for 0% -> 0%
where the time goes in v1:
time: 223 us
  waiting for transfers between devices  114 us (51%)
  starting transfers between devices  33.3 us (15%)
  matrix products  21.6 us (10%)
  local copies, waits for them, and re-layouts  19.6 us (9%)
  other arithmetic  19.4 us (9%)
  between operations  14.8 us (7%)
    ppermute x8, waiting for transfers between devices, butterfly(): cur = keep + lax.ppermute(send, 'vert', perm)  53.1 us
    ppermute x8, waiting for transfers between devices, butterfly(): got = lax.ppermute(cur, 'vert', perm)  28.8 us
    reduce_scatter x2, waiting for transfers between devices, operate(): lax.psum_scatter(lax.dot_general(weights, features, (((1,), (1,)), ((), (...  19.1 us
    gather x1, local copies, waits for them, and re-layouts, shards(): jnp.take(eig_table, obs_ids, axis=0)  18.7 us
    ppermute x8, starting transfers between devices, butterfly(): cur = keep + lax.ppermute(send, 'vert', perm)  17.6 us
    ppermute x8, starting transfers between devices, butterfly(): got = lax.ppermute(cur, 'vert', perm)  15.3 us
    dot_general x2, matrix products, operate(): lax.dot_general(weights, features, (((1,), (1,)), ((), ())), preferred_el...  11.5 us
    all_gather x2, waiting for transfers between devices, operate(): lax.all_gather(lowered, 'eig', axis=0, tiled=True)  10.8 us
  transfers between devices with their start and end apart: 22, of which 21 were waited for; matrix products, arithmetic and copies ran while one was open for 12% of the time, Pallas kernels for 0%

profile of v1, /device:TPU:0, one launch (start us, length us, event | category | flops | bytes accessed | tf_op | source)
XLA Modules:
  0.0 222.8 jit_solution(6012264839342716575)
XLA Ops:
  7.9 2.5 %select_convert_fusion = bf16[128,3072]{1,0:T(8,128)(2,1)} fusion(f32[128,3072]{1,0:T(8,128)} %param.19, pred[3072]{0:T(1024)(128)(4,1)S(1)} %iota_compare_fusion), kind=kLoop, calls=%fused_computation.23 | loop fusion | flops 393216 | bytes 2362368 | tf_op jit(solution)/shard_map/convert_element_type | solution.py:50
  10.5 0.4 fusion
  11.0 0.2 scatter.15
  11.2 18.7 %gather_fusion = bf16[3072,1024]{1,0:T(8,128)(2,1)} fusion(bf16[2048,1024]{1,0:T(8,128)(2,1)} %param.14, s32[3072]{0:T(1024)S(1)} %fusion.15), kind=kCustom, calls=%fused_computation | custom fusion | bytes 12595200 | tf_op jit(solution)/shard_map/jit(_take)/gather | solution.py:37
  29.9 6.9 %select_select_fusion = bf16[3072,1024]{1,0:T(8,128)(2,1)} fusion(bf16[3072,1024]{1,0:T(8,128)(2,1)} %gather_fusion, pred[3072]{0:T(1024)(128)(4,1)S(1)} %compare_and_fusion, pred[3072]{0:T(1024)(128)(4,1)S(1)} %iota_compare_fusion), kind=kLoop, calls=%fused_computation.1 | loop fusion | flops 6291456 | bytes 12589056 | tf_op jit(solution)/shard_map/jit(_where)/select_n | solution.py:36
  36.8 5.1 %convolution_multiply_fusion.1 = f32[256,1024]{1,0:T(8,128)S(1)} fusion(bf16[256,3072]{1,0:T(8,128)(2,1)} %all-gather.3.cloned.1.call-done, bf16[3072,1024]{1,0:T(8,128)(2,1)} %select_select_fusion, f32[1024]{0:T(1024)S(1)} %power_multiply_fusion), kind=kOutput, calls=%fused_computation.22 | convolution fusion | flops 1610874880 | bytes 8916992 | tf_op jit(solution)/shard_map/dot_general | solution.py:51
  41.9 3.0 %collective-permute-start = (f32[264,512]{1,0:T(8,128)S(1)}, f32[264,512]{1,0:T(8,128)}, u32[]{:S(2)}, u32[]{:S(2)}) collective-permute-start(f32[264,512]{1,0:T(8,128)S(1)} %fusion.10), channel_id=1, source_target_pairs={{0,2},{2,0},{4,6},{6,4},{8,10},{10,8},{12,14},{14,12},{16,18},{18,... | collective-permute-start | bytes 1622024 | tf_op jit(solution)/shard_map/ppermute | solution.py:19
  44.9 12.4 %collective-permute-done = f32[264,512]{1,0:T(8,128)} collective-permute-done((f32[264,512]{1,0:T(8,128)S(1)}, f32[264,512]{1,0:T(8,128)}, u32[]{:S(2)}, u32[]{:S(2)}) %collective-permute-start) | collective-permute-done | bytes 540704 | tf_op jit(solution)/shard_map/ppermute | solution.py:19
  57.3 1.1 fusion.12
  58.5 1.8 collective-permute-start.1
  60.3 5.9 %collective-permute-done.1 = f32[264,256]{1,0:T(8,128)S(1)} collective-permute-done((f32[264,256]{1,0:T(8,128)S(1)}, f32[264,256]{1,0:T(8,128)S(1)}, u32[]{:S(2)}, u32[]{:S(2)}) %collective-permute-start.1) | collective-permute-done | bytes 270368 | tf_op jit(solution)/shard_map/ppermute | solution.py:19
  66.3 1.6 collective-permute-start.2
  67.9 3.5 %collective-permute-done.2 = f32[264,128]{1,0:T(8,128)S(1)} collective-permute-done((f32[264,128]{1,0:T(8,128)S(1)}, f32[264,128]{1,0:T(8,128)S(1)}, u32[]{:S(2)}, u32[]{:S(2)}) %collective-permute-start.2) | collective-permute-done | bytes 135200 | tf_op jit(solution)/shard_map/ppermute | solution.py:19
  71.4 0.1 constant_dynamic-slice_fusion.3
  71.5 3.0 %collective-permute-start.3 = (f32[264,64]{1,0:T(8,128)S(1)}, f32[264,64]{1,0:T(8,128)S(1)}, u32[]{:S(2)}, u32[]{:S(2)}) collective-permute-start(f32[264,64]{1,0:T(8,128)S(1)} %constant_dynamic-slice_fusion.3), channel_id=1, source_target_pairs={{0,16},{2,18},{4,20},{6,22},{8,24},{10,26},{12,28},{14,30},{16,0},... | collective-permute-start | bytes 202760 | tf_op jit(solution)/shard_map/ppermute | solution.py:19
  74.4 4.6 %collective-permute-done.3 = f32[264,64]{1,0:T(8,128)S(1)} collective-permute-done((f32[264,64]{1,0:T(8,128)S(1)}, f32[264,64]{1,0:T(8,128)S(1)}, u32[]{:S(2)}, u32[]{:S(2)}) %collective-permute-start.3) | collective-permute-done | bytes 67616 | tf_op jit(solution)/shard_map/ppermute | solution.py:19
  79.1 0.1 dynamic-slice_add_fusion.4
  79.2 2.2 collective-permute-start.4
  81.4 3.1 %collective-permute-done.4 = bf16[272,64]{1,0:T(8,128)(2,1)S(1)} collective-permute-done((bf16[272,64]{1,0:T(8,128)(2,1)S(1)}, bf16[272,64]{1,0:T(8,128)(2,1)S(1)}, u32[]{:S(2)}, u32[]{:S(2)}) %collective-permute-start.4) | collective-permute-done | bytes 34848 | tf_op jit(solution)/shard_map/ppermute | solution.py:24
  84.5 0.1 maximum_select_fusion.6
  84.6 2.6 %collective-permute-start.5 = (bf16[272,128]{1,0:T(8,128)(2,1)S(1)}, bf16[272,128]{1,0:T(8,128)(2,1)S(1)}, u32[]{:S(2)}, u32[]{:S(2)}) collective-permute-start(bf16[272,128]{1,0:T(8,128)(2,1)S(1)} %maximum_select_fusion.6), channel_id=1, source_target_pairs={{0,8},{2,10},{4,12},{6,14},{8,0},{10,2},{12,4},{14,6},{16,24},{18,... | collective-permute-start | bytes 208904 | tf_op jit(solution)/shard_map/ppermute | solution.py:24
  87.2 2.3 %collective-permute-done.5 = bf16[272,128]{1,0:T(8,128)(2,1)S(1)} collective-permute-done((bf16[272,128]{1,0:T(8,128)(2,1)S(1)}, bf16[272,128]{1,0:T(8,128)(2,1)S(1)}, u32[]{:S(2)}, u32[]{:S(2)}) %collective-permute-start.5) | collective-permute-done | bytes 69664 | tf_op jit(solution)/shard_map/ppermute | solution.py:24
  89.5 1.6 collective-permute-start.6
  91.1 3.5 %collective-permute-done.6 = bf16[272,256]{1,0:T(8,128)(2,1)S(1)} collective-permute-done((bf16[272,256]{1,0:T(8,128)(2,1)S(1)}, bf16[272,256]{1,0:T(8,128)(2,1)S(1)}, u32[]{:S(2)}, u32[]{:S(2)}) %collective-permute-start.6) | collective-permute-done | bytes 139296 | tf_op jit(solution)/shard_map/ppermute | solution.py:24
  94.7 0.1 maximum_select_fusion.2
  94.8 1.6 collective-permute-start.7
  96.4 5.1 %collective-permute-done.7 = bf16[272,512]{1,0:T(8,128)(2,1)S(1)} collective-permute-done((bf16[272,512]{1,0:T(8,128)(2,1)S(1)}, bf16[272,512]{1,0:T(8,128)(2,1)S(1)}, u32[]{:S(2)}, u32[]{:S(2)}) %collective-permute-start.7) | collective-permute-done | bytes 278560 | tf_op jit(solution)/shard_map/ppermute | solution.py:24
  101.4 0.1 maximum_select_fusion
  101.6 5.8 %convolution_convert_fusion.1 = bf16[256,3072]{1,0:T(8,128)(2,1)} fusion(bf16[3072,1024]{1,0:T(8,128)(2,1)} %select_select_fusion, bf16[272,1024]{1,0:T(8,128)(2,1)S(1)} %maximum_select_fusion), kind=kOutput, calls=%fused_computation.3 | convolution fusion | flops 1611399168 | bytes 8388608 | tf_op jit(solution)/shard_map/dot_general | solution.py:75
  107.4 0.2 fusion.5
  107.7 1.1 collective-permute-done.8
  109.0 9.6 %reduce-scatter.3.cloned.1.call-done = bf16[128,3072]{1,0:T(8,128)(2,1)} async-done(((bf16[256,3072]{1,0:T(8,128)(2,1)}), bf16[128,3072]{1,0:T(8,128)(2,1)}) %reduce-scatter.3.cloned.1.call-update) | async-done | bytes 786448 | tf_op jit(solution)/shard_map/reduce_scatter | solution.py:74
  118.6 2.6 %fusion.1 = (f32[128]{0:T(128)S(1)}, f32[128]{0:T(128)S(1)}, bf16[128,3072]{1,0:T(8,128)(2,1)}) fusion(f32[3072]{0:T(1024)S(1)} %copy-done.2, bf16[128,3072]{1,0:T(8,128)(2,1)} %reduce-scatter.3.cloned.1.call-done, f32[128]{0:T(128)S(1)} %fusion.21, f32[128,3072]{1,0:T(8,128)S(1)} %copy-done, pred[3072]{0:T(1024)(128)(4,1)S(1)} %iota_compare_fusion), kind=kLoop, calls=%fused_computation.9 | loop fusion | flops 4718336 | bytes 3162624 | tf_op jit(solution)/shard_map/reduce_sum | solution.py:58
  121.2 0.2 reduce-scatter.5.cloned.1.call-start
  121.5 0.2 scatter.19
  121.7 10.8 %all-gather.5.cloned.1.call-done = bf16[256,3072]{1,0:T(8,128)(2,1)} async-done(((bf16[128,3072]{1,0:T(8,128)(2,1)}), bf16[256,3072]{1,0:T(8,128)(2,1)}) %all-gather.5.cloned.1.call-update) | async-done | bytes 1572880 | tf_op jit(solution)/shard_map/all_gather | solution.py:52
  132.5 5.1 %convolution_multiply_fusion = f32[256,1024]{1,0:T(8,128)S(1)} fusion(bf16[256,3072]{1,0:T(8,128)(2,1)} %all-gather.5.cloned.1.call-done, bf16[3072,1024]{1,0:T(8,128)(2,1)} %select_select_fusion, f32[1024]{0:T(1024)S(1)} %power_multiply_fusion), kind=kOutput, calls=%fused_computation.21 | convolution fusion | flops 1610874880 | bytes 8916992 | tf_op jit(solution)/shard_map/dot_general | solution.py:51
  137.6 1.8 collective-permute-start.9
  139.4 12.7 %collective-permute-done.9 = f32[264,512]{1,0:T(8,128)S(1)} collective-permute-done((f32[264,512]{1,0:T(8,128)S(1)}, f32[264,512]{1,0:T(8,128)S(1)}, u32[]{:S(2)}, u32[]{:S(2)}) %collective-permute-start.9) | collective-permute-done | bytes 540704 | tf_op jit(solution)/shard_map/ppermute | solution.py:19
  152.1 0.1 fusion.9
  152.3 1.8 collective-permute-start.10
  154.1 6.1 %collective-permute-done.10 = f32[264,256]{1,0:T(8,128)S(1)} collective-permute-done((f32[264,256]{1,0:T(8,128)S(1)}, f32[264,256]{1,0:T(8,128)S(1)}, u32[]{:S(2)}, u32[]{:S(2)}) %collective-permute-start.10) | collective-permute-done | bytes 270368 | tf_op jit(solution)/shard_map/ppermute | solution.py:19
  160.2 1.8 collective-permute-start.11
  162.0 3.3 %collective-permute-done.11 = f32[264,128]{1,0:T(8,128)S(1)} collective-permute-done((f32[264,128]{1,0:T(8,128)S(1)}, f32[264,128]{1,0:T(8,128)S(1)}, u32[]{:S(2)}, u32[]{:S(2)}) %collective-permute-start.11) | collective-permute-done | bytes 135200 | tf_op jit(solution)/shard_map/ppermute | solution.py:19
  165.3 0.1 constant_dynamic-slice_fusion
  165.4 2.7 %collective-permute-start.12 = (f32[264,64]{1,0:T(8,128)S(1)}, f32[264,64]{1,0:T(8,128)S(1)}, u32[]{:S(2)}, u32[]{:S(2)}) collective-permute-start(f32[264,64]{1,0:T(8,128)S(1)} %constant_dynamic-slice_fusion), channel_id=1, source_target_pairs={{0,16},{2,18},{4,20},{6,22},{8,24},{10,26},{12,28},{14,30},{16,0},... | collective-permute-start | bytes 202760 | tf_op jit(solution)/shard_map/ppermute | solution.py:19
  168.2 4.7 %collective-permute-done.12 = f32[264,64]{1,0:T(8,128)S(1)} collective-permute-done((f32[264,64]{1,0:T(8,128)S(1)}, f32[264,64]{1,0:T(8,128)S(1)}, u32[]{:S(2)}, u32[]{:S(2)}) %collective-permute-start.12) | collective-permute-done | bytes 67616 | tf_op jit(solution)/shard_map/ppermute | solution.py:19
  172.9 0.1 dynamic-slice_add_fusion.2
  173.0 1.4 collective-permute-start.13
  174.4 3.9 %collective-permute-done.13 = bf16[272,64]{1,0:T(8,128)(2,1)S(1)} collective-permute-done((bf16[272,64]{1,0:T(8,128)(2,1)S(1)}, bf16[272,64]{1,0:T(8,128)(2,1)S(1)}, u32[]{:S(2)}, u32[]{:S(2)}) %collective-permute-start.13) | collective-permute-done | bytes 34848 | tf_op jit(solution)/shard_map/ppermute | solution.py:24
  178.3 0.1 maximum_select_fusion.7
  178.4 2.9 %collective-permute-start.14 = (bf16[272,128]{1,0:T(8,128)(2,1)S(1)}, bf16[272,128]{1,0:T(8,128)(2,1)S(1)}, u32[]{:S(2)}, u32[]{:S(2)}) collective-permute-start(bf16[272,128]{1,0:T(8,128)(2,1)S(1)} %maximum_select_fusion.7), channel_id=1, source_target_pairs={{0,8},{2,10},{4,12},{6,14},{8,0},{10,2},{12,4},{14,6},{16,24},{18,... | collective-permute-start | bytes 208904 | tf_op jit(solution)/shard_map/ppermute | solution.py:24
  181.3 2.3 %collective-permute-done.14 = bf16[272,128]{1,0:T(8,128)(2,1)S(1)} collective-permute-done((bf16[272,128]{1,0:T(8,128)(2,1)S(1)}, bf16[272,128]{1,0:T(8,128)(2,1)S(1)}, u32[]{:S(2)}, u32[]{:S(2)}) %collective-permute-start.14) | collective-permute-done | bytes 69664 | tf_op jit(solution)/shard_map/ppermute | solution.py:24
  183.6 1.5 collective-permute-start.15
  185.2 3.6 %collective-permute-done.15 = bf16[272,256]{1,0:T(8,128)(2,1)S(1)} collective-permute-done((bf16[272,256]{1,0:T(8,128)(2,1)S(1)}, bf16[272,256]{1,0:T(8,128)(2,1)S(1)}, u32[]{:S(2)}, u32[]{:S(2)}) %collective-permute-start.15) | collective-permute-done | bytes 139296 | tf_op jit(solution)/shard_map/ppermute | solution.py:24
  188.8 0.1 maximum_select_fusion.3
  188.9 1.5 collective-permute-start.16
  190.4 5.1 %collective-permute-done.16 = bf16[272,512]{1,0:T(8,128)(2,1)S(1)} collective-permute-done((bf16[272,512]{1,0:T(8,128)(2,1)S(1)}, bf16[272,512]{1,0:T(8,128)(2,1)S(1)}, u32[]{:S(2)}, u32[]{:S(2)}) %collective-permute-start.16) | collective-permute-done | bytes 278560 | tf_op jit(solution)/shard_map/ppermute | solution.py:24
  195.5 0.1 maximum_select_fusion.1
  195.7 5.8 %convolution_convert_fusion = bf16[256,3072]{1,0:T(8,128)(2,1)} fusion(bf16[3072,1024]{1,0:T(8,128)(2,1)} %select_select_fusion, bf16[272,1024]{1,0:T(8,128)(2,1)S(1)} %maximum_select_fusion.1), kind=kOutput, calls=%fused_computation.2 | convolution fusion | flops 1611399168 | bytes 8388608 | tf_op jit(solution)/shard_map/dot_general | solution.py:75
  201.5 0.2 fusion.6
  201.8 1.1 collective-permute-done.17
  203.0 9.5 %reduce-scatter.5.cloned.1.call-done = bf16[128,3072]{1,0:T(8,128)(2,1)} async-done(((bf16[256,3072]{1,0:T(8,128)(2,1)}), bf16[128,3072]{1,0:T(8,128)(2,1)}) %reduce-scatter.5.cloned.1.call-update) | async-done | bytes 786448 | tf_op jit(solution)/shard_map/reduce_scatter | solution.py:74
  212.5 3.8 %fusion.4 = (f32[128,3072]{1,0:T(8,128)}, f32[128,3072]{1,0:T(8,128)}) fusion(bf16[128,3072]{1,0:T(8,128)(2,1)} %reduce-scatter.5.cloned.1.call-done, bf16[128,3072]{1,0:T(8,128)(2,1)S(1)} %copy-done.1, f32[128,3072]{1,0:T(8,128)S(1)} %copy-done, f32[128]{0:T(128)S(1)} %get-tuple-element.55, f32[128]{0:T(128)S(1)} %get-tuple-element.54, ...), kind=kLoop, calls=%fused_computation.12 | loop fusion | flops 7077888 | bytes 6308352 | tf_op jit(solution)/shard_map/sub | solution.py:93
  (50 shorter events, 1.1 us)
Async XLA Ops:
  7.2 29.6 %all-gather.3.cloned.1.call-start = ((), (), s32[]{:S(2)}) async-start(), calls=%async_computation.2 | async-start | bytes 2359296 | tf_op jit(solution)/shard_map/all_gather | solution.py:52
  7.9 2.6 %copy-start = (f32[128,3072]{1,0:T(8,128)S(1)}, f32[128,3072]{1,0:T(8,128)}, u32[]{:S(2)}) copy-start(f32[128,3072]{1,0:T(8,128)} %param.19) | copy-start | bytes 4718596
  7.9 2.6 %copy-start.2 = (f32[3072]{0:T(1024)S(1)}, f32[3072]{0:T(1024)}, u32[]{:S(2)}) copy-start(f32[3072]{0:T(1024)} %param.17) | copy-start | bytes 36868
  10.4 0.8 copy-start.3
  10.4 108.1 %reduce-scatter.3.cloned.1.call-start = ((), (), s32[]{:S(2)}) async-start(), calls=%async_computation.3 | async-start | bytes 2359296 | tf_op jit(solution)/shard_map/reduce_scatter | solution.py:74
  11.2 18.7 %copy-start.4 = (f32[1024]{0:T(1024)S(1)}, f32[1024]{0:T(1024)}, u32[]{:S(2)}) copy-start(f32[1024]{0:T(1024)} %param.18) | copy-start | bytes 12292
  41.9 15.4 %collective-permute-start = (f32[264,512]{1,0:T(8,128)S(1)}, f32[264,512]{1,0:T(8,128)}, u32[]{:S(2)}, u32[]{:S(2)}) collective-permute-start(f32[264,512]{1,0:T(8,128)S(1)} %fusion.10), channel_id=1, source_target_pairs={{0,2},{2,0},{4,6},{6,4},{8,10},{10,8},{12,14},{14,12},{16,18},{18,... | collective-permute-start | bytes 1622024 | tf_op jit(solution)/shard_map/ppermute | solution.py:19
  58.5 7.7 %collective-permute-start.1 = (f32[264,256]{1,0:T(8,128)S(1)}, f32[264,256]{1,0:T(8,128)S(1)}, u32[]{:S(2)}, u32[]{:S(2)}) collective-permute-start(f32[264,256]{1,0:T(8,128)S(1)} %constant_dynamic-slice_fusion.5), channel_id=1, source_target_pairs={{0,4},{2,6},{4,0},{6,2},{8,12},{10,14},{12,8},{14,10},{16,20},{18,... | collective-permute-start | bytes 811016 | tf_op jit(solution)/shard_map/ppermute | solution.py:19
  66.3 5.1 %collective-permute-start.2 = (f32[264,128]{1,0:T(8,128)S(1)}, f32[264,128]{1,0:T(8,128)S(1)}, u32[]{:S(2)}, u32[]{:S(2)}) collective-permute-start(f32[264,128]{1,0:T(8,128)S(1)} %constant_dynamic-slice_fusion.4), channel_id=1, source_target_pairs={{0,8},{2,10},{4,12},{6,14},{8,0},{10,2},{12,4},{14,6},{16,24},{18,... | collective-permute-start | bytes 405512 | tf_op jit(solution)/shard_map/ppermute | solution.py:19
  71.5 7.6 %collective-permute-start.3 = (f32[264,64]{1,0:T(8,128)S(1)}, f32[264,64]{1,0:T(8,128)S(1)}, u32[]{:S(2)}, u32[]{:S(2)}) collective-permute-start(f32[264,64]{1,0:T(8,128)S(1)} %constant_dynamic-slice_fusion.3), channel_id=1, source_target_pairs={{0,16},{2,18},{4,20},{6,22},{8,24},{10,26},{12,28},{14,30},{16,0},... | collective-permute-start | bytes 202760 | tf_op jit(solution)/shard_map/ppermute | solution.py:19
  79.2 5.3 %collective-permute-start.4 = (bf16[272,64]{1,0:T(8,128)(2,1)S(1)}, bf16[272,64]{1,0:T(8,128)(2,1)S(1)}, u32[]{:S(2)}, u32[]{:S(2)}) collective-permute-start(bf16[272,64]{1,0:T(8,128)(2,1)S(1)} %pad_maximum_fusion), channel_id=1, source_target_pairs={{0,16},{2,18},{4,20},{6,22},{8,24},{10,26},{12,28},{14,30},{16,0},... | collective-permute-start | bytes 104456 | tf_op jit(solution)/shard_map/ppermute | solution.py:24
  84.6 4.9 %collective-permute-start.5 = (bf16[272,128]{1,0:T(8,128)(2,1)S(1)}, bf16[272,128]{1,0:T(8,128)(2,1)S(1)}, u32[]{:S(2)}, u32[]{:S(2)}) collective-permute-start(bf16[272,128]{1,0:T(8,128)(2,1)S(1)} %maximum_select_fusion.6), channel_id=1, source_target_pairs={{0,8},{2,10},{4,12},{6,14},{8,0},{10,2},{12,4},{14,6},{16,24},{18,... | collective-permute-start | bytes 208904 | tf_op jit(solution)/shard_map/ppermute | solution.py:24
  89.5 5.1 %collective-permute-start.6 = (bf16[272,256]{1,0:T(8,128)(2,1)S(1)}, bf16[272,256]{1,0:T(8,128)(2,1)S(1)}, u32[]{:S(2)}, u32[]{:S(2)}) collective-permute-start(bf16[272,256]{1,0:T(8,128)(2,1)S(1)} %maximum_select_fusion.4), channel_id=1, source_target_pairs={{0,4},{2,6},{4,0},{6,2},{8,12},{10,14},{12,8},{14,10},{16,20},{18,... | collective-permute-start | bytes 417800 | tf_op jit(solution)/shard_map/ppermute | solution.py:24
  94.8 6.6 %collective-permute-start.7 = (bf16[272,512]{1,0:T(8,128)(2,1)S(1)}, bf16[272,512]{1,0:T(8,128)(2,1)S(1)}, u32[]{:S(2)}, u32[]{:S(2)}) collective-permute-start(bf16[272,512]{1,0:T(8,128)(2,1)S(1)} %maximum_select_fusion.2), channel_id=1, source_target_pairs={{0,2},{2,0},{4,6},{6,4},{8,10},{10,8},{12,14},{14,12},{16,18},{18,... | collective-permute-start | bytes 835592 | tf_op jit(solution)/shard_map/ppermute | solution.py:24
  107.4 25.1 %all-gather.5.cloned.1.call-start = ((), (), s32[]{:S(2)}) async-start(), calls=%async_computation.4 | async-start | bytes 2359296 | tf_op jit(solution)/shard_map/all_gather | solution.py:52
  107.7 1.2 collective-permute-start.8
  121.2 91.3 %reduce-scatter.5.cloned.1.call-start = ((), (), s32[]{:S(2)}) async-start(), calls=%async_computation.5 | async-start | bytes 2359296 | tf_op jit(solution)/shard_map/reduce_scatter | solution.py:74
  137.6 14.5 %collective-permute-start.9 = (f32[264,512]{1,0:T(8,128)S(1)}, f32[264,512]{1,0:T(8,128)S(1)}, u32[]{:S(2)}, u32[]{:S(2)}) collective-permute-start(f32[264,512]{1,0:T(8,128)S(1)} %fusion.7), channel_id=1, source_target_pairs={{0,2},{2,0},{4,6},{6,4},{8,10},{10,8},{12,14},{14,12},{16,18},{18,... | collective-permute-start | bytes 1622024 | tf_op jit(solution)/shard_map/ppermute | solution.py:19
  152.3 7.9 %collective-permute-start.10 = (f32[264,256]{1,0:T(8,128)S(1)}, f32[264,256]{1,0:T(8,128)S(1)}, u32[]{:S(2)}, u32[]{:S(2)}) collective-permute-start(f32[264,256]{1,0:T(8,128)S(1)} %constant_dynamic-slice_fusion.2), channel_id=1, source_target_pairs={{0,4},{2,6},{4,0},{6,2},{8,12},{10,14},{12,8},{14,10},{16,20},{18,... | collective-permute-start | bytes 811016 | tf_op jit(solution)/shard_map/ppermute | solution.py:19
  160.2 5.1 %collective-permute-start.11 = (f32[264,128]{1,0:T(8,128)S(1)}, f32[264,128]{1,0:T(8,128)S(1)}, u32[]{:S(2)}, u32[]{:S(2)}) collective-permute-start(f32[264,128]{1,0:T(8,128)S(1)} %constant_dynamic-slice_fusion.1), channel_id=1, source_target_pairs={{0,8},{2,10},{4,12},{6,14},{8,0},{10,2},{12,4},{14,6},{16,24},{18,... | collective-permute-start | bytes 405512 | tf_op jit(solution)/shard_map/ppermute | solution.py:19
  165.4 7.4 %collective-permute-start.12 = (f32[264,64]{1,0:T(8,128)S(1)}, f32[264,64]{1,0:T(8,128)S(1)}, u32[]{:S(2)}, u32[]{:S(2)}) collective-permute-start(f32[264,64]{1,0:T(8,128)S(1)} %constant_dynamic-slice_fusion), channel_id=1, source_target_pairs={{0,16},{2,18},{4,20},{6,22},{8,24},{10,26},{12,28},{14,30},{16,0},... | collective-permute-start | bytes 202760 | tf_op jit(solution)/shard_map/ppermute | solution.py:19
  173.0 5.3 %collective-permute-start.13 = (bf16[272,64]{1,0:T(8,128)(2,1)S(1)}, bf16[272,64]{1,0:T(8,128)(2,1)S(1)}, u32[]{:S(2)}, u32[]{:S(2)}) collective-permute-start(bf16[272,64]{1,0:T(8,128)(2,1)S(1)} %pad_maximum_fusion.1), channel_id=1, source_target_pairs={{0,16},{2,18},{4,20},{6,22},{8,24},{10,26},{12,28},{14,30},{16,0},... | collective-permute-start | bytes 104456 | tf_op jit(solution)/shard_map/ppermute | solution.py:24
  178.4 5.2 %collective-permute-start.14 = (bf16[272,128]{1,0:T(8,128)(2,1)S(1)}, bf16[272,128]{1,0:T(8,128)(2,1)S(1)}, u32[]{:S(2)}, u32[]{:S(2)}) collective-permute-start(bf16[272,128]{1,0:T(8,128)(2,1)S(1)} %maximum_select_fusion.7), channel_id=1, source_target_pairs={{0,8},{2,10},{4,12},{6,14},{8,0},{10,2},{12,4},{14,6},{16,24},{18,... | collective-permute-start | bytes 208904 | tf_op jit(solution)/shard_map/ppermute | solution.py:24
  183.6 5.1 %collective-permute-start.15 = (bf16[272,256]{1,0:T(8,128)(2,1)S(1)}, bf16[272,256]{1,0:T(8,128)(2,1)S(1)}, u32[]{:S(2)}, u32[]{:S(2)}) collective-permute-start(bf16[272,256]{1,0:T(8,128)(2,1)S(1)} %maximum_select_fusion.5), channel_id=1, source_target_pairs={{0,4},{2,6},{4,0},{6,2},{8,12},{10,14},{12,8},{14,10},{16,20},{18,... | collective-permute-start | bytes 417800 | tf_op jit(solution)/shard_map/ppermute | solution.py:24
  188.9 6.6 %collective-permute-start.16 = (bf16[272,512]{1,0:T(8,128)(2,1)S(1)}, bf16[272,512]{1,0:T(8,128)(2,1)S(1)}, u32[]{:S(2)}, u32[]{:S(2)}) collective-permute-start(bf16[272,512]{1,0:T(8,128)(2,1)S(1)} %maximum_select_fusion.3), channel_id=1, source_target_pairs={{0,2},{2,0},{4,6},{6,4},{8,10},{10,8},{12,14},{14,12},{16,18},{18,... | collective-permute-start | bytes 835592 | tf_op jit(solution)/shard_map/ppermute | solution.py:24
  201.4 11.1 %copy-start.1 = (bf16[128,3072]{1,0:T(8,128)(2,1)S(1)}, bf16[128,3072]{1,0:T(8,128)(2,1)}, u32[]{:S(2)}) copy-start(bf16[128,3072]{1,0:T(8,128)(2,1)} %reduce-scatter.3.cloned.1.call-done) | copy-start | bytes 2359300
  201.8 1.2 collective-permute-start.17
Sparse Core Ops, SparseCore 0:
  10.6 12.5 all-gather.2
  107.5 11.0 reduce-scatter.2
  121.4 11.0 all-gather.4
  201.6 10.8 reduce-scatter.4

commit v2 on v1

v2 whole, which is shorter than its diff:
```python
import jax
import jax.numpy as jnp
from jax import lax
from jax.sharding import PartitionSpec as P

ITERS = 2


def vert_sum(x, n_vert, finish):
    bits = n_vert.bit_length() - 1
    rounds = [list(range(b, min(b + 2, bits))) for b in range(0, bits, 2)]
    me = lax.axis_index("vert")
    cur = x
    plan = []
    for group in rounds:
        n = 1 << len(group)
        digit = sum(((me >> b) & 1) << i for i, b in enumerate(group))
        masks = [sum(((t >> i) & 1) << b for i, b in enumerate(group)) for t in range(n)]
        width = cur.shape[1] // n
        total = lax.dynamic_slice_in_dim(cur, digit * width, width, axis=1)
        for t in range(1, n):
            send = lax.dynamic_slice_in_dim(cur, (digit ^ t) * width, width, axis=1)
            total = total + lax.ppermute(send, "vert", [(i, i ^ masks[t]) for i in range(n_vert)])
        cur = total
        plan.append((n, digit, masks))
    cur = finish(cur)
    for n, digit, masks in reversed(plan):
        width = cur.shape[1]
        out = jnp.zeros((cur.shape[0], width * n), cur.dtype)
        out = lax.dynamic_update_slice_in_dim(out, cur, digit * width, axis=1)
        for t in range(1, n):
            got = lax.ppermute(cur, "vert", [(i, i ^ masks[t]) for i in range(n_vert)])
            out = lax.dynamic_update_slice_in_dim(out, got, (digit ^ t) * width, axis=1)
        cur = out
    return cur


def make_shards(n_vert, n_eig):
    pair = n_eig == 2
    swap = [(0, 1), (1, 0)]

    def shards(eig_table, obs_ids, counts, noise_var, eigenvalues, rhs):
        capacity = obs_ids.shape[0]
        own = rhs.shape[0]
        samples = own * n_eig
        group = eig_table.shape[1]
        filled = jnp.arange(capacity, dtype=jnp.int32) < counts[0]
        features = jnp.take(eig_table, obs_ids, axis=0)
        spectrum = 5.0 * jnp.power(3.0 + eigenvalues, -1.5)
        me_eig = lax.axis_index("eig")

        def finish(piece):
            weights = piece[:samples].astype(jnp.bfloat16)
            sums = piece[samples:]
            high = sums.astype(jnp.bfloat16)
            low = (sums - high.astype(jnp.float32)).astype(jnp.bfloat16)
            return jnp.concatenate([weights, high, low], 0)

        def operate(vector):
            lowered = vector.astype(jnp.bfloat16)
            if pair:
                rows = jnp.concatenate([lowered, lax.ppermute(lowered, "eig", swap)], 0)
            else:
                rows = lax.all_gather(lowered, "eig", axis=0, tiled=True)
            coeff = jnp.dot(rows, features, preferred_element_type=jnp.float32)
            sums = jnp.zeros((8, group), jnp.float32)
            sums = sums.at[0, :own].set(jnp.sum(vector * vector, axis=1))
            sums = sums.at[1, :own].set(jnp.sum(noise_var[None, :] * vector * vector, axis=1))
            gathered = vert_sum(
                jnp.concatenate([coeff * spectrum[None, :], sums], 0), n_vert, finish
            )
            weights = gathered[:samples]
            sums = gathered[samples : samples + 8].astype(jnp.float32) + gathered[
                samples + 8 : samples + 16
            ].astype(jnp.float32)
            wide = weights.astype(jnp.float32)
            energy = jnp.sum(wide * wide / spectrum[None, :], axis=1)
            partials = lax.dot_general(
                weights, features, (((1,), (1,)), ((), ())), preferred_element_type=jnp.float32
            ).astype(jnp.bfloat16)
            if pair:
                energy = energy[:own] + lax.ppermute(energy[own:], "eig", swap)
                image = partials[:own].astype(jnp.float32) + lax.ppermute(
                    partials[own:], "eig", swap
                ).astype(jnp.float32)
            else:
                energy = lax.psum_scatter(energy, "eig", scatter_dimension=0, tiled=True)
                image = lax.psum_scatter(
                    partials, "eig", scatter_dimension=0, tiled=True
                ).astype(jnp.float32)
            image = jnp.where(filled[None, :], image, jnp.zeros((), jnp.float32))
            norm = sums[0, :own]
            product = sums[1, :own] + energy
            return image + noise_var[None, :] * vector, norm, product

        residual = jnp.where(filled[None, :], rhs, jnp.zeros((), jnp.float32))
        solution = jnp.zeros_like(residual)
        applied, norm_now, product = operate(residual)
        step_size = norm_now / product
        direction, along = (residual, applied)
        for iteration in range(ITERS):
            solution = solution + step_size[:, None] * direction
            residual = residual - step_size[:, None] * along
            if iteration + 1 < ITERS:
                applied, norm_next, product = operate(residual)
                beta_ratio = norm_next / norm_now
                step_size = norm_next / (product - beta_ratio * norm_next / step_size)
                direction = residual + beta_ratio[:, None] * direction
                along = applied + beta_ratio[:, None] * along
                norm_now = norm_next
        return (solution, residual)

    return shards


def solution(mesh):
    return jax.shard_map(
        make_shards(mesh.shape["vert"], mesh.shape["eig"]),
        mesh=mesh,
        in_specs=(P("vert", "eig"), P("vert"), P("vert"), P("vert"), P("eig"), P("eig", "vert")),
        out_specs=(P("eig", "vert"), P("eig", "vert")),
        check_vma=False,
    )
```

time: 223 us -> 157 us (0.70)
  waiting for transfers between devices: 114 us -> 64.3 us
  between operations: 14.8 us -> 1.8 us
  other arithmetic: 19.4 us -> 10.5 us
  local copies, waits for them, and re-layouts: 19.6 us -> 25.2 us
    ppermute x18 -> x30, waiting for transfers between devices: 84.2 us -> 64.3 us  [the longest x12 43.5 us: vert_sum(): lax.ppermute(send, 'vert', [(i, i ^ masks[t]) for i in range(n_vert)])]
    reduce_scatter x2 -> x0, waiting for transfers between devices: 19.1 us -> none  [operate(): lax.psum_scatter(lax.dot_general(weights, features, (((1,), (1,)), ((), (...]
    all_gather x2 -> x0, waiting for transfers between devices: 10.8 us -> none  [operate(): lax.all_gather(lowered, 'eig', axis=0, tiled=True)]
    select_n x9 -> x0, other arithmetic: 7.73 us -> none  [the longest x1 6.85 us: shards(): jnp.where(filled[:, None], jnp.take(eig_table, obs_ids, axis=0), jnp.zero...]
    dynamic_update_slice x0 -> x16, local copies, waits for them, and re-layouts: none -> 4.46 us  [the longest x12 3.74 us: vert_sum(): out = lax.dynamic_update_slice_in_dim(out, got, (digit ^ t) * width, axis=1)]
    ppermute x18 -> x30, starting transfers between devices: 32.9 us -> 34.8 us  [the longest x12 16.5 us: vert_sum(): lax.ppermute(send, 'vert', [(i, i ^ masks[t]) for i in range(n_vert)])]
  transfers between devices with their start and end apart: 22 -> 30, of which waited for: 21 -> 19; matrix products, arithmetic and copies ran while one was open for 12% -> 16% of each run, Pallas kernels for 0% -> 0%
where the time goes in v2:
time: 157 us; the launch traced here: 156 us
  waiting for transfers between devices  64.3 us (41%)
  starting transfers between devices  34.8 us (22%)
  local copies, waits for them, and re-layouts  25.2 us (16%)
  matrix products  19.7 us (13%)
  other arithmetic  10.5 us (7%)
  between operations  1.8 us (1%)
    ppermute x12, waiting for transfers between devices, vert_sum(): lax.ppermute(send, 'vert', [(i, i ^ masks[t]) for i in range(n_vert)])  43.5 us
    gather x1, local copies, waits for them, and re-layouts, shards(): features = jnp.take(eig_table, obs_ids, axis=0)  18.8 us
    ppermute x12, starting transfers between devices, vert_sum(): lax.ppermute(send, 'vert', [(i, i ^ masks[t]) for i in range(n_vert)])  16.5 us
    ppermute x12, starting transfers between devices, vert_sum(): got = lax.ppermute(cur, 'vert', [(i, i ^ masks[t]) for i in range(n_vert)])  16.4 us
    ppermute x12, waiting for transfers between devices, vert_sum(): got = lax.ppermute(cur, 'vert', [(i, i ^ masks[t]) for i in range(n_vert)])  15.7 us
    dot_general x2, matrix products, operate(): coeff = jnp.dot(rows, features, preferred_element_type=jnp.float32)  10.1 us
    dot_general x2, matrix products, operate(): lax.dot_general(weights, features, (((1,), (1,)), ((), ())), preferred_el...  9.6 us
    dynamic_update_slice x12, local copies, waits for them, and re-layouts, vert_sum(): out = lax.dynamic_update_slice_in_dim(out, got, (digit ^ t) * width, axis=1)  3.74 us
  transfers between devices with their start and end apart: 30, of which 19 were waited for; matrix products, arithmetic and copies ran while one was open for 16% of the time, Pallas kernels for 0%

profile of v2, /device:TPU:0, one launch (start us, length us, event | category | flops | bytes accessed | tf_op | source)
XLA Modules:
  0.0 156.4 jit_solution(3852222586875937901)
XLA Ops:
  1.3 1.5 select_convert_fusion
  2.8 0.6 collective-permute-start
  3.4 18.8 %gather_fusion = bf16[3072,1024]{1,0:T(8,128)(2,1)} fusion(bf16[2048,1024]{1,0:T(8,128)(2,1)} %param.14, s32[3072]{0:T(1024)S(1)} %fusion.37), kind=kCustom, calls=%fused_computation | custom fusion | bytes 12595200 | tf_op jit(solution)/shard_map/jit(_take)/gather | solution.py:48
  22.3 0.4 fusion
  23.0 4.9 %fusion.16 = f32[256,1024]{1,0:T(8,128)S(1)} fusion(bf16[128,3072]{1,0:T(8,128)(2,1)} %collective-permute-done, bf16[128,3072]{1,0:T(8,128)(2,1)S(1)} %select_convert_fusion, f32[1024]{0:T(1024)S(1)} %power_multiply_fusion, bf16[3072,1024]{1,0:T(8,128)(2,1)} %gather_fusion, pred[3072]{0:T(1024)(128)(4,1)S(1)} %compare_and_fusion), kind=kOutput, calls=%fused_computation.34 | convolution fusion | flops 1617166336 | bytes 8920064 | tf_op jit(solution)/shard_map/dot_general | solution.py:65
  27.9 0.9 fusion.35
  28.9 2.5 %collective-permute-start.1 = (f32[264,256]{1,0:T(8,128)}, f32[264,256]{1,0:T(8,128)S(1)}, u32[]{:S(2)}, u32[]{:S(2)}) collective-permute-start(f32[264,256]{1,0:T(8,128)} %get-tuple-element.66), channel_id=1, source_target_pairs={{0,2},{2,0},{4,6},{6,4},{8,10},{10,8},{12,14},{14,12},{16,18},{18,... | collective-permute-start | bytes 811016 | tf_op jit(solution)/shard_map/ppermute | solution.py:23
  31.4 1.5 collective-permute-start.2
  32.9 6.0 %collective-permute-done.1 = f32[264,256]{1,0:T(8,128)S(1)} collective-permute-done((f32[264,256]{1,0:T(8,128)}, f32[264,256]{1,0:T(8,128)S(1)}, u32[]{:S(2)}, u32[]{:S(2)}) %collective-permute-start.1) | collective-permute-done | bytes 270368 | tf_op jit(solution)/shard_map/ppermute | solution.py:23
  38.9 7.0 %collective-permute-done.2 = f32[264,256]{1,0:T(8,128)S(1)} collective-permute-done((f32[264,256]{1,0:T(8,128)}, f32[264,256]{1,0:T(8,128)S(1)}, u32[]{:S(2)}, u32[]{:S(2)}) %collective-permute-start.2) | collective-permute-done | bytes 270368 | tf_op jit(solution)/shard_map/ppermute | solution.py:23
  46.0 0.7 copy-done.5
  46.7 1.1 fusion.34
  48.0 1.6 %collective-permute-start.4 = (f32[264,64]{1,0:T(8,128)S(1)}, f32[264,64]{1,0:T(8,128)S(1)}, u32[]{:S(2)}, u32[]{:S(2)}) collective-permute-start(f32[264,64]{1,0:T(8,128)S(1)} %get-tuple-element.72), channel_id=1, source_target_pairs={{0,8},{2,10},{4,12},{6,14},{8,0},{10,2},{12,4},{14,6},{16,24},{18,... | collective-permute-start | bytes 202760 | tf_op jit(solution)/shard_map/ppermute | solution.py:23
  49.6 2.6 %collective-permute-start.5 = (f32[264,64]{1,0:T(8,128)S(1)}, f32[264,64]{1,0:T(8,128)S(1)}, u32[]{:S(2)}, u32[]{:S(2)}) collective-permute-start(f32[264,64]{1,0:T(8,128)S(1)} %get-tuple-element.74), channel_id=1, source_target_pairs={{0,16},{2,18},{4,20},{6,22},{8,24},{10,26},{12,28},{14,30},{16,0},... | collective-permute-start | bytes 202760 | tf_op jit(solution)/shard_map/ppermute | solution.py:23
  52.4 2.2 %collective-permute-done.4 = f32[264,64]{1,0:T(8,128)S(1)} collective-permute-done((f32[264,64]{1,0:T(8,128)S(1)}, f32[264,64]{1,0:T(8,128)S(1)}, u32[]{:S(2)}, u32[]{:S(2)}) %collective-permute-start.4) | collective-permute-done | bytes 67616 | tf_op jit(solution)/shard_map/ppermute | solution.py:23
  54.6 7.2 %collective-permute-done.5 = f32[264,64]{1,0:T(8,128)S(1)} collective-permute-done((f32[264,64]{1,0:T(8,128)S(1)}, f32[264,64]{1,0:T(8,128)S(1)}, u32[]{:S(2)}, u32[]{:S(2)}) %collective-permute-start.5) | collective-permute-done | bytes 67616 | tf_op jit(solution)/shard_map/ppermute | solution.py:23
  62.0 2.1 %collective-permute-start.7 = (bf16[272,64]{1,0:T(8,128)(2,1)S(1)}, bf16[272,64]{1,0:T(8,128)(2,1)S(1)}, u32[]{:S(2)}, u32[]{:S(2)}) collective-permute-start(bf16[272,64]{1,0:T(8,128)(2,1)S(1)} %pad_maximum_fusion), channel_id=1, source_target_pairs={{0,8},{2,10},{4,12},{6,14},{8,0},{10,2},{12,4},{14,6},{16,24},{18,... | collective-permute-start | bytes 104456 | tf_op jit(solution)/shard_map/ppermute | solution.py:32
  64.0 1.1 collective-permute-start.8
  65.1 1.4 collective-permute-start.9
  66.5 0.3 dynamic_update_slice.48
  66.9 0.6 dynamic_update_slice.49
  67.5 2.9 %collective-permute-done.8 = bf16[272,64]{1,0:T(8,128)(2,1)S(1)} collective-permute-done((bf16[272,64]{1,0:T(8,128)(2,1)S(1)}, bf16[272,64]{1,0:T(8,128)(2,1)S(1)}, u32[]{:S(2)}, u32[]{:S(2)}) %collective-permute-start.8) | collective-permute-done | bytes 34848 | tf_op jit(solution)/shard_map/ppermute | solution.py:32
  70.7 0.7 collective-permute-done.9
  71.3 0.5 dynamic_update_slice.51
  71.9 1.8 %collective-permute-start.10 = (bf16[272,256]{1,0:T(8,128)(2,1)S(1)}, bf16[272,256]{1,0:T(8,128)(2,1)S(1)}, u32[]{:S(2)}, u32[]{:S(2)}) collective-permute-start(bf16[272,256]{1,0:T(8,128)(2,1)S(1)} %dynamic_update_slice.51), channel_id=1, source_target_pairs={{0,2},{2,0},{4,6},{6,4},{8,10},{10,8},{12,14},{14,12},{16,18},{18,... | collective-permute-start | bytes 417800 | tf_op jit(solution)/shard_map/ppermute | solution.py:32
  73.7 0.3 collective-permute-start.11
  74.0 1.4 collective-permute-start.12
  75.5 2.5 %collective-permute-done.10 = bf16[272,256]{1,0:T(8,128)(2,1)S(1)} collective-permute-done((bf16[272,256]{1,0:T(8,128)(2,1)S(1)}, bf16[272,256]{1,0:T(8,128)(2,1)S(1)}, u32[]{:S(2)}, u32[]{:S(2)}) %collective-permute-start.10) | collective-permute-done | bytes 139296 | tf_op jit(solution)/shard_map/ppermute | solution.py:32
  78.1 2.1 %collective-permute-done.11 = bf16[272,256]{1,0:T(8,128)(2,1)S(1)} collective-permute-done((bf16[272,256]{1,0:T(8,128)(2,1)S(1)}, bf16[272,256]{1,0:T(8,128)(2,1)S(1)}, u32[]{:S(2)}, u32[]{:S(2)}) %collective-permute-start.11) | collective-permute-done | bytes 139296 | tf_op jit(solution)/shard_map/ppermute | solution.py:32
  80.3 4.8 %convolution_convert_fusion.1 = bf16[256,3072]{1,0:T(8,128)(2,1)S(1)} fusion(bf16[272,1024]{1,0:T(8,128)(2,1)S(1)} %constant_dynamic-update-slice_fusion.4, bf16[3072,1024]{1,0:T(8,128)(2,1)} %gather_fusion, pred[3072]{0:T(1024)(128)(4,1)S(1)} %compare_and_fusion), kind=kOutput, calls=%fused_computation.3 | convolution fusion | flops 1614544896 | bytes 8391680 | tf_op jit(solution)/shard_map/dot_general | solution.py:78
  85.4 0.6 collective-permute-start.13
  86.0 1.5 collective-permute-done.13
  87.5 0.9 fusion.1
  88.4 1.0 convert_element_type.72
  89.6 0.3 scatter.19
  89.9 2.2 %collective-permute-done.15 = bf16[128,3072]{1,0:T(8,128)(2,1)} collective-permute-done((bf16[128,3072]{1,0:T(8,128)(2,1)}, bf16[128,3072]{1,0:T(8,128)(2,1)}, u32[]{:S(2)}, u32[]{:S(2)}) %collective-permute-start.15) | collective-permute-done | bytes 786464 | tf_op jit(solution)/shard_map/ppermute | solution.py:62
  92.0 5.2 %fusion.13 = f32[256,1024]{1,0:T(8,128)S(1)} fusion(bf16[128,3072]{1,0:T(8,128)(2,1)} %collective-permute-done.15, bf16[128,3072]{1,0:T(8,128)(2,1)} %convert_element_type.72, f32[1024]{0:T(1024)S(1)} %power_multiply_fusion, bf16[3072,1024]{1,0:T(8,128)(2,1)} %gather_fusion, pred[3072]{0:T(1024)(128)(4,1)S(1)} %compare_and_fusion), kind=kOutput, calls=%fused_computation.33 | convolution fusion | flops 1617166336 | bytes 8920064 | tf_op jit(solution)/shard_map/dot_general | solution.py:65
  97.3 1.7 %collective-permute-start.16 = (f32[264,256]{1,0:T(8,128)S(1)}, f32[264,256]{1,0:T(8,128)S(1)}, u32[]{:S(2)}, u32[]{:S(2)}) collective-permute-start(f32[264,256]{1,0:T(8,128)S(1)} %get-tuple-element.63), channel_id=1, source_target_pairs={{0,2},{2,0},{4,6},{6,4},{8,10},{10,8},{12,14},{14,12},{16,18},{18,... | collective-permute-start | bytes 811016 | tf_op jit(solution)/shard_map/ppermute | solution.py:23
  99.0 0.6 collective-permute-start.17
  99.6 1.2 collective-permute-start.18
  100.9 5.9 %collective-permute-done.16 = f32[264,256]{1,0:T(8,128)S(1)} collective-permute-done((f32[264,256]{1,0:T(8,128)S(1)}, f32[264,256]{1,0:T(8,128)S(1)}, u32[]{:S(2)}, u32[]{:S(2)}) %collective-permute-start.16) | collective-permute-done | bytes 270368 | tf_op jit(solution)/shard_map/ppermute | solution.py:23
  106.7 6.3 %collective-permute-done.17 = f32[264,256]{1,0:T(8,128)S(1)} collective-permute-done((f32[264,256]{1,0:T(8,128)S(1)}, f32[264,256]{1,0:T(8,128)S(1)}, u32[]{:S(2)}, u32[]{:S(2)}) %collective-permute-start.17) | collective-permute-done | bytes 270368 | tf_op jit(solution)/shard_map/ppermute | solution.py:23
  113.4 1.0 collective-permute-start.19
  114.3 2.3 %collective-permute-start.20 = (f32[264,64]{1,0:T(8,128)S(1)}, f32[264,64]{1,0:T(8,128)S(1)}, u32[]{:S(2)}, u32[]{:S(2)}) collective-permute-start(f32[264,64]{1,0:T(8,128)S(1)} %get-tuple-element.71), channel_id=1, source_target_pairs={{0,16},{2,18},{4,20},{6,22},{8,24},{10,26},{12,28},{14,30},{16,0},... | collective-permute-start | bytes 202760 | tf_op jit(solution)/shard_map/ppermute | solution.py:23
  116.6 1.2 collective-permute-start.21
  117.8 1.4 collective-permute-done.19
  119.2 7.5 %collective-permute-done.20 = f32[264,64]{1,0:T(8,128)S(1)} collective-permute-done((f32[264,64]{1,0:T(8,128)S(1)}, f32[264,64]{1,0:T(8,128)S(1)}, u32[]{:S(2)}, u32[]{:S(2)}) %collective-permute-start.20) | collective-permute-done | bytes 67616 | tf_op jit(solution)/shard_map/ppermute | solution.py:23
  126.9 2.1 %collective-permute-start.22 = (bf16[272,64]{1,0:T(8,128)(2,1)S(1)}, bf16[272,64]{1,0:T(8,128)(2,1)}, u32[]{:S(2)}, u32[]{:S(2)}) collective-permute-start(bf16[272,64]{1,0:T(8,128)(2,1)S(1)} %pad_maximum_fusion.1), channel_id=1, source_target_pairs={{0,8},{2,10},{4,12},{6,14},{8,0},{10,2},{12,4},{14,6},{16,24},{18,... | collective-permute-start | bytes 104456 | tf_op jit(solution)/shard_map/ppermute | solution.py:32
  129.0 1.3 collective-permute-start.23
  130.2 1.4 collective-permute-start.24
  131.6 0.3 dynamic_update_slice.56
  132.1 1.4 dynamic_update_slice.57
  133.5 3.0 %collective-permute-done.23 = bf16[272,64]{1,0:T(8,128)(2,1)S(1)} collective-permute-done((bf16[272,64]{1,0:T(8,128)(2,1)S(1)}, bf16[272,64]{1,0:T(8,128)(2,1)S(1)}, u32[]{:S(2)}, u32[]{:S(2)}) %collective-permute-start.23) | collective-permute-done | bytes 34848 | tf_op jit(solution)/shard_map/ppermute | solution.py:32
  136.8 0.6 dynamic_update_slice.59
  137.4 1.0 collective-permute-start.25
  138.4 0.7 collective-permute-start.26
  139.1 1.8 %collective-permute-start.27 = (bf16[272,256]{1,0:T(8,128)(2,1)S(1)}, bf16[272,256]{1,0:T(8,128)(2,1)S(1)}, u32[]{:S(2)}, u32[]{:S(2)}) collective-permute-start(bf16[272,256]{1,0:T(8,128)(2,1)S(1)} %dynamic_update_slice.59), channel_id=1, source_target_pairs={{0,6},{2,4},{4,2},{6,0},{8,14},{10,12},{12,10},{14,8},{16,22},{18,... | collective-permute-start | bytes 417800 | tf_op jit(solution)/shard_map/ppermute | solution.py:32
  141.0 1.9 %collective-permute-done.25 = bf16[272,256]{1,0:T(8,128)(2,1)S(1)} collective-permute-done((bf16[272,256]{1,0:T(8,128)(2,1)S(1)}, bf16[272,256]{1,0:T(8,128)(2,1)S(1)}, u32[]{:S(2)}, u32[]{:S(2)}) %collective-permute-start.25) | collective-permute-done | bytes 139296 | tf_op jit(solution)/shard_map/ppermute | solution.py:32
  143.0 2.4 %collective-permute-done.26 = bf16[272,256]{1,0:T(8,128)(2,1)S(1)} collective-permute-done((bf16[272,256]{1,0:T(8,128)(2,1)S(1)}, bf16[272,256]{1,0:T(8,128)(2,1)S(1)}, u32[]{:S(2)}, u32[]{:S(2)}) %collective-permute-start.26) | collective-permute-done | bytes 139296 | tf_op jit(solution)/shard_map/ppermute | solution.py:32
  145.4 4.8 %convolution_convert_fusion = bf16[256,3072]{1,0:T(8,128)(2,1)S(1)} fusion(bf16[272,1024]{1,0:T(8,128)(2,1)S(1)} %constant_dynamic-update-slice_fusion, bf16[3072,1024]{1,0:T(8,128)(2,1)} %gather_fusion, pred[3072]{0:T(1024)(128)(4,1)S(1)} %compare_and_fusion), kind=kOutput, calls=%fused_computation.2 | convolution fusion | flops 1614544896 | bytes 8391680 | tf_op jit(solution)/shard_map/dot_general | solution.py:78
  150.7 0.6 collective-permute-start.28
  151.2 1.5 collective-permute-done.28
  152.7 0.8 fusion.40
  153.5 2.9 %fusion.4 = (f32[128,3072]{1,0:T(8,128)}, f32[128,3072]{1,0:T(8,128)}) fusion(f32[128,3072]{1,0:T(8,128)S(1)} %get-tuple-element.58, bf16[128,3072]{1,0:T(8,128)(2,1)S(1)} %collective-permute-done.29, bf16[128,3072]{1,0:T(8,128)(2,1)S(1)} %copy-done.4, f32[128,3072]{1,0:T(8,128)S(1)} %copy-done, bf16[256,3072]{1,0:T(8,128)(2,1)S(1)} %convolution_convert_fusion, ...), kind=kLoop, calls=%fused_computation.20 | loop fusion | flops 8650752 | bytes 9454080 | tf_op jit(solution)/shard_map/sub | solution.py:103
  (78 shorter events, 3.2 us)
Async XLA Ops:
  0.6 2.8 %copy-start.7 = (s32[3072]{0:T(1024)S(1)}, s32[3072]{0:T(1024)}, u32[]{:S(2)}) copy-start(s32[3072]{0:T(1024)} %param.15) | copy-start | bytes 36868
  2.8 20.1 %collective-permute-start = (bf16[128,3072]{1,0:T(8,128)(2,1)S(1)}, bf16[128,3072]{1,0:T(8,128)(2,1)}, u32[]{:S(2)}, u32[]{:S(2)}) collective-permute-start(bf16[128,3072]{1,0:T(8,128)(2,1)S(1)} %select_convert_fusion), channel_id=1, source_target_pairs={{0,1},{1,0},{2,3},{3,2},{4,5},{5,4},{6,7},{7,6},{8,9},{9,8},{10,11... | collective-permute-start | bytes 2359304 | tf_op jit(solution)/shard_map/ppermute | solution.py:62
  3.4 18.8 %copy-start = (f32[128,3072]{1,0:T(8,128)S(1)}, f32[128,3072]{1,0:T(8,128)}, u32[]{:S(2)}) copy-start(f32[128,3072]{1,0:T(8,128)} %param.19) | copy-start | bytes 4718596
  3.4 18.8 %copy-start.6 = (f32[3072]{0:T(1024)S(1)}, f32[3072]{0:T(1024)}, u32[]{:S(2)}) copy-start(f32[3072]{0:T(1024)} %param.17) | copy-start | bytes 36868
  22.3 0.7 copy-start.9
  28.9 10.1 %collective-permute-start.1 = (f32[264,256]{1,0:T(8,128)}, f32[264,256]{1,0:T(8,128)S(1)}, u32[]{:S(2)}, u32[]{:S(2)}) collective-permute-start(f32[264,256]{1,0:T(8,128)} %get-tuple-element.66), channel_id=1, source_target_pairs={{0,2},{2,0},{4,6},{6,4},{8,10},{10,8},{12,14},{14,12},{16,18},{18,... | collective-permute-start | bytes 811016 | tf_op jit(solution)/shard_map/ppermute | solution.py:23
  31.4 14.6 %collective-permute-start.2 = (f32[264,256]{1,0:T(8,128)}, f32[264,256]{1,0:T(8,128)S(1)}, u32[]{:S(2)}, u32[]{:S(2)}) collective-permute-start(f32[264,256]{1,0:T(8,128)} %get-tuple-element.67), channel_id=1, source_target_pairs={{0,4},{2,6},{4,0},{6,2},{8,12},{10,14},{12,8},{14,10},{16,20},{18,... | collective-permute-start | bytes 811016 | tf_op jit(solution)/shard_map/ppermute | solution.py:23
  32.9 13.8 %collective-permute-start.3 = (f32[264,256]{1,0:T(8,128)}, f32[264,256]{1,0:T(8,128)}, u32[]{:S(2)}, u32[]{:S(2)}) collective-permute-start(f32[264,256]{1,0:T(8,128)} %get-tuple-element.68), channel_id=1, source_target_pairs={{0,6},{2,4},{4,2},{6,0},{8,14},{10,12},{12,10},{14,8},{16,22},{18,... | collective-permute-start | bytes 811016 | tf_op jit(solution)/shard_map/ppermute | solution.py:23
  46.0 0.7 copy-start.5
  48.0 6.7 %collective-permute-start.4 = (f32[264,64]{1,0:T(8,128)S(1)}, f32[264,64]{1,0:T(8,128)S(1)}, u32[]{:S(2)}, u32[]{:S(2)}) collective-permute-start(f32[264,64]{1,0:T(8,128)S(1)} %get-tuple-element.72), channel_id=1, source_target_pairs={{0,8},{2,10},{4,12},{6,14},{8,0},{10,2},{12,4},{14,6},{16,24},{18,... | collective-permute-start | bytes 202760 | tf_op jit(solution)/shard_map/ppermute | solution.py:23
  49.6 12.2 %collective-permute-start.5 = (f32[264,64]{1,0:T(8,128)S(1)}, f32[264,64]{1,0:T(8,128)S(1)}, u32[]{:S(2)}, u32[]{:S(2)}) collective-permute-start(f32[264,64]{1,0:T(8,128)S(1)} %get-tuple-element.74), channel_id=1, source_target_pairs={{0,16},{2,18},{4,20},{6,22},{8,24},{10,26},{12,28},{14,30},{16,0},... | collective-permute-start | bytes 202760 | tf_op jit(solution)/shard_map/ppermute | solution.py:23
  52.2 9.6 %collective-permute-start.6 = (f32[264,64]{1,0:T(8,128)S(1)}, f32[264,64]{1,0:T(8,128)S(1)}, u32[]{:S(2)}, u32[]{:S(2)}) collective-permute-start(f32[264,64]{1,0:T(8,128)S(1)} %get-tuple-element.73), channel_id=1, source_target_pairs={{0,24},{2,26},{4,28},{6,30},{8,16},{10,18},{12,20},{14,22},{16,8},... | collective-permute-start | bytes 202760 | tf_op jit(solution)/shard_map/ppermute | solution.py:23
  62.0 4.9 %collective-permute-start.7 = (bf16[272,64]{1,0:T(8,128)(2,1)S(1)}, bf16[272,64]{1,0:T(8,128)(2,1)S(1)}, u32[]{:S(2)}, u32[]{:S(2)}) collective-permute-start(bf16[272,64]{1,0:T(8,128)(2,1)S(1)} %pad_maximum_fusion), channel_id=1, source_target_pairs={{0,8},{2,10},{4,12},{6,14},{8,0},{10,2},{12,4},{14,6},{16,24},{18,... | collective-permute-start | bytes 104456 | tf_op jit(solution)/shard_map/ppermute | solution.py:32
  64.0 6.4 %collective-permute-start.8 = (bf16[272,64]{1,0:T(8,128)(2,1)S(1)}, bf16[272,64]{1,0:T(8,128)(2,1)S(1)}, u32[]{:S(2)}, u32[]{:S(2)}) collective-permute-start(bf16[272,64]{1,0:T(8,128)(2,1)S(1)} %pad_maximum_fusion), channel_id=1, source_target_pairs={{0,16},{2,18},{4,20},{6,22},{8,24},{10,26},{12,28},{14,30},{16,0},... | collective-permute-start | bytes 104456 | tf_op jit(solution)/shard_map/ppermute | solution.py:32
  65.1 6.2 %collective-permute-start.9 = (bf16[272,64]{1,0:T(8,128)(2,1)S(1)}, bf16[272,64]{1,0:T(8,128)(2,1)S(1)}, u32[]{:S(2)}, u32[]{:S(2)}) collective-permute-start(bf16[272,64]{1,0:T(8,128)(2,1)S(1)} %pad_maximum_fusion), channel_id=1, source_target_pairs={{0,24},{2,26},{4,28},{6,30},{8,16},{10,18},{12,20},{14,22},{16,8},... | collective-permute-start | bytes 104456 | tf_op jit(solution)/shard_map/ppermute | solution.py:32
  71.9 6.2 %collective-permute-start.10 = (bf16[272,256]{1,0:T(8,128)(2,1)S(1)}, bf16[272,256]{1,0:T(8,128)(2,1)S(1)}, u32[]{:S(2)}, u32[]{:S(2)}) collective-permute-start(bf16[272,256]{1,0:T(8,128)(2,1)S(1)} %dynamic_update_slice.51), channel_id=1, source_target_pairs={{0,2},{2,0},{4,6},{6,4},{8,10},{10,8},{12,14},{14,12},{16,18},{18,... | collective-permute-start | bytes 417800 | tf_op jit(solution)/shard_map/ppermute | solution.py:32
  73.7 6.5 %collective-permute-start.11 = (bf16[272,256]{1,0:T(8,128)(2,1)S(1)}, bf16[272,256]{1,0:T(8,128)(2,1)S(1)}, u32[]{:S(2)}, u32[]{:S(2)}) collective-permute-start(bf16[272,256]{1,0:T(8,128)(2,1)S(1)} %dynamic_update_slice.51), channel_id=1, source_target_pairs={{0,4},{2,6},{4,0},{6,2},{8,12},{10,14},{12,8},{14,10},{16,20},{18,... | collective-permute-start | bytes 417800 | tf_op jit(solution)/shard_map/ppermute | solution.py:32
  74.0 6.2 %collective-permute-start.12 = (bf16[272,256]{1,0:T(8,128)(2,1)S(1)}, bf16[272,256]{1,0:T(8,128)(2,1)S(1)}, u32[]{:S(2)}, u32[]{:S(2)}) collective-permute-start(bf16[272,256]{1,0:T(8,128)(2,1)S(1)} %dynamic_update_slice.51), channel_id=1, source_target_pairs={{0,6},{2,4},{4,2},{6,0},{8,14},{10,12},{12,10},{14,8},{16,22},{18,... | collective-permute-start | bytes 417800 | tf_op jit(solution)/shard_map/ppermute | solution.py:32
  85.0 3.4 %copy-start.1 = (bf16[256,3072]{1,0:T(8,128)(2,1)}, bf16[256,3072]{1,0:T(8,128)(2,1)S(1)}, u32[]{:S(2)}) copy-start(bf16[256,3072]{1,0:T(8,128)(2,1)S(1)} %convolution_convert_fusion.1) | copy-start | bytes 4718596
  85.1 2.4 %collective-permute-start.14 = (bf16[128,3072]{1,0:T(8,128)(2,1)S(1)}, bf16[128,3072]{1,0:T(8,128)(2,1)S(1)}, u32[]{:S(2)}, u32[]{:S(2)}) collective-permute-start(bf16[128,3072]{1,0:T(8,128)(2,1)S(1)} %slice.168), channel_id=1, source_target_pairs={{0,1},{1,0},{2,3},{3,2},{4,5},{5,4},{6,7},{7,6},{8,9},{9,8},{10,11... | collective-permute-start | bytes 2359304 | tf_op jit(solution)/shard_map/ppermute | solution.py:83
  85.4 2.0 %collective-permute-start.13 = (f32[128]{0:T(128)S(1)}, f32[128]{0:T(128)S(1)}, u32[]{:S(2)}, u32[]{:S(2)}) collective-permute-start(f32[128]{0:T(128)S(1)} %slice.144), channel_id=1, source_target_pairs={{0,1},{1,0},{2,3},{3,2},{4,5},{5,4},{6,7},{7,6},{8,9},{9,8},{10,11... | collective-permute-start | bytes 1544 | tf_op jit(solution)/shard_map/ppermute | solution.py:82
  86.0 1.5 copy-start.8
  87.5 0.9 copy-start.3
  89.4 2.6 %collective-permute-start.15 = (bf16[128,3072]{1,0:T(8,128)(2,1)}, bf16[128,3072]{1,0:T(8,128)(2,1)}, u32[]{:S(2)}, u32[]{:S(2)}) collective-permute-start(bf16[128,3072]{1,0:T(8,128)(2,1)} %convert_element_type.72), channel_id=1, source_target_pairs={{0,1},{1,0},{2,3},{3,2},{4,5},{5,4},{6,7},{7,6},{8,9},{9,8},{10,11... | collective-permute-start | bytes 2359304 | tf_op jit(solution)/shard_map/ppermute | solution.py:62
  97.3 9.4 %collective-permute-start.16 = (f32[264,256]{1,0:T(8,128)S(1)}, f32[264,256]{1,0:T(8,128)S(1)}, u32[]{:S(2)}, u32[]{:S(2)}) collective-permute-start(f32[264,256]{1,0:T(8,128)S(1)} %get-tuple-element.63), channel_id=1, source_target_pairs={{0,2},{2,0},{4,6},{6,4},{8,10},{10,8},{12,14},{14,12},{16,18},{18,... | collective-permute-start | bytes 811016 | tf_op jit(solution)/shard_map/ppermute | solution.py:23
  99.0 14.0 %collective-permute-start.17 = (f32[264,256]{1,0:T(8,128)S(1)}, f32[264,256]{1,0:T(8,128)S(1)}, u32[]{:S(2)}, u32[]{:S(2)}) collective-permute-start(f32[264,256]{1,0:T(8,128)S(1)} %get-tuple-element.64), channel_id=1, source_target_pairs={{0,4},{2,6},{4,0},{6,2},{8,12},{10,14},{12,8},{14,10},{16,20},{18,... | collective-permute-start | bytes 811016 | tf_op jit(solution)/shard_map/ppermute | solution.py:23
  99.6 13.4 %collective-permute-start.18 = (f32[264,256]{1,0:T(8,128)S(1)}, f32[264,256]{1,0:T(8,128)S(1)}, u32[]{:S(2)}, u32[]{:S(2)}) collective-permute-start(f32[264,256]{1,0:T(8,128)S(1)} %get-tuple-element.65), channel_id=1, source_target_pairs={{0,6},{2,4},{4,2},{6,0},{8,14},{10,12},{12,10},{14,8},{16,22},{18,... | collective-permute-start | bytes 811016 | tf_op jit(solution)/shard_map/ppermute | solution.py:23
  113.4 5.9 %collective-permute-start.19 = (f32[264,64]{1,0:T(8,128)S(1)}, f32[264,64]{1,0:T(8,128)S(1)}, u32[]{:S(2)}, u32[]{:S(2)}) collective-permute-start(f32[264,64]{1,0:T(8,128)S(1)} %get-tuple-element.69), channel_id=1, source_target_pairs={{0,8},{2,10},{4,12},{6,14},{8,0},{10,2},{12,4},{14,6},{16,24},{18,... | collective-permute-start | bytes 202760 | tf_op jit(solution)/shard_map/ppermute | solution.py:23
  114.3 12.4 %collective-permute-start.20 = (f32[264,64]{1,0:T(8,128)S(1)}, f32[264,64]{1,0:T(8,128)S(1)}, u32[]{:S(2)}, u32[]{:S(2)}) collective-permute-start(f32[264,64]{1,0:T(8,128)S(1)} %get-tuple-element.71), channel_id=1, source_target_pairs={{0,16},{2,18},{4,20},{6,22},{8,24},{10,26},{12,28},{14,30},{16,0},... | collective-permute-start | bytes 202760 | tf_op jit(solution)/shard_map/ppermute | solution.py:23
  116.6 10.1 %collective-permute-start.21 = (f32[264,64]{1,0:T(8,128)S(1)}, f32[264,64]{1,0:T(8,128)S(1)}, u32[]{:S(2)}, u32[]{:S(2)}) collective-permute-start(f32[264,64]{1,0:T(8,128)S(1)} %get-tuple-element.70), channel_id=1, source_target_pairs={{0,24},{2,26},{4,28},{6,30},{8,16},{10,18},{12,20},{14,22},{16,8},... | collective-permute-start | bytes 202760 | tf_op jit(solution)/shard_map/ppermute | solution.py:23
  126.9 5.2 %collective-permute-start.22 = (bf16[272,64]{1,0:T(8,128)(2,1)S(1)}, bf16[272,64]{1,0:T(8,128)(2,1)}, u32[]{:S(2)}, u32[]{:S(2)}) collective-permute-start(bf16[272,64]{1,0:T(8,128)(2,1)S(1)} %pad_maximum_fusion.1), channel_id=1, source_target_pairs={{0,8},{2,10},{4,12},{6,14},{8,0},{10,2},{12,4},{14,6},{16,24},{18,... | collective-permute-start | bytes 104456 | tf_op jit(solution)/shard_map/ppermute | solution.py:32
  129.0 7.6 %collective-permute-start.23 = (bf16[272,64]{1,0:T(8,128)(2,1)S(1)}, bf16[272,64]{1,0:T(8,128)(2,1)S(1)}, u32[]{:S(2)}, u32[]{:S(2)}) collective-permute-start(bf16[272,64]{1,0:T(8,128)(2,1)S(1)} %pad_maximum_fusion.1), channel_id=1, source_target_pairs={{0,16},{2,18},{4,20},{6,22},{8,24},{10,26},{12,28},{14,30},{16,0},... | collective-permute-start | bytes 104456 | tf_op jit(solution)/shard_map/ppermute | solution.py:32
  130.2 6.6 %collective-permute-start.24 = (bf16[272,64]{1,0:T(8,128)(2,1)S(1)}, bf16[272,64]{1,0:T(8,128)(2,1)S(1)}, u32[]{:S(2)}, u32[]{:S(2)}) collective-permute-start(bf16[272,64]{1,0:T(8,128)(2,1)S(1)} %pad_maximum_fusion.1), channel_id=1, source_target_pairs={{0,24},{2,26},{4,28},{6,30},{8,16},{10,18},{12,20},{14,22},{16,8},... | collective-permute-start | bytes 104456 | tf_op jit(solution)/shard_map/ppermute | solution.py:32
  137.4 5.6 %collective-permute-start.25 = (bf16[272,256]{1,0:T(8,128)(2,1)S(1)}, bf16[272,256]{1,0:T(8,128)(2,1)S(1)}, u32[]{:S(2)}, u32[]{:S(2)}) collective-permute-start(bf16[272,256]{1,0:T(8,128)(2,1)S(1)} %dynamic_update_slice.59), channel_id=1, source_target_pairs={{0,2},{2,0},{4,6},{6,4},{8,10},{10,8},{12,14},{14,12},{16,18},{18,... | collective-permute-start | bytes 417800 | tf_op jit(solution)/shard_map/ppermute | solution.py:32
  138.4 7.0 %collective-permute-start.26 = (bf16[272,256]{1,0:T(8,128)(2,1)S(1)}, bf16[272,256]{1,0:T(8,128)(2,1)S(1)}, u32[]{:S(2)}, u32[]{:S(2)}) collective-permute-start(bf16[272,256]{1,0:T(8,128)(2,1)S(1)} %dynamic_update_slice.59), channel_id=1, source_target_pairs={{0,4},{2,6},{4,0},{6,2},{8,12},{10,14},{12,8},{14,10},{16,20},{18,... | collective-permute-start | bytes 417800 | tf_op jit(solution)/shard_map/ppermute | solution.py:32
  139.1 6.3 %collective-permute-start.27 = (bf16[272,256]{1,0:T(8,128)(2,1)S(1)}, bf16[272,256]{1,0:T(8,128)(2,1)S(1)}, u32[]{:S(2)}, u32[]{:S(2)}) collective-permute-start(bf16[272,256]{1,0:T(8,128)(2,1)S(1)} %dynamic_update_slice.59), channel_id=1, source_target_pairs={{0,6},{2,4},{4,2},{6,0},{8,14},{10,12},{12,10},{14,8},{16,22},{18,... | collective-permute-start | bytes 417800 | tf_op jit(solution)/shard_map/ppermute | solution.py:32
  145.4 8.1 %copy-start.4 = (bf16[128,3072]{1,0:T(8,128)(2,1)S(1)}, bf16[128,3072]{1,0:T(8,128)(2,1)}, u32[]{:S(2)}) copy-start(bf16[128,3072]{1,0:T(8,128)(2,1)} %copy-done.3) | copy-start | bytes 2359300
  150.3 3.2 %copy-start.2 = (bf16[256,3072]{1,0:T(8,128)(2,1)S(1)}, bf16[256,3072]{1,0:T(8,128)(2,1)}, u32[]{:S(2)}) copy-start(bf16[256,3072]{1,0:T(8,128)(2,1)} %copy-done.1) | copy-start | bytes 4718596
  150.4 3.1 %collective-permute-start.29 = (bf16[128,3072]{1,0:T(8,128)(2,1)S(1)}, bf16[128,3072]{1,0:T(8,128)(2,1)S(1)}, u32[]{:S(2)}, u32[]{:S(2)}) collective-permute-start(bf16[128,3072]{1,0:T(8,128)(2,1)S(1)} %slice.177), channel_id=1, source_target_pairs={{0,1},{1,0},{2,3},{3,2},{4,5},{5,4},{6,7},{7,6},{8,9},{9,8},{10,11... | collective-permute-start | bytes 2359304 | tf_op jit(solution)/shard_map/ppermute | solution.py:83
  150.7 2.0 %collective-permute-start.28 = (f32[128]{0:T(128)S(1)}, f32[128]{0:T(128)S(1)}, u32[]{:S(2)}, u32[]{:S(2)}) collective-permute-start(f32[128]{0:T(128)S(1)} %slice.155), channel_id=1, source_target_pairs={{0,1},{1,0},{2,3},{3,2},{4,5},{5,4},{6,7},{7,6},{8,9},{9,8},{10,11... | collective-permute-start | bytes 1544 | tf_op jit(solution)/shard_map/ppermute | solution.py:82

commit v3 on v2

--- a/solution.py
+++ b/solution.py
@@ -6,13 +6,13 @@
 ITERS = 2
 
 
-def vert_sum(x, n_vert, finish):
+def vert_sum(x, n_vert, finish, encode, decode):
     bits = n_vert.bit_length() - 1
     rounds = [list(range(b, min(b + 2, bits))) for b in range(0, bits, 2)]
     me = lax.axis_index("vert")
     cur = x
     plan = []
-    for group in rounds:
+    for first, group in enumerate(rounds):
         n = 1 << len(group)
         digit = sum(((me >> b) & 1) << i for i, b in enumerate(group))
         masks = [sum(((t >> i) & 1) << b for i, b in enumerate(group)) for t in range(n)]
@@ -20,7 +20,10 @@
         total = lax.dynamic_slice_in_dim(cur, digit * width, width, axis=1)
         for t in range(1, n):
             send = lax.dynamic_slice_in_dim(cur, (digit ^ t) * width, width, axis=1)
-            total = total + lax.ppermute(send, "vert", [(i, i ^ masks[t]) for i in range(n_vert)])
+            if first == 0:
+                send = encode(send)
+            got = lax.ppermute(send, "vert", [(i, i ^ masks[t]) for i in range(n_vert)])
+            total = total + (decode(got) if first == 0 else got)
         cur = total
         plan.append((n, digit, masks))
     cur = finish(cur)
@@ -56,6 +59,16 @@
             low = (sums - high.astype(jnp.float32)).astype(jnp.bfloat16)
             return jnp.concatenate([weights, high, low], 0)
 
+        def decode(block):
+            return jnp.concatenate(
+                [
+                    block[:samples].astype(jnp.float32),
+                    block[samples : samples + 8].astype(jnp.float32)
+                    + block[samples + 8 :].astype(jnp.float32),
+                ],
+                0,
+            )
+
         def operate(vector):
             lowered = vector.astype(jnp.bfloat16)
             if pair:
@@ -67,7 +80,7 @@
             sums = sums.at[0, :own].set(jnp.sum(vector * vector, axis=1))
             sums = sums.at[1, :own].set(jnp.sum(noise_var[None, :] * vector * vector, axis=1))
             gathered = vert_sum(
-                jnp.concatenate([coeff * spectrum[None, :], sums], 0), n_vert, finish
+                jnp.concatenate([coeff * spectrum[None, :], sums], 0), n_vert, finish, finish, decode
             )
             weights = gathered[:samples]
             sums = gathered[samples : samples + 8].astype(jnp.float32) + gathered[

time: 157 us -> 145 us (0.924)
  waiting for transfers between devices: 64.3 us -> 53.5 us
  other arithmetic: 10.5 us -> 8.22 us
  starting transfers between devices: 34.8 us -> 36.7 us
    ppermute x12, waiting for transfers between devices: 43.5 us -> 32.1 us  [vert_sum(): got = lax.ppermute(send, 'vert', [(i, i ^ masks[t]) for i in range(n_vert)])]
  transfers between devices with their start and end apart: 30 -> 30, of which waited for: 19 -> 21; matrix products, arithmetic and copies ran while one was open for 16% -> 16% of each run, Pallas kernels for 0% -> 0%
where the time goes in v3:
time: 145 us; the launch traced here: 144 us
  waiting for transfers between devices  53.5 us (37%)
  starting transfers between devices  36.7 us (25%)
  local copies, waits for them, and re-layouts  24.5 us (17%)
  matrix products  19.4 us (13%)
  other arithmetic  8.22 us (6%)
  between operations  2.02 us (1%)
    ppermute x12, waiting for transfers between devices, vert_sum(): got = lax.ppermute(send, 'vert', [(i, i ^ masks[t]) for i in range(n_vert)])  32.1 us
    gather x1, local copies, waits for them, and re-layouts, shards(): features = jnp.take(eig_table, obs_ids, axis=0)  18.7 us
    ppermute x12, starting transfers between devices, vert_sum(): got = lax.ppermute(cur, 'vert', [(i, i ^ masks[t]) for i in range(n_vert)])  17.9 us
    ppermute x12, starting transfers between devices, vert_sum(): got = lax.ppermute(send, 'vert', [(i, i ^ masks[t]) for i in range(n_vert)])  16.9 us
    ppermute x12, waiting for transfers between devices, vert_sum(): got = lax.ppermute(cur, 'vert', [(i, i ^ masks[t]) for i in range(n_vert)])  16.2 us
    dot_general x2, matrix products, operate(): coeff = jnp.dot(rows, features, preferred_element_type=jnp.float32)  9.83 us
    dot_general x2, matrix products, operate(): lax.dot_general(weights, features, (((1,), (1,)), ((), ())), preferred_el...  9.56 us
    dynamic_update_slice x12, local copies, waits for them, and re-layouts, vert_sum(): out = lax.dynamic_update_slice_in_dim(out, got, (digit ^ t) * width, axis=1)  3.76 us
  transfers between devices with their start and end apart: 30, of which 21 were waited for; matrix products, arithmetic and copies ran while one was open for 16% of the time, Pallas kernels for 0%

profile of v3, /device:TPU:0, one launch (start us, length us, event | category | flops | bytes accessed | tf_op | source)
XLA Modules:
  0.0 144.3 jit_solution(4318062191011632901)
XLA Ops:
  1.3 1.5 %select_convert_fusion = bf16[128,3072]{1,0:T(8,128)(2,1)S(1)} fusion(f32[128,3072]{1,0:T(8,128)} %param.19, pred[3072]{0:T(1024)(128)(4,1)S(1)} %iota_compare_fusion), kind=kLoop, calls=%fused_computation.35 | loop fusion | flops 393216 | bytes 2362368 | tf_op jit(solution)/shard_map/convert_element_type | solution.py:73
  2.9 0.6 collective-permute-start
  3.4 18.7 %gather_fusion = bf16[3072,1024]{1,0:T(8,128)(2,1)} fusion(bf16[2048,1024]{1,0:T(8,128)(2,1)} %param.14, s32[3072]{0:T(1024)S(1)} %fusion.37), kind=kCustom, calls=%fused_computation | custom fusion | bytes 12595200 | tf_op jit(solution)/shard_map/jit(_take)/gather | solution.py:51
  22.1 0.4 fusion
  22.6 0.2 scatter.15
  22.9 4.7 %fusion.16 = f32[256,1024]{1,0:T(8,128)S(1)} fusion(bf16[128,3072]{1,0:T(8,128)(2,1)S(1)} %collective-permute-done, bf16[128,3072]{1,0:T(8,128)(2,1)S(1)} %select_convert_fusion, f32[1024]{0:T(1024)S(1)} %power_multiply_fusion, bf16[3072,1024]{1,0:T(8,128)(2,1)} %gather_fusion, pred[3072]{0:T(1024)(128)(4,1)S(1)} %compare_and_fusion), kind=kOutput, calls=%fused_computation.34 | convolution fusion | flops 1617166336 | bytes 8920064 | tf_op jit(solution)/shard_map/dot_general | solution.py:78
  27.8 3.6 %collective-permute-start.3 = (bf16[272,256]{1,0:T(8,128)(2,1)S(1)}, bf16[272,256]{1,0:T(8,128)(2,1)S(1)}, u32[]{:S(2)}, u32[]{:S(2)}) collective-permute-start(bf16[272,256]{1,0:T(8,128)(2,1)S(1)} %pad_maximum_fusion.2), channel_id=1, source_target_pairs={{0,6},{2,4},{4,2},{6,0},{8,14},{10,12},{12,10},{14,8},{16,22},{18,... | collective-permute-start | bytes 417800 | tf_op jit(solution)/shard_map/ppermute | solution.py:25
  31.4 0.6 collective-permute-start.2
  32.1 3.7 %collective-permute-done.3 = bf16[272,256]{1,0:T(8,128)(2,1)S(1)} collective-permute-done((bf16[272,256]{1,0:T(8,128)(2,1)S(1)}, bf16[272,256]{1,0:T(8,128)(2,1)S(1)}, u32[]{:S(2)}, u32[]{:S(2)}) %collective-permute-start.3) | collective-permute-done | bytes 139296 | tf_op jit(solution)/shard_map/ppermute | solution.py:25
  35.8 2.8 %collective-permute-done.2 = bf16[272,256]{1,0:T(8,128)(2,1)S(1)} collective-permute-done((bf16[272,256]{1,0:T(8,128)(2,1)S(1)}, bf16[272,256]{1,0:T(8,128)(2,1)S(1)}, u32[]{:S(2)}, u32[]{:S(2)}) %collective-permute-start.2) | collective-permute-done | bytes 139296 | tf_op jit(solution)/shard_map/ppermute | solution.py:25
  38.6 0.3 collective-permute-done.1
  39.2 1.6 %collective-permute-start.4 = (f32[264,64]{1,0:T(8,128)S(1)}, f32[264,64]{1,0:T(8,128)S(1)}, u32[]{:S(2)}, u32[]{:S(2)}) collective-permute-start(f32[264,64]{1,0:T(8,128)S(1)} %get-tuple-element.84), channel_id=1, source_target_pairs={{0,8},{2,10},{4,12},{6,14},{8,0},{10,2},{12,4},{14,6},{16,24},{18,... | collective-permute-start | bytes 202760 | tf_op jit(solution)/shard_map/ppermute | solution.py:25
  40.8 2.6 %collective-permute-start.5 = (f32[264,64]{1,0:T(8,128)S(1)}, f32[264,64]{1,0:T(8,128)S(1)}, u32[]{:S(2)}, u32[]{:S(2)}) collective-permute-start(f32[264,64]{1,0:T(8,128)S(1)} %get-tuple-element.86), channel_id=1, source_target_pairs={{0,16},{2,18},{4,20},{6,22},{8,24},{10,26},{12,28},{14,30},{16,0},... | collective-permute-start | bytes 202760 | tf_op jit(solution)/shard_map/ppermute | solution.py:25
  43.7 2.8 %collective-permute-done.4 = f32[264,64]{1,0:T(8,128)S(1)} collective-permute-done((f32[264,64]{1,0:T(8,128)S(1)}, f32[264,64]{1,0:T(8,128)S(1)}, u32[]{:S(2)}, u32[]{:S(2)}) %collective-permute-start.4) | collective-permute-done | bytes 67616 | tf_op jit(solution)/shard_map/ppermute | solution.py:25
  46.4 7.6 %collective-permute-done.5 = f32[264,64]{1,0:T(8,128)S(1)} collective-permute-done((f32[264,64]{1,0:T(8,128)S(1)}, f32[264,64]{1,0:T(8,128)S(1)}, u32[]{:S(2)}, u32[]{:S(2)}) %collective-permute-start.5) | collective-permute-done | bytes 67616 | tf_op jit(solution)/shard_map/ppermute | solution.py:25
  54.2 2.3 %collective-permute-start.7 = (bf16[272,64]{1,0:T(8,128)(2,1)S(1)}, bf16[272,64]{1,0:T(8,128)(2,1)S(1)}, u32[]{:S(2)}, u32[]{:S(2)}) collective-permute-start(bf16[272,64]{1,0:T(8,128)(2,1)S(1)} %pad_maximum_fusion.6), channel_id=1, source_target_pairs={{0,8},{2,10},{4,12},{6,14},{8,0},{10,2},{12,4},{14,6},{16,24},{18,... | collective-permute-start | bytes 104456 | tf_op jit(solution)/shard_map/ppermute | solution.py:35
  56.5 1.1 collective-permute-start.8
  57.6 1.4 collective-permute-start.9
  59.0 0.3 dynamic_update_slice.48
  59.5 0.6 dynamic_update_slice.49
  60.1 3.7 %collective-permute-done.8 = bf16[272,64]{1,0:T(8,128)(2,1)S(1)} collective-permute-done((bf16[272,64]{1,0:T(8,128)(2,1)S(1)}, bf16[272,64]{1,0:T(8,128)(2,1)S(1)}, u32[]{:S(2)}, u32[]{:S(2)}) %collective-permute-start.8) | collective-permute-done | bytes 34848 | tf_op jit(solution)/shard_map/ppermute | solution.py:35
  63.8 0.3 dynamic_update_slice.50
  64.1 0.6 dynamic_update_slice.51
  64.7 1.5 %collective-permute-start.10 = (bf16[272,256]{1,0:T(8,128)(2,1)S(1)}, bf16[272,256]{1,0:T(8,128)(2,1)S(1)}, u32[]{:S(2)}, u32[]{:S(2)}) collective-permute-start(bf16[272,256]{1,0:T(8,128)(2,1)S(1)} %dynamic_update_slice.51), channel_id=1, source_target_pairs={{0,2},{2,0},{4,6},{6,4},{8,10},{10,8},{12,14},{14,12},{16,18},{18,... | collective-permute-start | bytes 417800 | tf_op jit(solution)/shard_map/ppermute | solution.py:35
  66.4 1.8 %collective-permute-start.12 = (bf16[272,256]{1,0:T(8,128)(2,1)S(1)}, bf16[272,256]{1,0:T(8,128)(2,1)S(1)}, u32[]{:S(2)}, u32[]{:S(2)}) collective-permute-start(bf16[272,256]{1,0:T(8,128)(2,1)S(1)} %dynamic_update_slice.51), channel_id=1, source_target_pairs={{0,6},{2,4},{4,2},{6,0},{8,14},{10,12},{12,10},{14,8},{16,22},{18,... | collective-permute-start | bytes 417800 | tf_op jit(solution)/shard_map/ppermute | solution.py:35
  68.3 2.4 %collective-permute-done.10 = bf16[272,256]{1,0:T(8,128)(2,1)S(1)} collective-permute-done((bf16[272,256]{1,0:T(8,128)(2,1)S(1)}, bf16[272,256]{1,0:T(8,128)(2,1)S(1)}, u32[]{:S(2)}, u32[]{:S(2)}) %collective-permute-start.10) | collective-permute-done | bytes 139296 | tf_op jit(solution)/shard_map/ppermute | solution.py:35
  70.7 2.1 %collective-permute-done.11 = bf16[272,256]{1,0:T(8,128)(2,1)S(1)} collective-permute-done((bf16[272,256]{1,0:T(8,128)(2,1)S(1)}, bf16[272,256]{1,0:T(8,128)(2,1)S(1)}, u32[]{:S(2)}, u32[]{:S(2)}) %collective-permute-start.11) | collective-permute-done | bytes 139296 | tf_op jit(solution)/shard_map/ppermute | solution.py:35
  72.8 4.7 %convolution_convert_fusion.1 = bf16[256,3072]{1,0:T(8,128)(2,1)S(1)} fusion(bf16[272,1024]{1,0:T(8,128)(2,1)S(1)} %constant_dynamic-update-slice_fusion.4, bf16[3072,1024]{1,0:T(8,128)(2,1)} %gather_fusion, pred[3072]{0:T(1024)(128)(4,1)S(1)} %compare_and_fusion), kind=kOutput, calls=%fused_computation.3 | convolution fusion | flops 1614544896 | bytes 8391680 | tf_op jit(solution)/shard_map/dot_general | solution.py:91
  77.9 0.6 collective-permute-start.13
  78.5 1.5 %collective-permute-done.13 = f32[128]{0:T(128)S(1)} collective-permute-done((f32[128]{0:T(128)S(1)}, f32[128]{0:T(128)S(1)}, u32[]{:S(2)}, u32[]{:S(2)}) %collective-permute-start.13) | collective-permute-done | bytes 544 | tf_op jit(solution)/shard_map/ppermute | solution.py:95
  80.0 0.9 fusion.1
  81.0 1.0 convert_element_type.204
  82.1 0.3 scatter.19
  82.4 2.2 %collective-permute-done.15 = bf16[128,3072]{1,0:T(8,128)(2,1)} collective-permute-done((bf16[128,3072]{1,0:T(8,128)(2,1)}, bf16[128,3072]{1,0:T(8,128)(2,1)}, u32[]{:S(2)}, u32[]{:S(2)}) %collective-permute-start.15) | collective-permute-done | bytes 786464 | tf_op jit(solution)/shard_map/ppermute | solution.py:75
  84.6 5.2 %fusion.13 = f32[256,1024]{1,0:T(8,128)S(1)} fusion(bf16[128,3072]{1,0:T(8,128)(2,1)} %collective-permute-done.15, bf16[128,3072]{1,0:T(8,128)(2,1)} %convert_element_type.204, f32[1024]{0:T(1024)S(1)} %power_multiply_fusion, bf16[3072,1024]{1,0:T(8,128)(2,1)} %gather_fusion, pred[3072]{0:T(1024)(128)(4,1)S(1)} %compare_and_fusion), kind=kOutput, calls=%fused_computation.33 | convolution fusion | flops 1617166336 | bytes 8920064 | tf_op jit(solution)/shard_map/dot_general | solution.py:78
  89.9 1.6 %collective-permute-start.18 = (bf16[272,256]{1,0:T(8,128)(2,1)S(1)}, bf16[272,256]{1,0:T(8,128)(2,1)S(1)}, u32[]{:S(2)}, u32[]{:S(2)}) collective-permute-start(bf16[272,256]{1,0:T(8,128)(2,1)S(1)} %pad_maximum_fusion.5), channel_id=1, source_target_pairs={{0,6},{2,4},{4,2},{6,0},{8,14},{10,12},{12,10},{14,8},{16,22},{18,... | collective-permute-start | bytes 417800 | tf_op jit(solution)/shard_map/ppermute | solution.py:25
  91.6 1.5 %collective-permute-start.17 = (bf16[272,256]{1,0:T(8,128)(2,1)S(1)}, bf16[272,256]{1,0:T(8,128)(2,1)S(1)}, u32[]{:S(2)}, u32[]{:S(2)}) collective-permute-start(bf16[272,256]{1,0:T(8,128)(2,1)S(1)} %pad_maximum_fusion.4), channel_id=1, source_target_pairs={{0,4},{2,6},{4,0},{6,2},{8,12},{10,14},{12,8},{14,10},{16,20},{18,... | collective-permute-start | bytes 417800 | tf_op jit(solution)/shard_map/ppermute | solution.py:25
  93.1 0.6 collective-permute-start.16
  93.7 3.8 %collective-permute-done.18 = bf16[272,256]{1,0:T(8,128)(2,1)S(1)} collective-permute-done((bf16[272,256]{1,0:T(8,128)(2,1)S(1)}, bf16[272,256]{1,0:T(8,128)(2,1)S(1)}, u32[]{:S(2)}, u32[]{:S(2)}) %collective-permute-start.18) | collective-permute-done | bytes 139296 | tf_op jit(solution)/shard_map/ppermute | solution.py:25
  97.5 2.1 %collective-permute-done.17 = bf16[272,256]{1,0:T(8,128)(2,1)S(1)} collective-permute-done((bf16[272,256]{1,0:T(8,128)(2,1)S(1)}, bf16[272,256]{1,0:T(8,128)(2,1)S(1)}, u32[]{:S(2)}, u32[]{:S(2)}) %collective-permute-start.17) | collective-permute-done | bytes 139296 | tf_op jit(solution)/shard_map/ppermute | solution.py:25
  100.0 0.9 collective-permute-start.19
  100.9 2.3 %collective-permute-start.20 = (f32[264,64]{1,0:T(8,128)S(1)}, f32[264,64]{1,0:T(8,128)S(1)}, u32[]{:S(2)}, u32[]{:S(2)}) collective-permute-start(f32[264,64]{1,0:T(8,128)S(1)} %get-tuple-element.83), channel_id=1, source_target_pairs={{0,16},{2,18},{4,20},{6,22},{8,24},{10,26},{12,28},{14,30},{16,0},... | collective-permute-start | bytes 202760 | tf_op jit(solution)/shard_map/ppermute | solution.py:25
  103.1 1.3 collective-permute-start.21
  104.4 3.9 %collective-permute-done.19 = f32[264,64]{1,0:T(8,128)S(1)} collective-permute-done((f32[264,64]{1,0:T(8,128)S(1)}, f32[264,64]{1,0:T(8,128)S(1)}, u32[]{:S(2)}, u32[]{:S(2)}) %collective-permute-start.19) | collective-permute-done | bytes 67616 | tf_op jit(solution)/shard_map/ppermute | solution.py:25
  108.4 0.3 collective-permute-done.20
  108.7 4.9 %collective-permute-done.21 = f32[264,64]{1,0:T(8,128)S(1)} collective-permute-done((f32[264,64]{1,0:T(8,128)S(1)}, f32[264,64]{1,0:T(8,128)S(1)}, u32[]{:S(2)}, u32[]{:S(2)}) %collective-permute-start.21) | collective-permute-done | bytes 67616 | tf_op jit(solution)/shard_map/ppermute | solution.py:25
  113.8 2.7 %collective-permute-start.22 = (bf16[272,64]{1,0:T(8,128)(2,1)S(1)}, bf16[272,64]{1,0:T(8,128)(2,1)}, u32[]{:S(2)}, u32[]{:S(2)}) collective-permute-start(bf16[272,64]{1,0:T(8,128)(2,1)S(1)} %pad_maximum_fusion.7), channel_id=1, source_target_pairs={{0,8},{2,10},{4,12},{6,14},{8,0},{10,2},{12,4},{14,6},{16,24},{18,... | collective-permute-start | bytes 104456 | tf_op jit(solution)/shard_map/ppermute | solution.py:35
  116.5 1.9 %collective-permute-start.23 = (bf16[272,64]{1,0:T(8,128)(2,1)S(1)}, bf16[272,64]{1,0:T(8,128)(2,1)S(1)}, u32[]{:S(2)}, u32[]{:S(2)}) collective-permute-start(bf16[272,64]{1,0:T(8,128)(2,1)S(1)} %pad_maximum_fusion.7), channel_id=1, source_target_pairs={{0,16},{2,18},{4,20},{6,22},{8,24},{10,26},{12,28},{14,30},{16,0},... | collective-permute-start | bytes 104456 | tf_op jit(solution)/shard_map/ppermute | solution.py:35
  118.4 1.4 collective-permute-start.24
  119.8 0.3 dynamic_update_slice.56
  120.1 1.4 dynamic_update_slice.57
  121.6 3.5 %collective-permute-done.23 = bf16[272,64]{1,0:T(8,128)(2,1)S(1)} collective-permute-done((bf16[272,64]{1,0:T(8,128)(2,1)S(1)}, bf16[272,64]{1,0:T(8,128)(2,1)S(1)}, u32[]{:S(2)}, u32[]{:S(2)}) %collective-permute-start.23) | collective-permute-done | bytes 34848 | tf_op jit(solution)/shard_map/ppermute | solution.py:35
  125.0 0.3 dynamic_update_slice.58
  125.3 0.6 dynamic_update_slice.59
  125.9 1.4 collective-permute-start.25
  127.3 0.7 collective-permute-start.26
  128.0 1.4 collective-permute-start.27
  129.5 2.3 %collective-permute-done.25 = bf16[272,256]{1,0:T(8,128)(2,1)S(1)} collective-permute-done((bf16[272,256]{1,0:T(8,128)(2,1)S(1)}, bf16[272,256]{1,0:T(8,128)(2,1)S(1)}, u32[]{:S(2)}, u32[]{:S(2)}) %collective-permute-start.25) | collective-permute-done | bytes 139296 | tf_op jit(solution)/shard_map/ppermute | solution.py:35
  131.8 0.7 collective-permute-done.26
  132.5 1.5 %collective-permute-done.27 = bf16[272,256]{1,0:T(8,128)(2,1)S(1)} collective-permute-done((bf16[272,256]{1,0:T(8,128)(2,1)S(1)}, bf16[272,256]{1,0:T(8,128)(2,1)S(1)}, u32[]{:S(2)}, u32[]{:S(2)}) %collective-permute-start.27) | collective-permute-done | bytes 139296 | tf_op jit(solution)/shard_map/ppermute | solution.py:35
  134.0 4.8 %convolution_convert_fusion = bf16[256,3072]{1,0:T(8,128)(2,1)S(1)} fusion(bf16[272,1024]{1,0:T(8,128)(2,1)S(1)} %constant_dynamic-update-slice_fusion, bf16[3072,1024]{1,0:T(8,128)(2,1)} %gather_fusion, pred[3072]{0:T(1024)(128)(4,1)} %copy-done.8), kind=kOutput, calls=%fused_computation.2 | convolution fusion | flops 1614544896 | bytes 8391680 | tf_op jit(solution)/shard_map/dot_general | solution.py:91
  139.3 0.6 collective-permute-start.28
  139.8 1.5 %collective-permute-done.28 = f32[128]{0:T(128)S(1)} collective-permute-done((f32[128]{0:T(128)S(1)}, f32[128]{0:T(128)S(1)}, u32[]{:S(2)}, u32[]{:S(2)}) %collective-permute-start.28) | collective-permute-done | bytes 544 | tf_op jit(solution)/shard_map/ppermute | solution.py:95
  141.4 2.9 %fusion.4 = (f32[128,3072]{1,0:T(8,128)}, f32[128,3072]{1,0:T(8,128)}) fusion(f32[128,3072]{1,0:T(8,128)S(1)} %get-tuple-element.64, bf16[128,3072]{1,0:T(8,128)(2,1)S(1)} %collective-permute-done.29, bf16[128,3072]{1,0:T(8,128)(2,1)S(1)} %copy-done.4, f32[128,3072]{1,0:T(8,128)S(1)} %copy-done, bf16[256,3072]{1,0:T(8,128)(2,1)S(1)} %convolution_convert_fusion, ...), kind=kLoop, calls=%fused_computation.20 | loop fusion | flops 8650752 | bytes 9454080 | tf_op jit(solution)/shard_map/sub | solution.py:116
  (110 shorter events, 3.3 us)
Async XLA Ops:
  0.6 2.8 %copy-start.6 = (s32[3072]{0:T(1024)S(1)}, s32[3072]{0:T(1024)}, u32[]{:S(2)}) copy-start(s32[3072]{0:T(1024)} %param.15) | copy-start | bytes 36868
  2.9 20.0 %collective-permute-start = (bf16[128,3072]{1,0:T(8,128)(2,1)S(1)}, bf16[128,3072]{1,0:T(8,128)(2,1)S(1)}, u32[]{:S(2)}, u32[]{:S(2)}) collective-permute-start(bf16[128,3072]{1,0:T(8,128)(2,1)S(1)} %select_convert_fusion), channel_id=1, source_target_pairs={{0,1},{1,0},{2,3},{3,2},{4,5},{5,4},{6,7},{7,6},{8,9},{9,8},{10,11... | collective-permute-start | bytes 2359304 | tf_op jit(solution)/shard_map/ppermute | solution.py:75
  3.4 18.7 %copy-start = (f32[128,3072]{1,0:T(8,128)S(1)}, f32[128,3072]{1,0:T(8,128)}, u32[]{:S(2)}) copy-start(f32[128,3072]{1,0:T(8,128)} %param.19) | copy-start | bytes 4718596
  3.4 18.7 %copy-start.5 = (f32[3072]{0:T(1024)S(1)}, f32[3072]{0:T(1024)}, u32[]{:S(2)}) copy-start(f32[3072]{0:T(1024)} %param.17) | copy-start | bytes 36868
  22.1 0.7 copy-start.7
  22.9 61.7 %copy-start.8 = (pred[3072]{0:T(1024)(128)(4,1)}, pred[3072]{0:T(1024)(128)(4,1)S(1)}, u32[]{:S(2)}) copy-start(pred[3072]{0:T(1024)(128)(4,1)S(1)} %compare_and_fusion) | copy-start | bytes 9220
  27.8 8.0 %collective-permute-start.3 = (bf16[272,256]{1,0:T(8,128)(2,1)S(1)}, bf16[272,256]{1,0:T(8,128)(2,1)S(1)}, u32[]{:S(2)}, u32[]{:S(2)}) collective-permute-start(bf16[272,256]{1,0:T(8,128)(2,1)S(1)} %pad_maximum_fusion.2), channel_id=1, source_target_pairs={{0,6},{2,4},{4,2},{6,0},{8,14},{10,12},{12,10},{14,8},{16,22},{18,... | collective-permute-start | bytes 417800 | tf_op jit(solution)/shard_map/ppermute | solution.py:25
  31.4 7.2 %collective-permute-start.2 = (bf16[272,256]{1,0:T(8,128)(2,1)S(1)}, bf16[272,256]{1,0:T(8,128)(2,1)S(1)}, u32[]{:S(2)}, u32[]{:S(2)}) collective-permute-start(bf16[272,256]{1,0:T(8,128)(2,1)S(1)} %pad_maximum_fusion.1), channel_id=1, source_target_pairs={{0,4},{2,6},{4,0},{6,2},{8,12},{10,14},{12,8},{14,10},{16,20},{18,... | collective-permute-start | bytes 417800 | tf_op jit(solution)/shard_map/ppermute | solution.py:25
  31.9 6.9 %collective-permute-start.1 = (bf16[272,256]{1,0:T(8,128)(2,1)S(1)}, bf16[272,256]{1,0:T(8,128)(2,1)S(1)}, u32[]{:S(2)}, u32[]{:S(2)}) collective-permute-start(bf16[272,256]{1,0:T(8,128)(2,1)S(1)} %pad_maximum_fusion), channel_id=1, source_target_pairs={{0,2},{2,0},{4,6},{6,4},{8,10},{10,8},{12,14},{14,12},{16,18},{18,... | collective-permute-start | bytes 417800 | tf_op jit(solution)/shard_map/ppermute | solution.py:25
  39.2 7.2 %collective-permute-start.4 = (f32[264,64]{1,0:T(8,128)S(1)}, f32[264,64]{1,0:T(8,128)S(1)}, u32[]{:S(2)}, u32[]{:S(2)}) collective-permute-start(f32[264,64]{1,0:T(8,128)S(1)} %get-tuple-element.84), channel_id=1, source_target_pairs={{0,8},{2,10},{4,12},{6,14},{8,0},{10,2},{12,4},{14,6},{16,24},{18,... | collective-permute-start | bytes 202760 | tf_op jit(solution)/shard_map/ppermute | solution.py:25
  40.8 13.1 %collective-permute-start.5 = (f32[264,64]{1,0:T(8,128)S(1)}, f32[264,64]{1,0:T(8,128)S(1)}, u32[]{:S(2)}, u32[]{:S(2)}) collective-permute-start(f32[264,64]{1,0:T(8,128)S(1)} %get-tuple-element.86), channel_id=1, source_target_pairs={{0,16},{2,18},{4,20},{6,22},{8,24},{10,26},{12,28},{14,30},{16,0},... | collective-permute-start | bytes 202760 | tf_op jit(solution)/shard_map/ppermute | solution.py:25
  43.4 10.6 %collective-permute-start.6 = (f32[264,64]{1,0:T(8,128)S(1)}, f32[264,64]{1,0:T(8,128)S(1)}, u32[]{:S(2)}, u32[]{:S(2)}) collective-permute-start(f32[264,64]{1,0:T(8,128)S(1)} %get-tuple-element.85), channel_id=1, source_target_pairs={{0,24},{2,26},{4,28},{6,30},{8,16},{10,18},{12,20},{14,22},{16,8},... | collective-permute-start | bytes 202760 | tf_op jit(solution)/shard_map/ppermute | solution.py:25
  54.2 5.3 %collective-permute-start.7 = (bf16[272,64]{1,0:T(8,128)(2,1)S(1)}, bf16[272,64]{1,0:T(8,128)(2,1)S(1)}, u32[]{:S(2)}, u32[]{:S(2)}) collective-permute-start(bf16[272,64]{1,0:T(8,128)(2,1)S(1)} %pad_maximum_fusion.6), channel_id=1, source_target_pairs={{0,8},{2,10},{4,12},{6,14},{8,0},{10,2},{12,4},{14,6},{16,24},{18,... | collective-permute-start | bytes 104456 | tf_op jit(solution)/shard_map/ppermute | solution.py:35
  56.5 7.3 %collective-permute-start.8 = (bf16[272,64]{1,0:T(8,128)(2,1)S(1)}, bf16[272,64]{1,0:T(8,128)(2,1)S(1)}, u32[]{:S(2)}, u32[]{:S(2)}) collective-permute-start(bf16[272,64]{1,0:T(8,128)(2,1)S(1)} %pad_maximum_fusion.6), channel_id=1, source_target_pairs={{0,16},{2,18},{4,20},{6,22},{8,24},{10,26},{12,28},{14,30},{16,0},... | collective-permute-start | bytes 104456 | tf_op jit(solution)/shard_map/ppermute | solution.py:35
  57.6 6.5 %collective-permute-start.9 = (bf16[272,64]{1,0:T(8,128)(2,1)S(1)}, bf16[272,64]{1,0:T(8,128)(2,1)S(1)}, u32[]{:S(2)}, u32[]{:S(2)}) collective-permute-start(bf16[272,64]{1,0:T(8,128)(2,1)S(1)} %pad_maximum_fusion.6), channel_id=1, source_target_pairs={{0,24},{2,26},{4,28},{6,30},{8,16},{10,18},{12,20},{14,22},{16,8},... | collective-permute-start | bytes 104456 | tf_op jit(solution)/shard_map/ppermute | solution.py:35
  64.7 6.0 %collective-permute-start.10 = (bf16[272,256]{1,0:T(8,128)(2,1)S(1)}, bf16[272,256]{1,0:T(8,128)(2,1)S(1)}, u32[]{:S(2)}, u32[]{:S(2)}) collective-permute-start(bf16[272,256]{1,0:T(8,128)(2,1)S(1)} %dynamic_update_slice.51), channel_id=1, source_target_pairs={{0,2},{2,0},{4,6},{6,4},{8,10},{10,8},{12,14},{14,12},{16,18},{18,... | collective-permute-start | bytes 417800 | tf_op jit(solution)/shard_map/ppermute | solution.py:35
  66.2 6.5 %collective-permute-start.11 = (bf16[272,256]{1,0:T(8,128)(2,1)S(1)}, bf16[272,256]{1,0:T(8,128)(2,1)S(1)}, u32[]{:S(2)}, u32[]{:S(2)}) collective-permute-start(bf16[272,256]{1,0:T(8,128)(2,1)S(1)} %dynamic_update_slice.51), channel_id=1, source_target_pairs={{0,4},{2,6},{4,0},{6,2},{8,12},{10,14},{12,8},{14,10},{16,20},{18,... | collective-permute-start | bytes 417800 | tf_op jit(solution)/shard_map/ppermute | solution.py:35
  66.4 6.4 %collective-permute-start.12 = (bf16[272,256]{1,0:T(8,128)(2,1)S(1)}, bf16[272,256]{1,0:T(8,128)(2,1)S(1)}, u32[]{:S(2)}, u32[]{:S(2)}) collective-permute-start(bf16[272,256]{1,0:T(8,128)(2,1)S(1)} %dynamic_update_slice.51), channel_id=1, source_target_pairs={{0,6},{2,4},{4,2},{6,0},{8,14},{10,12},{12,10},{14,8},{16,22},{18,... | collective-permute-start | bytes 417800 | tf_op jit(solution)/shard_map/ppermute | solution.py:35
  77.6 3.4 %copy-start.1 = (bf16[256,3072]{1,0:T(8,128)(2,1)}, bf16[256,3072]{1,0:T(8,128)(2,1)S(1)}, u32[]{:S(2)}) copy-start(bf16[256,3072]{1,0:T(8,128)(2,1)S(1)} %convolution_convert_fusion.1) | copy-start | bytes 4718596
  77.6 2.4 %collective-permute-start.14 = (bf16[128,3072]{1,0:T(8,128)(2,1)S(1)}, bf16[128,3072]{1,0:T(8,128)(2,1)S(1)}, u32[]{:S(2)}, u32[]{:S(2)}) collective-permute-start(bf16[128,3072]{1,0:T(8,128)(2,1)S(1)} %slice.309), channel_id=1, source_target_pairs={{0,1},{1,0},{2,3},{3,2},{4,5},{5,4},{6,7},{7,6},{8,9},{9,8},{10,11... | collective-permute-start | bytes 2359304 | tf_op jit(solution)/shard_map/ppermute | solution.py:96
  77.9 2.0 %collective-permute-start.13 = (f32[128]{0:T(128)S(1)}, f32[128]{0:T(128)S(1)}, u32[]{:S(2)}, u32[]{:S(2)}) collective-permute-start(f32[128]{0:T(128)S(1)} %slice.255), channel_id=1, source_target_pairs={{0,1},{1,0},{2,3},{3,2},{4,5},{5,4},{6,7},{7,6},{8,9},{9,8},{10,11... | collective-permute-start | bytes 1544 | tf_op jit(solution)/shard_map/ppermute | solution.py:95
  80.0 1.0 copy-start.9
  80.0 1.0 copy-start.3
  82.0 2.6 %collective-permute-start.15 = (bf16[128,3072]{1,0:T(8,128)(2,1)}, bf16[128,3072]{1,0:T(8,128)(2,1)}, u32[]{:S(2)}, u32[]{:S(2)}) collective-permute-start(bf16[128,3072]{1,0:T(8,128)(2,1)} %convert_element_type.204), channel_id=1, source_target_pairs={{0,1},{1,0},{2,3},{3,2},{4,5},{5,4},{6,7},{7,6},{8,9},{9,8},{10,11... | collective-permute-start | bytes 2359304 | tf_op jit(solution)/shard_map/ppermute | solution.py:75
  89.9 7.5 %collective-permute-start.18 = (bf16[272,256]{1,0:T(8,128)(2,1)S(1)}, bf16[272,256]{1,0:T(8,128)(2,1)S(1)}, u32[]{:S(2)}, u32[]{:S(2)}) collective-permute-start(bf16[272,256]{1,0:T(8,128)(2,1)S(1)} %pad_maximum_fusion.5), channel_id=1, source_target_pairs={{0,6},{2,4},{4,2},{6,0},{8,14},{10,12},{12,10},{14,8},{16,22},{18,... | collective-permute-start | bytes 417800 | tf_op jit(solution)/shard_map/ppermute | solution.py:25
  91.6 8.0 %collective-permute-start.17 = (bf16[272,256]{1,0:T(8,128)(2,1)S(1)}, bf16[272,256]{1,0:T(8,128)(2,1)S(1)}, u32[]{:S(2)}, u32[]{:S(2)}) collective-permute-start(bf16[272,256]{1,0:T(8,128)(2,1)S(1)} %pad_maximum_fusion.4), channel_id=1, source_target_pairs={{0,4},{2,6},{4,0},{6,2},{8,12},{10,14},{12,8},{14,10},{16,20},{18,... | collective-permute-start | bytes 417800 | tf_op jit(solution)/shard_map/ppermute | solution.py:25
  93.1 6.6 %collective-permute-start.16 = (bf16[272,256]{1,0:T(8,128)(2,1)S(1)}, bf16[272,256]{1,0:T(8,128)(2,1)S(1)}, u32[]{:S(2)}, u32[]{:S(2)}) collective-permute-start(bf16[272,256]{1,0:T(8,128)(2,1)S(1)} %pad_maximum_fusion.3), channel_id=1, source_target_pairs={{0,2},{2,0},{4,6},{6,4},{8,10},{10,8},{12,14},{14,12},{16,18},{18,... | collective-permute-start | bytes 417800 | tf_op jit(solution)/shard_map/ppermute | solution.py:25
  100.0 8.4 %collective-permute-start.19 = (f32[264,64]{1,0:T(8,128)S(1)}, f32[264,64]{1,0:T(8,128)S(1)}, u32[]{:S(2)}, u32[]{:S(2)}) collective-permute-start(f32[264,64]{1,0:T(8,128)S(1)} %get-tuple-element.81), channel_id=1, source_target_pairs={{0,8},{2,10},{4,12},{6,14},{8,0},{10,2},{12,4},{14,6},{16,24},{18,... | collective-permute-start | bytes 202760 | tf_op jit(solution)/shard_map/ppermute | solution.py:25
  100.9 7.9 %collective-permute-start.20 = (f32[264,64]{1,0:T(8,128)S(1)}, f32[264,64]{1,0:T(8,128)S(1)}, u32[]{:S(2)}, u32[]{:S(2)}) collective-permute-start(f32[264,64]{1,0:T(8,128)S(1)} %get-tuple-element.83), channel_id=1, source_target_pairs={{0,16},{2,18},{4,20},{6,22},{8,24},{10,26},{12,28},{14,30},{16,0},... | collective-permute-start | bytes 202760 | tf_op jit(solution)/shard_map/ppermute | solution.py:25
  103.1 10.5 %collective-permute-start.21 = (f32[264,64]{1,0:T(8,128)S(1)}, f32[264,64]{1,0:T(8,128)S(1)}, u32[]{:S(2)}, u32[]{:S(2)}) collective-permute-start(f32[264,64]{1,0:T(8,128)S(1)} %get-tuple-element.82), channel_id=1, source_target_pairs={{0,24},{2,26},{4,28},{6,30},{8,16},{10,18},{12,20},{14,22},{16,8},... | collective-permute-start | bytes 202760 | tf_op jit(solution)/shard_map/ppermute | solution.py:25
  113.8 6.3 %collective-permute-start.22 = (bf16[272,64]{1,0:T(8,128)(2,1)S(1)}, bf16[272,64]{1,0:T(8,128)(2,1)}, u32[]{:S(2)}, u32[]{:S(2)}) collective-permute-start(bf16[272,64]{1,0:T(8,128)(2,1)S(1)} %pad_maximum_fusion.7), channel_id=1, source_target_pairs={{0,8},{2,10},{4,12},{6,14},{8,0},{10,2},{12,4},{14,6},{16,24},{18,... | collective-permute-start | bytes 104456 | tf_op jit(solution)/shard_map/ppermute | solution.py:35
  116.5 8.5 %collective-permute-start.23 = (bf16[272,64]{1,0:T(8,128)(2,1)S(1)}, bf16[272,64]{1,0:T(8,128)(2,1)S(1)}, u32[]{:S(2)}, u32[]{:S(2)}) collective-permute-start(bf16[272,64]{1,0:T(8,128)(2,1)S(1)} %pad_maximum_fusion.7), channel_id=1, source_target_pairs={{0,16},{2,18},{4,20},{6,22},{8,24},{10,26},{12,28},{14,30},{16,0},... | collective-permute-start | bytes 104456 | tf_op jit(solution)/shard_map/ppermute | solution.py:35
  118.4 6.9 %collective-permute-start.24 = (bf16[272,64]{1,0:T(8,128)(2,1)S(1)}, bf16[272,64]{1,0:T(8,128)(2,1)S(1)}, u32[]{:S(2)}, u32[]{:S(2)}) collective-permute-start(bf16[272,64]{1,0:T(8,128)(2,1)S(1)} %pad_maximum_fusion.7), channel_id=1, source_target_pairs={{0,24},{2,26},{4,28},{6,30},{8,16},{10,18},{12,20},{14,22},{16,8},... | collective-permute-start | bytes 104456 | tf_op jit(solution)/shard_map/ppermute | solution.py:35
  125.9 5.9 %collective-permute-start.25 = (bf16[272,256]{1,0:T(8,128)(2,1)S(1)}, bf16[272,256]{1,0:T(8,128)(2,1)S(1)}, u32[]{:S(2)}, u32[]{:S(2)}) collective-permute-start(bf16[272,256]{1,0:T(8,128)(2,1)S(1)} %dynamic_update_slice.59), channel_id=1, source_target_pairs={{0,2},{2,0},{4,6},{6,4},{8,10},{10,8},{12,14},{14,12},{16,18},{18,... | collective-permute-start | bytes 417800 | tf_op jit(solution)/shard_map/ppermute | solution.py:35
  127.3 5.2 %collective-permute-start.26 = (bf16[272,256]{1,0:T(8,128)(2,1)S(1)}, bf16[272,256]{1,0:T(8,128)(2,1)S(1)}, u32[]{:S(2)}, u32[]{:S(2)}) collective-permute-start(bf16[272,256]{1,0:T(8,128)(2,1)S(1)} %dynamic_update_slice.59), channel_id=1, source_target_pairs={{0,4},{2,6},{4,0},{6,2},{8,12},{10,14},{12,8},{14,10},{16,20},{18,... | collective-permute-start | bytes 417800 | tf_op jit(solution)/shard_map/ppermute | solution.py:35
  128.0 6.0 %collective-permute-start.27 = (bf16[272,256]{1,0:T(8,128)(2,1)S(1)}, bf16[272,256]{1,0:T(8,128)(2,1)S(1)}, u32[]{:S(2)}, u32[]{:S(2)}) collective-permute-start(bf16[272,256]{1,0:T(8,128)(2,1)S(1)} %dynamic_update_slice.59), channel_id=1, source_target_pairs={{0,6},{2,4},{4,2},{6,0},{8,14},{10,12},{12,10},{14,8},{16,22},{18,... | collective-permute-start | bytes 417800 | tf_op jit(solution)/shard_map/ppermute | solution.py:35
  134.0 7.3 %copy-start.4 = (bf16[128,3072]{1,0:T(8,128)(2,1)S(1)}, bf16[128,3072]{1,0:T(8,128)(2,1)}, u32[]{:S(2)}) copy-start(bf16[128,3072]{1,0:T(8,128)(2,1)} %copy-done.3) | copy-start | bytes 2359300
  138.9 2.4 %copy-start.10 = (f32[128]{0:T(128)S(1)}, f32[128]{0:T(128)}, u32[]{:S(2)}) copy-start(f32[128]{0:T(128)} %copy-done.9) | copy-start | bytes 1540
  138.9 2.5 %copy-start.2 = (bf16[256,3072]{1,0:T(8,128)(2,1)S(1)}, bf16[256,3072]{1,0:T(8,128)(2,1)}, u32[]{:S(2)}) copy-start(bf16[256,3072]{1,0:T(8,128)(2,1)} %copy-done.1) | copy-start | bytes 4718596
  139.0 2.4 %collective-permute-start.29 = (bf16[128,3072]{1,0:T(8,128)(2,1)S(1)}, bf16[128,3072]{1,0:T(8,128)(2,1)S(1)}, u32[]{:S(2)}, u32[]{:S(2)}) collective-permute-start(bf16[128,3072]{1,0:T(8,128)(2,1)S(1)} %slice.333), channel_id=1, source_target_pairs={{0,1},{1,0},{2,3},{3,2},{4,5},{5,4},{6,7},{7,6},{8,9},{9,8},{10,11... | collective-permute-start | bytes 2359304 | tf_op jit(solution)/shard_map/ppermute | solution.py:96
  139.3 2.0 %collective-permute-start.28 = (f32[128]{0:T(128)S(1)}, f32[128]{0:T(128)S(1)}, u32[]{:S(2)}, u32[]{:S(2)}) collective-permute-start(f32[128]{0:T(128)S(1)} %slice.281), channel_id=1, source_target_pairs={{0,1},{1,0},{2,3},{3,2},{4,5},{5,4},{6,7},{7,6},{8,9},{9,8},{10,11... | collective-permute-start | bytes 1544 | tf_op jit(solution)/shard_map/ppermute | solution.py:95

commit v4 on v3

--- a/solution.py
+++ b/solution.py
@@ -4,6 +4,7 @@
 from jax.sharding import PartitionSpec as P
 
 ITERS = 2
+CHUNKS = 2
 
 
 def vert_sum(x, n_vert, finish, encode, decode):
@@ -48,8 +49,13 @@
         samples = own * n_eig
         group = eig_table.shape[1]
         filled = jnp.arange(capacity, dtype=jnp.int32) < counts[0]
-        features = jnp.take(eig_table, obs_ids, axis=0)
-        spectrum = 5.0 * jnp.power(3.0 + eigenvalues, -1.5)
+        width = group // CHUNKS
+        def gather(table, c):
+            return jnp.take(table[:, c * width : (c + 1) * width], obs_ids, axis=0)
+
+        features = [gather(eig_table, c) for c in range(CHUNKS)]
+        spectrum_all = 5.0 * jnp.power(3.0 + eigenvalues, -1.5)
+        spectra = [spectrum_all[c * width : (c + 1) * width] for c in range(CHUNKS)]
         me_eig = lax.axis_index("eig")
 
         def finish(piece):
@@ -75,22 +81,30 @@
                 rows = jnp.concatenate([lowered, lax.ppermute(lowered, "eig", swap)], 0)
             else:
                 rows = lax.all_gather(lowered, "eig", axis=0, tiled=True)
-            coeff = jnp.dot(rows, features, preferred_element_type=jnp.float32)
-            sums = jnp.zeros((8, group), jnp.float32)
+            sums = jnp.zeros((8, width), jnp.float32)
             sums = sums.at[0, :own].set(jnp.sum(vector * vector, axis=1))
             sums = sums.at[1, :own].set(jnp.sum(noise_var[None, :] * vector * vector, axis=1))
-            gathered = vert_sum(
-                jnp.concatenate([coeff * spectrum[None, :], sums], 0), n_vert, finish, finish, decode
-            )
-            weights = gathered[:samples]
-            sums = gathered[samples : samples + 8].astype(jnp.float32) + gathered[
-                samples + 8 : samples + 16
-            ].astype(jnp.float32)
-            wide = weights.astype(jnp.float32)
-            energy = jnp.sum(wide * wide / spectrum[None, :], axis=1)
-            partials = lax.dot_general(
-                weights, features, (((1,), (1,)), ((), ())), preferred_element_type=jnp.float32
-            ).astype(jnp.bfloat16)
+            energy = 0.0
+            accumulated = None
+            for c in range(CHUNKS):
+                coeff = jnp.dot(rows, features[c], preferred_element_type=jnp.float32)
+                block = jnp.concatenate(
+                    [coeff * spectra[c][None, :], sums if c == 0 else jnp.zeros_like(sums)], 0
+                )
+                gathered = vert_sum(block, n_vert, finish, finish, decode)
+                weights = gathered[:samples]
+                if c == 0:
+                    totals = gathered[samples : samples + 8].astype(jnp.float32) + gathered[
+                        samples + 8 : samples + 16
+                    ].astype(jnp.float32)
+                wide = weights.astype(jnp.float32)
+                energy = energy + jnp.sum(wide * wide / spectra[c][None, :], axis=1)
+                term = lax.dot_general(
+                    weights, features[c], (((1,), (1,)), ((), ())), preferred_element_type=jnp.float32
+                )
+                accumulated = term if accumulated is None else accumulated + term
+            sums = totals
+            partials = accumulated.astype(jnp.bfloat16)
             if pair:
                 energy = energy[:own] + lax.ppermute(energy[own:], "eig", swap)
                 image = partials[:own].astype(jnp.float32) + lax.ppermute(

time: 145 us -> 204 us (1.41)
  starting transfers between devices: 36.7 us -> 94.3 us
  waiting for transfers between devices: 53.5 us -> 23.5 us
  local copies, waits for them, and re-layouts: 24.5 us -> 52 us
    ppermute x12 -> x24, starting transfers between devices: 17.9 us -> 56.4 us  [vert_sum(): got = lax.ppermute(cur, 'vert', [(i, i ^ masks[t]) for i in range(n_vert)])]
    ppermute x12 -> x24, waiting for transfers between devices: 32.1 us -> 8.73 us  [vert_sum(): got = lax.ppermute(send, 'vert', [(i, i ^ masks[t]) for i in range(n_vert)])]
    ppermute x12 -> x24, starting transfers between devices: 16.9 us -> 36 us  [vert_sum(): got = lax.ppermute(send, 'vert', [(i, i ^ masks[t]) for i in range(n_vert)])]
    dynamic_update_slice x12 -> x24, local copies, waits for them, and re-layouts: 3.76 us -> 16.9 us  [vert_sum(): out = lax.dynamic_update_slice_in_dim(out, got, (digit ^ t) * width, axis=1)]
    gather x1 -> x2, local copies, waits for them, and re-layouts: 18.7 us -> 28.3 us  [gather(): return jnp.take(table[:, c * width:(c + 1) * width], obs_ids, axis=0)]
    ppermute x12 -> x24, waiting for transfers between devices: 16.2 us -> 9.71 us  [vert_sum(): got = lax.ppermute(cur, 'vert', [(i, i ^ masks[t]) for i in range(n_vert)])]
    slice x0 -> x4, local copies, waits for them, and re-layouts: none -> 3.88 us  [the longest x1 3.84 us: gather(): return jnp.take(table[:, c * width:(c + 1) * width], obs_ids, axis=0)]
    dot_general x4 -> x8, matrix products: 19.4 us -> 20.5 us  [the longest x4 11.7 us: operate(): coeff = jnp.dot(rows, features[c], preferred_element_type=jnp.float32)]
  transfers between devices with their start and end apart: 30 -> 54, of which waited for: 21 -> 11; matrix products, arithmetic and copies ran while one was open for 16% -> 31% of each run, Pallas kernels for 0% -> 0%
where the time goes in v4:
time: 204 us; the launch traced here: 203 us
  starting transfers between devices  94.3 us (46%)
  local copies, waits for them, and re-layouts  52 us (25%)
  waiting for transfers between devices  23.5 us (12%)
  matrix products  20.5 us (10%)
  other arithmetic  10.1 us (5%)
  between operations  2.62 us (1%)
    ppermute x24, starting transfers between devices, vert_sum(): got = lax.ppermute(cur, 'vert', [(i, i ^ masks[t]) for i in range(n_vert)])  56.4 us
    ppermute x24, starting transfers between devices, vert_sum(): got = lax.ppermute(send, 'vert', [(i, i ^ masks[t]) for i in range(n_vert)])  36 us
    gather x2, local copies, waits for them, and re-layouts, gather(): return jnp.take(table[:, c * width:(c + 1) * width], obs_ids, axis=0)  28.3 us
    dynamic_update_slice x24, local copies, waits for them, and re-layouts, vert_sum(): out = lax.dynamic_update_slice_in_dim(out, got, (digit ^ t) * width, axis=1)  16.9 us
    dot_general x4, matrix products, operate(): coeff = jnp.dot(rows, features[c], preferred_element_type=jnp.float32)  11.7 us
    ppermute x24, waiting for transfers between devices, vert_sum(): got = lax.ppermute(cur, 'vert', [(i, i ^ masks[t]) for i in range(n_vert)])  9.71 us
    dot_general x4, matrix products, operate(): lax.dot_general(weights, features[c], (((1,), (1,)), ((), ())), preferred...  8.86 us
    ppermute x24, waiting for transfers between devices, vert_sum(): got = lax.ppermute(send, 'vert', [(i, i ^ masks[t]) for i in range(n_vert)])  8.73 us
  transfers between devices with their start and end apart: 54, of which 11 were waited for; matrix products, arithmetic and copies ran while one was open for 31% of the time, Pallas kernels for 0%

profile of v4, /device:TPU:0, one launch (start us, length us, event | category | flops | bytes accessed | tf_op | source)
XLA Modules:
  0.0 203.1 jit_solution(6673417525919034163)
XLA Ops:
  1.3 1.5 select_convert_fusion
  3.4 3.8 %fusion.55 = (bf16[2048,512]{1,0:T(8,128)(2,1)}, bf16[2048,512]{1,0:T(8,128)(2,1)S(1)}) fusion(bf16[2048,1024]{1,0:T(8,128)(2,1)} %param.16), kind=kLoop, calls=%fused_computation.227 | loop fusion | bytes 8388608 | tf_op jit(solution)/shard_map/slice | solution.py:54
  7.2 15.1 %gather_fusion = bf16[3072,512]{1,0:T(8,128)(2,1)} fusion(bf16[2048,512]{1,0:T(8,128)(2,1)} %get-tuple-element.90, s32[3072]{0:T(1024)S(1)} %fusion.43), kind=kCustom, calls=%fused_computation.clone | custom fusion | bytes 6303744 | tf_op jit(solution)/shard_map/jit(_take)/gather | solution.py:54
  22.4 13.2 %gather_fusion.1 = bf16[3072,512]{1,0:T(8,128)(2,1)} fusion(bf16[2048,512]{1,0:T(8,128)(2,1)S(1)} %get-tuple-element.91, s32[3072]{0:T(1024)S(1)} %fusion.43), kind=kCustom, calls=%fused_computation.1.clone | custom fusion | bytes 6303744 | tf_op jit(solution)/shard_map/jit(_take)/gather | solution.py:54
  35.6 1.8 fusion.2
  37.8 3.6 %convolution_multiply_fusion.3 = f32[256,512]{1,0:T(8,128)S(1)} fusion(bf16[128,3072]{1,0:T(8,128)(2,1)} %collective-permute-done, bf16[128,3072]{1,0:T(8,128)(2,1)} %copy-done.9, f32[512]{0:T(512)S(1)} %get-tuple-element.124, bf16[3072,512]{1,0:T(8,128)(2,1)} %gather_fusion, pred[3072]{0:T(1024)(128)(4,1)S(1)} %compare_and_fusion), kind=kOutput, calls=%fused_computation.26 | convolution fusion | flops 810156032 | bytes 5248000 | tf_op jit(solution)/shard_map/dot_general | solution.py:90
  41.5 3.7 %collective-permute-start.3 = (bf16[272,128]{1,0:T(8,128)(2,1)S(1)}, bf16[272,128]{1,0:T(8,128)(2,1)S(1)}, u32[]{:S(2)}, u32[]{:S(2)}) collective-permute-start(bf16[272,128]{1,0:T(8,128)(2,1)S(1)} %pad_maximum_fusion.8), channel_id=1, source_target_pairs={{0,6},{2,4},{4,2},{6,0},{8,14},{10,12},{12,10},{14,8},{16,22},{18,... | collective-permute-start | bytes 208904 | tf_op jit(solution)/shard_map/ppermute | solution.py:26
  45.9 2.2 %convolution_multiply_fusion.2 = f32[256,512]{1,0:T(8,128)S(1)} fusion(bf16[128,3072]{1,0:T(8,128)(2,1)} %collective-permute-done, bf16[128,3072]{1,0:T(8,128)(2,1)S(1)} %copy-done.10, f32[512]{0:T(512)S(1)} %get-tuple-element.125, bf16[3072,512]{1,0:T(8,128)(2,1)S(1)} %copy-done.7, pred[3072]{0:T(1024)(128)(4,1)S(1)} %compare_and_fusion), kind=kOutput, calls=%fused_computation.25 | convolution fusion | flops 810156032 | bytes 5248000 | tf_op jit(solution)/shard_map/dot_general | solution.py:90
  48.3 2.9 %collective-permute-start.15 = (bf16[272,128]{1,0:T(8,128)(2,1)S(1)}, bf16[272,128]{1,0:T(8,128)(2,1)S(1)}, u32[]{:S(2)}, u32[]{:S(2)}) collective-permute-start(bf16[272,128]{1,0:T(8,128)(2,1)S(1)} %pad_maximum_fusion.12), channel_id=1, source_target_pairs={{0,6},{2,4},{4,2},{6,0},{8,14},{10,12},{12,10},{14,8},{16,22},{18,... | collective-permute-start | bytes 208904 | tf_op jit(solution)/shard_map/ppermute | solution.py:26
  52.3 2.0 collective-permute-start.4
  54.3 2.6 %collective-permute-start.5 = (f32[264,32]{1,0:T(8,128)S(1)}, f32[264,32]{1,0:T(8,128)S(1)}, u32[]{:S(2)}, u32[]{:S(2)}) collective-permute-start(f32[264,32]{1,0:T(8,128)S(1)} %get-tuple-element.120), channel_id=1, source_target_pairs={{0,16},{2,18},{4,20},{6,22},{8,24},{10,26},{12,28},{14,30},{16,0},... | collective-permute-start | bytes 101384 | tf_op jit(solution)/shard_map/ppermute | solution.py:26
  58.2 3.5 %collective-permute-start.17 = (f32[264,32]{1,0:T(8,128)S(1)}, f32[264,32]{1,0:T(8,128)S(1)}, u32[]{:S(2)}, u32[]{:S(2)}) collective-permute-start(f32[264,32]{1,0:T(8,128)S(1)} %get-tuple-element.123), channel_id=1, source_target_pairs={{0,16},{2,18},{4,20},{6,22},{8,24},{10,26},{12,28},{14,30},{16,0},... | collective-permute-start | bytes 101384 | tf_op jit(solution)/shard_map/ppermute | solution.py:26
  62.9 4.6 %collective-permute-done.5 = f32[264,32]{1,0:T(8,128)S(1)} collective-permute-done((f32[264,32]{1,0:T(8,128)S(1)}, f32[264,32]{1,0:T(8,128)S(1)}, u32[]{:S(2)}, u32[]{:S(2)}) %collective-permute-start.5) | collective-permute-done | bytes 33824 | tf_op jit(solution)/shard_map/ppermute | solution.py:26
  67.6 9.7 %collective-permute-start.7 = (bf16[272,32]{1,0:T(8,128)(2,1)S(1)}, bf16[272,32]{1,0:T(8,128)(2,1)S(1)}, u32[]{:S(2)}, u32[]{:S(2)}) collective-permute-start(bf16[272,32]{1,0:T(8,128)(2,1)S(1)} %pad_maximum_fusion.9), channel_id=1, source_target_pairs={{0,8},{2,10},{4,12},{6,14},{8,0},{10,2},{12,4},{14,6},{16,24},{18,... | collective-permute-start | bytes 52232 | tf_op jit(solution)/shard_map/ppermute | solution.py:36
  77.3 1.4 collective-permute-start.8
  78.7 1.4 collective-permute-start.9
  80.3 2.8 %collective-permute-start.19 = (bf16[272,32]{1,0:T(8,128)(2,1)S(1)}, bf16[272,32]{1,0:T(8,128)(2,1)}, u32[]{:S(2)}, u32[]{:S(2)}) collective-permute-start(bf16[272,32]{1,0:T(8,128)(2,1)S(1)} %pad_maximum_fusion.13), channel_id=1, source_target_pairs={{0,8},{2,10},{4,12},{6,14},{8,0},{10,2},{12,4},{14,6},{16,24},{18,... | collective-permute-start | bytes 52232 | tf_op jit(solution)/shard_map/ppermute | solution.py:36
  83.1 4.3 %collective-permute-start.20 = (bf16[272,32]{1,0:T(8,128)(2,1)S(1)}, bf16[272,32]{1,0:T(8,128)(2,1)}, u32[]{:S(2)}, u32[]{:S(2)}) collective-permute-start(bf16[272,32]{1,0:T(8,128)(2,1)S(1)} %pad_maximum_fusion.13), channel_id=1, source_target_pairs={{0,16},{2,18},{4,20},{6,22},{8,24},{10,26},{12,28},{14,30},{16,0},... | collective-permute-start | bytes 52232 | tf_op jit(solution)/shard_map/ppermute | solution.py:36
  87.4 1.5 collective-permute-start.21
  89.5 1.4 dynamic_update_slice.97
  91.4 1.4 dynamic_update_slice.99
  92.8 1.5 collective-permute-start.10
  94.4 1.5 collective-permute-start.11
  96.4 1.3 dynamic_update_slice.105
  97.8 1.4 dynamic_update_slice.106
  99.2 1.4 dynamic_update_slice.107
  100.5 1.5 collective-permute-start.22
  102.1 1.5 collective-permute-start.23
  103.7 1.2 collective-permute-done.22
  104.9 2.4 %collective-permute-start.24 = (bf16[272,128]{1,0:T(8,128)(2,1)S(1)}, bf16[272,128]{1,0:T(8,128)(2,1)S(1)}, u32[]{:S(2)}, u32[]{:S(2)}) collective-permute-start(bf16[272,128]{1,0:T(8,128)(2,1)S(1)} %dynamic_update_slice.107), channel_id=1, source_target_pairs={{0,6},{2,4},{4,2},{6,0},{8,14},{10,12},{12,10},{14,8},{16,22},{18,... | collective-permute-start | bytes 208904 | tf_op jit(solution)/shard_map/ppermute | solution.py:36
  107.4 2.7 %collective-permute-done.24 = bf16[272,128]{1,0:T(8,128)(2,1)S(1)} collective-permute-done((bf16[272,128]{1,0:T(8,128)(2,1)S(1)}, bf16[272,128]{1,0:T(8,128)(2,1)S(1)}, u32[]{:S(2)}, u32[]{:S(2)}) %collective-permute-start.24) | collective-permute-done | bytes 69664 | tf_op jit(solution)/shard_map/ppermute | solution.py:36
  110.2 1.2 fusion.14
  112.3 1.9 fusion
  115.3 1.4 collective-permute-done.25
  118.9 2.3 %collective-permute-done.27 = bf16[128,3072]{1,0:T(8,128)(2,1)} collective-permute-done((bf16[128,3072]{1,0:T(8,128)(2,1)}, bf16[128,3072]{1,0:T(8,128)(2,1)}, u32[]{:S(2)}, u32[]{:S(2)}) %collective-permute-start.27) | collective-permute-done | bytes 786464 | tf_op jit(solution)/shard_map/ppermute | solution.py:81
  121.2 3.4 %convolution_multiply_fusion.1 = f32[256,512]{1,0:T(8,128)S(1)} fusion(bf16[128,3072]{1,0:T(8,128)(2,1)} %collective-permute-done.27, bf16[128,3072]{1,0:T(8,128)(2,1)} %convert_element_type.366, f32[512]{0:T(512)S(1)} %get-tuple-element.124, bf16[3072,512]{1,0:T(8,128)(2,1)} %gather_fusion, pred[3072]{0:T(1024)(128)(4,1)S(1)} %compare_and_fusion), kind=kOutput, calls=%fused_computation.24 | convolution fusion | flops 810156032 | bytes 5248000 | tf_op jit(solution)/shard_map/dot_general | solution.py:90
  124.9 2.5 %convolution_multiply_fusion = f32[256,512]{1,0:T(8,128)S(1)} fusion(bf16[128,3072]{1,0:T(8,128)(2,1)} %collective-permute-done.27, bf16[128,3072]{1,0:T(8,128)(2,1)} %convert_element_type.366, f32[512]{0:T(512)S(1)} %get-tuple-element.125, bf16[3072,512]{1,0:T(8,128)(2,1)S(1)} %copy-done.8, pred[3072]{0:T(1024)(128)(4,1)S(1)} %compare_and_fusion), kind=kOutput, calls=%fused_computation.23 | convolution fusion | flops 810156032 | bytes 5248000 | tf_op jit(solution)/shard_map/dot_general | solution.py:90
  127.4 2.5 %collective-permute-start.30 = (bf16[272,128]{1,0:T(8,128)(2,1)S(1)}, bf16[272,128]{1,0:T(8,128)(2,1)S(1)}, u32[]{:S(2)}, u32[]{:S(2)}) collective-permute-start(bf16[272,128]{1,0:T(8,128)(2,1)S(1)} %pad_maximum_fusion.16), channel_id=1, source_target_pairs={{0,6},{2,4},{4,2},{6,0},{8,14},{10,12},{12,10},{14,8},{16,22},{18,... | collective-permute-start | bytes 208904 | tf_op jit(solution)/shard_map/ppermute | solution.py:26
  131.0 2.5 %collective-permute-start.42 = (bf16[272,128]{1,0:T(8,128)(2,1)S(1)}, bf16[272,128]{1,0:T(8,128)(2,1)S(1)}, u32[]{:S(2)}, u32[]{:S(2)}) collective-permute-start(bf16[272,128]{1,0:T(8,128)(2,1)S(1)} %pad_maximum_fusion.20), channel_id=1, source_target_pairs={{0,6},{2,4},{4,2},{6,0},{8,14},{10,12},{12,10},{14,8},{16,22},{18,... | collective-permute-start | bytes 208904 | tf_op jit(solution)/shard_map/ppermute | solution.py:26
  135.7 1.2 collective-permute-start.31
  136.9 1.8 collective-permute-start.32
  138.7 1.5 collective-permute-start.33
  140.8 2.7 %collective-permute-start.44 = (f32[264,32]{1,0:T(8,128)S(1)}, f32[264,32]{1,0:T(8,128)S(1)}, u32[]{:S(2)}, u32[]{:S(2)}) collective-permute-start(f32[264,32]{1,0:T(8,128)S(1)} %get-tuple-element.114), channel_id=1, source_target_pairs={{0,16},{2,18},{4,20},{6,22},{8,24},{10,26},{12,28},{14,30},{16,0},... | collective-permute-start | bytes 101384 | tf_op jit(solution)/shard_map/ppermute | solution.py:26
  143.5 3.1 %collective-permute-start.45 = (f32[264,32]{1,0:T(8,128)S(1)}, f32[264,32]{1,0:T(8,128)S(1)}, u32[]{:S(2)}, u32[]{:S(2)}) collective-permute-start(f32[264,32]{1,0:T(8,128)S(1)} %get-tuple-element.113), channel_id=1, source_target_pairs={{0,24},{2,26},{4,28},{6,30},{8,16},{10,18},{12,20},{14,22},{16,8},... | collective-permute-start | bytes 101384 | tf_op jit(solution)/shard_map/ppermute | solution.py:26
  146.6 3.5 %collective-permute-done.32 = f32[264,32]{1,0:T(8,128)S(1)} collective-permute-done((f32[264,32]{1,0:T(8,128)S(1)}, f32[264,32]{1,0:T(8,128)S(1)}, u32[]{:S(2)}, u32[]{:S(2)}) %collective-permute-start.32) | collective-permute-done | bytes 33824 | tf_op jit(solution)/shard_map/ppermute | solution.py:26
  150.2 9.2 %collective-permute-start.34 = (bf16[272,32]{1,0:T(8,128)(2,1)S(1)}, bf16[272,32]{1,0:T(8,128)(2,1)S(1)}, u32[]{:S(2)}, u32[]{:S(2)}) collective-permute-start(bf16[272,32]{1,0:T(8,128)(2,1)S(1)} %pad_maximum_fusion.17), channel_id=1, source_target_pairs={{0,8},{2,10},{4,12},{6,14},{8,0},{10,2},{12,4},{14,6},{16,24},{18,... | collective-permute-start | bytes 52232 | tf_op jit(solution)/shard_map/ppermute | solution.py:36
  160.1 1.8 collective-permute-start.36
  162.1 3.9 %collective-permute-start.46 = (bf16[272,32]{1,0:T(8,128)(2,1)S(1)}, bf16[272,32]{1,0:T(8,128)(2,1)}, u32[]{:S(2)}, u32[]{:S(2)}) collective-permute-start(bf16[272,32]{1,0:T(8,128)(2,1)S(1)} %pad_maximum_fusion.21), channel_id=1, source_target_pairs={{0,8},{2,10},{4,12},{6,14},{8,0},{10,2},{12,4},{14,6},{16,24},{18,... | collective-permute-start | bytes 52232 | tf_op jit(solution)/shard_map/ppermute | solution.py:36
  166.6 1.8 collective-permute-start.48
  169.0 1.4 dynamic_update_slice.113
  171.0 1.4 dynamic_update_slice.115
  172.4 3.1 %collective-permute-start.37 = (bf16[272,128]{1,0:T(8,128)(2,1)S(1)}, bf16[272,128]{1,0:T(8,128)(2,1)}, u32[]{:S(2)}, u32[]{:S(2)}) collective-permute-start(bf16[272,128]{1,0:T(8,128)(2,1)S(1)} %dynamic_update_slice.115), channel_id=1, source_target_pairs={{0,2},{2,0},{4,6},{6,4},{8,10},{10,8},{12,14},{14,12},{16,18},{18,... | collective-permute-start | bytes 208904 | tf_op jit(solution)/shard_map/ppermute | solution.py:36
  175.5 1.5 collective-permute-start.39
  177.1 1.3 dynamic_update_slice.121
  178.4 1.4 dynamic_update_slice.122
  179.8 1.4 dynamic_update_slice.123
  181.2 2.0 collective-permute-start.49
  183.3 2.2 %collective-permute-done.49 = bf16[272,128]{1,0:T(8,128)(2,1)S(1)} collective-permute-done((bf16[272,128]{1,0:T(8,128)(2,1)S(1)}, bf16[272,128]{1,0:T(8,128)(2,1)S(1)}, u32[]{:S(2)}, u32[]{:S(2)}) %collective-permute-start.49) | collective-permute-done | bytes 69664 | tf_op jit(solution)/shard_map/ppermute | solution.py:36
  185.6 1.6 collective-permute-start.51
  187.6 3.2 %collective-permute-done.51 = bf16[272,128]{1,0:T(8,128)(2,1)S(1)} collective-permute-done((bf16[272,128]{1,0:T(8,128)(2,1)S(1)}, bf16[272,128]{1,0:T(8,128)(2,1)S(1)}, u32[]{:S(2)}, u32[]{:S(2)}) %collective-permute-start.51) | collective-permute-done | bytes 69664 | tf_op jit(solution)/shard_map/ppermute | solution.py:36
  190.8 4.1 %fusion.11 = f32[256,3072]{1,0:T(8,128)S(1)} fusion(bf16[272,512]{1,0:T(8,128)(2,1)S(1)} %constant_dynamic-update-slice_fusion, bf16[3072,512]{1,0:T(8,128)(2,1)} %gather_fusion.1, pred[3072]{0:T(1024)(128)(4,1)S(1)} %compare_and_fusion), kind=kOutput, calls=%fused_computation.66 | convolution fusion | flops 806879232 | bytes 6556672 | tf_op jit(solution)/shard_map/dot_general | solution.py:102
  196.0 1.7 fusion.1
  198.7 1.4 collective-permute-done.52
  200.2 2.9 %fusion.6 = (f32[128,3072]{1,0:T(8,128)}, f32[128,3072]{1,0:T(8,128)}) fusion(f32[128,3072]{1,0:T(8,128)S(1)} %get-tuple-element.73, bf16[128,3072]{1,0:T(8,128)(2,1)S(1)} %collective-permute-done.53, bf16[128,3072]{1,0:T(8,128)(2,1)S(1)} %copy-done.4, f32[128,3072]{1,0:T(8,128)S(1)} %copy-done, bf16[256,3072]{1,0:T(8,128)(2,1)S(1)} %fusion.1, ...), kind=kLoop, calls=%fused_computation.16 | loop fusion | flops 8650752 | bytes 9454080 | tf_op jit(solution)/shard_map/sub | solution.py:130
  (238 shorter events, 20.7 us)
Async XLA Ops:
  2.8 4.4 %copy-start.9 = (bf16[128,3072]{1,0:T(8,128)(2,1)}, bf16[128,3072]{1,0:T(8,128)(2,1)S(1)}, u32[]{:S(2)}) copy-start(bf16[128,3072]{1,0:T(8,128)(2,1)S(1)} %select_convert_fusion) | copy-start | bytes 2359300
  2.8 34.9 %collective-permute-start = (bf16[128,3072]{1,0:T(8,128)(2,1)S(1)}, bf16[128,3072]{1,0:T(8,128)(2,1)}, u32[]{:S(2)}, u32[]{:S(2)}) collective-permute-start(bf16[128,3072]{1,0:T(8,128)(2,1)S(1)} %select_convert_fusion), channel_id=1, source_target_pairs={{0,1},{1,0},{2,3},{3,2},{4,5},{5,4},{6,7},{7,6},{8,9},{9,8},{10,11... | collective-permute-start | bytes 2359304 | tf_op jit(solution)/shard_map/ppermute | solution.py:81
  3.4 3.8 %copy-start.14 = (s32[3072]{0:T(1024)S(1)}, s32[3072]{0:T(1024)}, u32[]{:S(2)}) copy-start(s32[3072]{0:T(1024)} %param.17) | copy-start | bytes 36868
  22.4 13.2 %copy-start.11 = (f32[3072]{0:T(1024)S(1)}, f32[3072]{0:T(1024)}, u32[]{:S(2)}) copy-start(f32[3072]{0:T(1024)} %param.19) | copy-start | bytes 36868
  37.8 8.2 %copy-start.7 = (bf16[3072,512]{1,0:T(8,128)(2,1)S(1)}, bf16[3072,512]{1,0:T(8,128)(2,1)}, u32[]{:S(2)}) copy-start(bf16[3072,512]{1,0:T(8,128)(2,1)} %gather_fusion.1) | copy-start | bytes 9437188
  41.4 4.6 %copy-start.10 = (bf16[128,3072]{1,0:T(8,128)(2,1)S(1)}, bf16[128,3072]{1,0:T(8,128)(2,1)}, u32[]{:S(2)}) copy-start(bf16[128,3072]{1,0:T(8,128)(2,1)} %copy-done.9) | copy-start | bytes 2359300
  41.5 10.2 %collective-permute-start.3 = (bf16[272,128]{1,0:T(8,128)(2,1)S(1)}, bf16[272,128]{1,0:T(8,128)(2,1)S(1)}, u32[]{:S(2)}, u32[]{:S(2)}) collective-permute-start(bf16[272,128]{1,0:T(8,128)(2,1)S(1)} %pad_maximum_fusion.8), channel_id=1, source_target_pairs={{0,6},{2,4},{4,2},{6,0},{8,14},{10,12},{12,10},{14,8},{16,22},{18,... | collective-permute-start | bytes 208904 | tf_op jit(solution)/shard_map/ppermute | solution.py:26
  45.3 6.7 %collective-permute-start.2 = (bf16[272,128]{1,0:T(8,128)(2,1)S(1)}, bf16[272,128]{1,0:T(8,128)(2,1)S(1)}, u32[]{:S(2)}, u32[]{:S(2)}) collective-permute-start(bf16[272,128]{1,0:T(8,128)(2,1)S(1)} %pad_maximum_fusion.7), channel_id=1, source_target_pairs={{0,4},{2,6},{4,0},{6,2},{8,12},{10,14},{12,8},{14,10},{16,20},{18,... | collective-permute-start | bytes 208904 | tf_op jit(solution)/shard_map/ppermute | solution.py:26
  45.8 6.2 %collective-permute-start.1 = (bf16[272,128]{1,0:T(8,128)(2,1)S(1)}, bf16[272,128]{1,0:T(8,128)(2,1)S(1)}, u32[]{:S(2)}, u32[]{:S(2)}) collective-permute-start(bf16[272,128]{1,0:T(8,128)(2,1)S(1)} %pad_maximum_fusion.6), channel_id=1, source_target_pairs={{0,2},{2,0},{4,6},{6,4},{8,10},{10,8},{12,14},{14,12},{16,18},{18,... | collective-permute-start | bytes 208904 | tf_op jit(solution)/shard_map/ppermute | solution.py:26
  48.3 8.6 %collective-permute-start.15 = (bf16[272,128]{1,0:T(8,128)(2,1)S(1)}, bf16[272,128]{1,0:T(8,128)(2,1)S(1)}, u32[]{:S(2)}, u32[]{:S(2)}) collective-permute-start(bf16[272,128]{1,0:T(8,128)(2,1)S(1)} %pad_maximum_fusion.12), channel_id=1, source_target_pairs={{0,6},{2,4},{4,2},{6,0},{8,14},{10,12},{12,10},{14,8},{16,22},{18,... | collective-permute-start | bytes 208904 | tf_op jit(solution)/shard_map/ppermute | solution.py:26
  51.2 6.5 %collective-permute-start.14 = (bf16[272,128]{1,0:T(8,128)(2,1)S(1)}, bf16[272,128]{1,0:T(8,128)(2,1)S(1)}, u32[]{:S(2)}, u32[]{:S(2)}) collective-permute-start(bf16[272,128]{1,0:T(8,128)(2,1)S(1)} %pad_maximum_fusion.11), channel_id=1, source_target_pairs={{0,4},{2,6},{4,0},{6,2},{8,12},{10,14},{12,8},{14,10},{16,20},{18,... | collective-permute-start | bytes 208904 | tf_op jit(solution)/shard_map/ppermute | solution.py:26
  51.7 6.0 %collective-permute-start.13 = (bf16[272,128]{1,0:T(8,128)(2,1)S(1)}, bf16[272,128]{1,0:T(8,128)(2,1)S(1)}, u32[]{:S(2)}, u32[]{:S(2)}) collective-permute-start(bf16[272,128]{1,0:T(8,128)(2,1)S(1)} %pad_maximum_fusion.10), channel_id=1, source_target_pairs={{0,2},{2,0},{4,6},{6,4},{8,10},{10,8},{12,14},{14,12},{16,18},{18,... | collective-permute-start | bytes 208904 | tf_op jit(solution)/shard_map/ppermute | solution.py:26
  52.3 9.4 %collective-permute-start.4 = (f32[264,32]{1,0:T(8,128)S(1)}, f32[264,32]{1,0:T(8,128)S(1)}, u32[]{:S(2)}, u32[]{:S(2)}) collective-permute-start(f32[264,32]{1,0:T(8,128)S(1)} %get-tuple-element.118), channel_id=1, source_target_pairs={{0,8},{2,10},{4,12},{6,14},{8,0},{10,2},{12,4},{14,6},{16,24},{18,... | collective-permute-start | bytes 101384 | tf_op jit(solution)/shard_map/ppermute | solution.py:26
  54.3 13.1 %collective-permute-start.5 = (f32[264,32]{1,0:T(8,128)S(1)}, f32[264,32]{1,0:T(8,128)S(1)}, u32[]{:S(2)}, u32[]{:S(2)}) collective-permute-start(f32[264,32]{1,0:T(8,128)S(1)} %get-tuple-element.120), channel_id=1, source_target_pairs={{0,16},{2,18},{4,20},{6,22},{8,24},{10,26},{12,28},{14,30},{16,0},... | collective-permute-start | bytes 101384 | tf_op jit(solution)/shard_map/ppermute | solution.py:26
  56.9 10.6 %collective-permute-start.6 = (f32[264,32]{1,0:T(8,128)S(1)}, f32[264,32]{1,0:T(8,128)S(1)}, u32[]{:S(2)}, u32[]{:S(2)}) collective-permute-start(f32[264,32]{1,0:T(8,128)S(1)} %get-tuple-element.119), channel_id=1, source_target_pairs={{0,24},{2,26},{4,28},{6,30},{8,16},{10,18},{12,20},{14,22},{16,8},... | collective-permute-start | bytes 101384 | tf_op jit(solution)/shard_map/ppermute | solution.py:26
  58.0 20.7 %collective-permute-start.16 = (f32[264,32]{1,0:T(8,128)S(1)}, f32[264,32]{1,0:T(8,128)S(1)}, u32[]{:S(2)}, u32[]{:S(2)}) collective-permute-start(f32[264,32]{1,0:T(8,128)S(1)} %get-tuple-element.121), channel_id=1, source_target_pairs={{0,8},{2,10},{4,12},{6,14},{8,0},{10,2},{12,4},{14,6},{16,24},{18,... | collective-permute-start | bytes 101384 | tf_op jit(solution)/shard_map/ppermute | solution.py:26
  58.2 21.9 %collective-permute-start.17 = (f32[264,32]{1,0:T(8,128)S(1)}, f32[264,32]{1,0:T(8,128)S(1)}, u32[]{:S(2)}, u32[]{:S(2)}) collective-permute-start(f32[264,32]{1,0:T(8,128)S(1)} %get-tuple-element.123), channel_id=1, source_target_pairs={{0,16},{2,18},{4,20},{6,22},{8,24},{10,26},{12,28},{14,30},{16,0},... | collective-permute-start | bytes 101384 | tf_op jit(solution)/shard_map/ppermute | solution.py:26
  61.7 18.4 %collective-permute-start.18 = (f32[264,32]{1,0:T(8,128)S(1)}, f32[264,32]{1,0:T(8,128)S(1)}, u32[]{:S(2)}, u32[]{:S(2)}) collective-permute-start(f32[264,32]{1,0:T(8,128)S(1)} %get-tuple-element.122), channel_id=1, source_target_pairs={{0,24},{2,26},{4,28},{6,30},{8,16},{10,18},{12,20},{14,22},{16,8},... | collective-permute-start | bytes 101384 | tf_op jit(solution)/shard_map/ppermute | solution.py:26
  67.6 19.8 %collective-permute-start.7 = (bf16[272,32]{1,0:T(8,128)(2,1)S(1)}, bf16[272,32]{1,0:T(8,128)(2,1)S(1)}, u32[]{:S(2)}, u32[]{:S(2)}) collective-permute-start(bf16[272,32]{1,0:T(8,128)(2,1)S(1)} %pad_maximum_fusion.9), channel_id=1, source_target_pairs={{0,8},{2,10},{4,12},{6,14},{8,0},{10,2},{12,4},{14,6},{16,24},{18,... | collective-permute-start | bytes 52232 | tf_op jit(solution)/shard_map/ppermute | solution.py:36
  77.3 13.5 %collective-permute-start.8 = (bf16[272,32]{1,0:T(8,128)(2,1)S(1)}, bf16[272,32]{1,0:T(8,128)(2,1)S(1)}, u32[]{:S(2)}, u32[]{:S(2)}) collective-permute-start(bf16[272,32]{1,0:T(8,128)(2,1)S(1)} %pad_maximum_fusion.9), channel_id=1, source_target_pairs={{0,16},{2,18},{4,20},{6,22},{8,24},{10,26},{12,28},{14,30},{16,0},... | collective-permute-start | bytes 52232 | tf_op jit(solution)/shard_map/ppermute | solution.py:36
  78.7 12.7 %collective-permute-start.9 = (bf16[272,32]{1,0:T(8,128)(2,1)S(1)}, bf16[272,32]{1,0:T(8,128)(2,1)}, u32[]{:S(2)}, u32[]{:S(2)}) collective-permute-start(bf16[272,32]{1,0:T(8,128)(2,1)S(1)} %pad_maximum_fusion.9), channel_id=1, source_target_pairs={{0,24},{2,26},{4,28},{6,30},{8,16},{10,18},{12,20},{14,22},{16,8},... | collective-permute-start | bytes 52232 | tf_op jit(solution)/shard_map/ppermute | solution.py:36
  80.3 15.6 %collective-permute-start.19 = (bf16[272,32]{1,0:T(8,128)(2,1)S(1)}, bf16[272,32]{1,0:T(8,128)(2,1)}, u32[]{:S(2)}, u32[]{:S(2)}) collective-permute-start(bf16[272,32]{1,0:T(8,128)(2,1)S(1)} %pad_maximum_fusion.13), channel_id=1, source_target_pairs={{0,8},{2,10},{4,12},{6,14},{8,0},{10,2},{12,4},{14,6},{16,24},{18,... | collective-permute-start | bytes 52232 | tf_op jit(solution)/shard_map/ppermute | solution.py:36
  83.1 14.6 %collective-permute-start.20 = (bf16[272,32]{1,0:T(8,128)(2,1)S(1)}, bf16[272,32]{1,0:T(8,128)(2,1)}, u32[]{:S(2)}, u32[]{:S(2)}) collective-permute-start(bf16[272,32]{1,0:T(8,128)(2,1)S(1)} %pad_maximum_fusion.13), channel_id=1, source_target_pairs={{0,16},{2,18},{4,20},{6,22},{8,24},{10,26},{12,28},{14,30},{16,0},... | collective-permute-start | bytes 52232 | tf_op jit(solution)/shard_map/ppermute | solution.py:36
  87.4 11.8 %collective-permute-start.21 = (bf16[272,32]{1,0:T(8,128)(2,1)S(1)}, bf16[272,32]{1,0:T(8,128)(2,1)}, u32[]{:S(2)}, u32[]{:S(2)}) collective-permute-start(bf16[272,32]{1,0:T(8,128)(2,1)S(1)} %pad_maximum_fusion.13), channel_id=1, source_target_pairs={{0,24},{2,26},{4,28},{6,30},{8,16},{10,18},{12,20},{14,22},{16,8},... | collective-permute-start | bytes 52232 | tf_op jit(solution)/shard_map/ppermute | solution.py:36
  92.8 18.5 %collective-permute-start.10 = (bf16[272,128]{1,0:T(8,128)(2,1)S(1)}, bf16[272,128]{1,0:T(8,128)(2,1)}, u32[]{:S(2)}, u32[]{:S(2)}) collective-permute-start(bf16[272,128]{1,0:T(8,128)(2,1)S(1)} %dynamic_update_slice.99), channel_id=1, source_target_pairs={{0,2},{2,0},{4,6},{6,4},{8,10},{10,8},{12,14},{14,12},{16,18},{18,... | collective-permute-start | bytes 208904 | tf_op jit(solution)/shard_map/ppermute | solution.py:36
  94.4 17.9 %collective-permute-start.11 = (bf16[272,128]{1,0:T(8,128)(2,1)S(1)}, bf16[272,128]{1,0:T(8,128)(2,1)S(1)}, u32[]{:S(2)}, u32[]{:S(2)}) collective-permute-start(bf16[272,128]{1,0:T(8,128)(2,1)S(1)} %dynamic_update_slice.99), channel_id=1, source_target_pairs={{0,4},{2,6},{4,0},{6,2},{8,12},{10,14},{12,8},{14,10},{16,20},{18,... | collective-permute-start | bytes 208904 | tf_op jit(solution)/shard_map/ppermute | solution.py:36
  95.9 16.4 %collective-permute-start.12 = (bf16[272,128]{1,0:T(8,128)(2,1)S(1)}, bf16[272,128]{1,0:T(8,128)(2,1)S(1)}, u32[]{:S(2)}, u32[]{:S(2)}) collective-permute-start(bf16[272,128]{1,0:T(8,128)(2,1)S(1)} %dynamic_update_slice.99), channel_id=1, source_target_pairs={{0,6},{2,4},{4,2},{6,0},{8,14},{10,12},{12,10},{14,8},{16,22},{18,... | collective-permute-start | bytes 208904 | tf_op jit(solution)/shard_map/ppermute | solution.py:36
  100.5 4.4 %collective-permute-start.22 = (bf16[272,128]{1,0:T(8,128)(2,1)S(1)}, bf16[272,128]{1,0:T(8,128)(2,1)S(1)}, u32[]{:S(2)}, u32[]{:S(2)}) collective-permute-start(bf16[272,128]{1,0:T(8,128)(2,1)S(1)} %dynamic_update_slice.107), channel_id=1, source_target_pairs={{0,2},{2,0},{4,6},{6,4},{8,10},{10,8},{12,14},{14,12},{16,18},{18,... | collective-permute-start | bytes 208904 | tf_op jit(solution)/shard_map/ppermute | solution.py:36
  102.1 5.3 %collective-permute-start.23 = (bf16[272,128]{1,0:T(8,128)(2,1)S(1)}, bf16[272,128]{1,0:T(8,128)(2,1)S(1)}, u32[]{:S(2)}, u32[]{:S(2)}) collective-permute-start(bf16[272,128]{1,0:T(8,128)(2,1)S(1)} %dynamic_update_slice.107), channel_id=1, source_target_pairs={{0,4},{2,6},{4,0},{6,2},{8,12},{10,14},{12,8},{14,10},{16,20},{18,... | collective-permute-start | bytes 208904 | tf_op jit(solution)/shard_map/ppermute | solution.py:36
  104.9 5.2 %collective-permute-start.24 = (bf16[272,128]{1,0:T(8,128)(2,1)S(1)}, bf16[272,128]{1,0:T(8,128)(2,1)S(1)}, u32[]{:S(2)}, u32[]{:S(2)}) collective-permute-start(bf16[272,128]{1,0:T(8,128)(2,1)S(1)} %dynamic_update_slice.107), channel_id=1, source_target_pairs={{0,6},{2,4},{4,2},{6,0},{8,14},{10,12},{12,10},{14,8},{16,22},{18,... | collective-permute-start | bytes 208904 | tf_op jit(solution)/shard_map/ppermute | solution.py:36
  114.2 3.4 %copy-start.1 = (bf16[256,3072]{1,0:T(8,128)(2,1)}, bf16[256,3072]{1,0:T(8,128)(2,1)S(1)}, u32[]{:S(2)}) copy-start(bf16[256,3072]{1,0:T(8,128)(2,1)S(1)} %fusion) | copy-start | bytes 4718596
  114.3 2.4 %collective-permute-start.26 = (bf16[128,3072]{1,0:T(8,128)(2,1)S(1)}, bf16[128,3072]{1,0:T(8,128)(2,1)S(1)}, u32[]{:S(2)}, u32[]{:S(2)}) collective-permute-start(bf16[128,3072]{1,0:T(8,128)(2,1)S(1)} %slice.491), channel_id=1, source_target_pairs={{0,1},{1,0},{2,3},{3,2},{4,5},{5,4},{6,7},{7,6},{8,9},{9,8},{10,11... | collective-permute-start | bytes 2359304 | tf_op jit(solution)/shard_map/ppermute | solution.py:110
  114.7 2.0 collective-permute-start.25
  118.6 2.6 %collective-permute-start.27 = (bf16[128,3072]{1,0:T(8,128)(2,1)}, bf16[128,3072]{1,0:T(8,128)(2,1)}, u32[]{:S(2)}, u32[]{:S(2)}) collective-permute-start(bf16[128,3072]{1,0:T(8,128)(2,1)} %convert_element_type.366), channel_id=1, source_target_pairs={{0,1},{1,0},{2,3},{3,2},{4,5},{5,4},{6,7},{7,6},{8,9},{9,8},{10,11... | collective-permute-start | bytes 2359304 | tf_op jit(solution)/shard_map/ppermute | solution.py:81
  118.9 5.9 %copy-start.8 = (bf16[3072,512]{1,0:T(8,128)(2,1)S(1)}, bf16[3072,512]{1,0:T(8,128)(2,1)}, u32[]{:S(2)}) copy-start(bf16[3072,512]{1,0:T(8,128)(2,1)} %gather_fusion.1) | copy-start | bytes 9437188
  127.4 6.7 %collective-permute-start.30 = (bf16[272,128]{1,0:T(8,128)(2,1)S(1)}, bf16[272,128]{1,0:T(8,128)(2,1)S(1)}, u32[]{:S(2)}, u32[]{:S(2)}) collective-permute-start(bf16[272,128]{1,0:T(8,128)(2,1)S(1)} %pad_maximum_fusion.16), channel_id=1, source_target_pairs={{0,6},{2,4},{4,2},{6,0},{8,14},{10,12},{12,10},{14,8},{16,22},{18,... | collective-permute-start | bytes 208904 | tf_op jit(solution)/shard_map/ppermute | solution.py:26
  129.9 4.8 %collective-permute-start.29 = (bf16[272,128]{1,0:T(8,128)(2,1)S(1)}, bf16[272,128]{1,0:T(8,128)(2,1)S(1)}, u32[]{:S(2)}, u32[]{:S(2)}) collective-permute-start(bf16[272,128]{1,0:T(8,128)(2,1)S(1)} %pad_maximum_fusion.15), channel_id=1, source_target_pairs={{0,4},{2,6},{4,0},{6,2},{8,12},{10,14},{12,8},{14,10},{16,20},{18,... | collective-permute-start | bytes 208904 | tf_op jit(solution)/shard_map/ppermute | solution.py:26
  130.5 5.0 %collective-permute-start.28 = (bf16[272,128]{1,0:T(8,128)(2,1)S(1)}, bf16[272,128]{1,0:T(8,128)(2,1)S(1)}, u32[]{:S(2)}, u32[]{:S(2)}) collective-permute-start(bf16[272,128]{1,0:T(8,128)(2,1)S(1)} %pad_maximum_fusion.14), channel_id=1, source_target_pairs={{0,2},{2,0},{4,6},{6,4},{8,10},{10,8},{12,14},{14,12},{16,18},{18,... | collective-permute-start | bytes 208904 | tf_op jit(solution)/shard_map/ppermute | solution.py:26
  131.0 7.7 %collective-permute-start.42 = (bf16[272,128]{1,0:T(8,128)(2,1)S(1)}, bf16[272,128]{1,0:T(8,128)(2,1)S(1)}, u32[]{:S(2)}, u32[]{:S(2)}) collective-permute-start(bf16[272,128]{1,0:T(8,128)(2,1)S(1)} %pad_maximum_fusion.20), channel_id=1, source_target_pairs={{0,6},{2,4},{4,2},{6,0},{8,14},{10,12},{12,10},{14,8},{16,22},{18,... | collective-permute-start | bytes 208904 | tf_op jit(solution)/shard_map/ppermute | solution.py:26
  133.5 6.6 %collective-permute-start.41 = (bf16[272,128]{1,0:T(8,128)(2,1)S(1)}, bf16[272,128]{1,0:T(8,128)(2,1)S(1)}, u32[]{:S(2)}, u32[]{:S(2)}) collective-permute-start(bf16[272,128]{1,0:T(8,128)(2,1)S(1)} %pad_maximum_fusion.19), channel_id=1, source_target_pairs={{0,4},{2,6},{4,0},{6,2},{8,12},{10,14},{12,8},{14,10},{16,20},{18,... | collective-permute-start | bytes 208904 | tf_op jit(solution)/shard_map/ppermute | solution.py:26
  134.1 6.1 %collective-permute-start.40 = (bf16[272,128]{1,0:T(8,128)(2,1)S(1)}, bf16[272,128]{1,0:T(8,128)(2,1)S(1)}, u32[]{:S(2)}, u32[]{:S(2)}) collective-permute-start(bf16[272,128]{1,0:T(8,128)(2,1)S(1)} %pad_maximum_fusion.18), channel_id=1, source_target_pairs={{0,2},{2,0},{4,6},{6,4},{8,10},{10,8},{12,14},{14,12},{16,18},{18,... | collective-permute-start | bytes 208904 | tf_op jit(solution)/shard_map/ppermute | solution.py:26
  135.7 7.8 %collective-permute-start.31 = (f32[264,32]{1,0:T(8,128)S(1)}, f32[264,32]{1,0:T(8,128)S(1)}, u32[]{:S(2)}, u32[]{:S(2)}) collective-permute-start(f32[264,32]{1,0:T(8,128)S(1)} %get-tuple-element.115), channel_id=1, source_target_pairs={{0,8},{2,10},{4,12},{6,14},{8,0},{10,2},{12,4},{14,6},{16,24},{18,... | collective-permute-start | bytes 101384 | tf_op jit(solution)/shard_map/ppermute | solution.py:26
  136.9 13.1 %collective-permute-start.32 = (f32[264,32]{1,0:T(8,128)S(1)}, f32[264,32]{1,0:T(8,128)S(1)}, u32[]{:S(2)}, u32[]{:S(2)}) collective-permute-start(f32[264,32]{1,0:T(8,128)S(1)} %get-tuple-element.117), channel_id=1, source_target_pairs={{0,16},{2,18},{4,20},{6,22},{8,24},{10,26},{12,28},{14,30},{16,0},... | collective-permute-start | bytes 101384 | tf_op jit(solution)/shard_map/ppermute | solution.py:26
  138.7 11.3 %collective-permute-start.33 = (f32[264,32]{1,0:T(8,128)S(1)}, f32[264,32]{1,0:T(8,128)S(1)}, u32[]{:S(2)}, u32[]{:S(2)}) collective-permute-start(f32[264,32]{1,0:T(8,128)S(1)} %get-tuple-element.116), channel_id=1, source_target_pairs={{0,24},{2,26},{4,28},{6,30},{8,16},{10,18},{12,20},{14,22},{16,8},... | collective-permute-start | bytes 101384 | tf_op jit(solution)/shard_map/ppermute | solution.py:26
  140.5 19.6 %collective-permute-start.43 = (f32[264,32]{1,0:T(8,128)S(1)}, f32[264,32]{1,0:T(8,128)S(1)}, u32[]{:S(2)}, u32[]{:S(2)}) collective-permute-start(f32[264,32]{1,0:T(8,128)S(1)} %get-tuple-element.112), channel_id=1, source_target_pairs={{0,8},{2,10},{4,12},{6,14},{8,0},{10,2},{12,4},{14,6},{16,24},{18,... | collective-permute-start | bytes 101384 | tf_op jit(solution)/shard_map/ppermute | solution.py:26
  140.8 21.1 %collective-permute-start.44 = (f32[264,32]{1,0:T(8,128)S(1)}, f32[264,32]{1,0:T(8,128)S(1)}, u32[]{:S(2)}, u32[]{:S(2)}) collective-permute-start(f32[264,32]{1,0:T(8,128)S(1)} %get-tuple-element.114), channel_id=1, source_target_pairs={{0,16},{2,18},{4,20},{6,22},{8,24},{10,26},{12,28},{14,30},{16,0},... | collective-permute-start | bytes 101384 | tf_op jit(solution)/shard_map/ppermute | solution.py:26
  143.5 18.4 %collective-permute-start.45 = (f32[264,32]{1,0:T(8,128)S(1)}, f32[264,32]{1,0:T(8,128)S(1)}, u32[]{:S(2)}, u32[]{:S(2)}) collective-permute-start(f32[264,32]{1,0:T(8,128)S(1)} %get-tuple-element.113), channel_id=1, source_target_pairs={{0,24},{2,26},{4,28},{6,30},{8,16},{10,18},{12,20},{14,22},{16,8},... | collective-permute-start | bytes 101384 | tf_op jit(solution)/shard_map/ppermute | solution.py:26
  150.2 16.5 %collective-permute-start.34 = (bf16[272,32]{1,0:T(8,128)(2,1)S(1)}, bf16[272,32]{1,0:T(8,128)(2,1)S(1)}, u32[]{:S(2)}, u32[]{:S(2)}) collective-permute-start(bf16[272,32]{1,0:T(8,128)(2,1)S(1)} %pad_maximum_fusion.17), channel_id=1, source_target_pairs={{0,8},{2,10},{4,12},{6,14},{8,0},{10,2},{12,4},{14,6},{16,24},{18,... | collective-permute-start | bytes 52232 | tf_op jit(solution)/shard_map/ppermute | solution.py:36
  159.4 11.0 %collective-permute-start.35 = (bf16[272,32]{1,0:T(8,128)(2,1)S(1)}, bf16[272,32]{1,0:T(8,128)(2,1)S(1)}, u32[]{:S(2)}, u32[]{:S(2)}) collective-permute-start(bf16[272,32]{1,0:T(8,128)(2,1)S(1)} %pad_maximum_fusion.17), channel_id=1, source_target_pairs={{0,16},{2,18},{4,20},{6,22},{8,24},{10,26},{12,28},{14,30},{16,0},... | collective-permute-start | bytes 52232 | tf_op jit(solution)/shard_map/ppermute | solution.py:36
  160.1 10.9 %collective-permute-start.36 = (bf16[272,32]{1,0:T(8,128)(2,1)S(1)}, bf16[272,32]{1,0:T(8,128)(2,1)}, u32[]{:S(2)}, u32[]{:S(2)}) collective-permute-start(bf16[272,32]{1,0:T(8,128)(2,1)S(1)} %pad_maximum_fusion.17), channel_id=1, source_target_pairs={{0,24},{2,26},{4,28},{6,30},{8,16},{10,18},{12,20},{14,22},{16,8},... | collective-permute-start | bytes 52232 | tf_op jit(solution)/shard_map/ppermute | solution.py:36
  162.1 13.5 %collective-permute-start.46 = (bf16[272,32]{1,0:T(8,128)(2,1)S(1)}, bf16[272,32]{1,0:T(8,128)(2,1)}, u32[]{:S(2)}, u32[]{:S(2)}) collective-permute-start(bf16[272,32]{1,0:T(8,128)(2,1)S(1)} %pad_maximum_fusion.21), channel_id=1, source_target_pairs={{0,8},{2,10},{4,12},{6,14},{8,0},{10,2},{12,4},{14,6},{16,24},{18,... | collective-permute-start | bytes 52232 | tf_op jit(solution)/shard_map/ppermute | solution.py:36
  166.0 12.4 %collective-permute-start.47 = (bf16[272,32]{1,0:T(8,128)(2,1)S(1)}, bf16[272,32]{1,0:T(8,128)(2,1)}, u32[]{:S(2)}, u32[]{:S(2)}) collective-permute-start(bf16[272,32]{1,0:T(8,128)(2,1)S(1)} %pad_maximum_fusion.21), channel_id=1, source_target_pairs={{0,16},{2,18},{4,20},{6,22},{8,24},{10,26},{12,28},{14,30},{16,0},... | collective-permute-start | bytes 52232 | tf_op jit(solution)/shard_map/ppermute | solution.py:36
  166.6 13.2 %collective-permute-start.48 = (bf16[272,32]{1,0:T(8,128)(2,1)S(1)}, bf16[272,32]{1,0:T(8,128)(2,1)}, u32[]{:S(2)}, u32[]{:S(2)}) collective-permute-start(bf16[272,32]{1,0:T(8,128)(2,1)S(1)} %pad_maximum_fusion.21), channel_id=1, source_target_pairs={{0,24},{2,26},{4,28},{6,30},{8,16},{10,18},{12,20},{14,22},{16,8},... | collective-permute-start | bytes 52232 | tf_op jit(solution)/shard_map/ppermute | solution.py:36
  172.4 22.5 %collective-permute-start.37 = (bf16[272,128]{1,0:T(8,128)(2,1)S(1)}, bf16[272,128]{1,0:T(8,128)(2,1)}, u32[]{:S(2)}, u32[]{:S(2)}) collective-permute-start(bf16[272,128]{1,0:T(8,128)(2,1)S(1)} %dynamic_update_slice.115), channel_id=1, source_target_pairs={{0,2},{2,0},{4,6},{6,4},{8,10},{10,8},{12,14},{14,12},{16,18},{18,... | collective-permute-start | bytes 208904 | tf_op jit(solution)/shard_map/ppermute | solution.py:36
  175.5 20.4 %collective-permute-start.38 = (bf16[272,128]{1,0:T(8,128)(2,1)S(1)}, bf16[272,128]{1,0:T(8,128)(2,1)S(1)}, u32[]{:S(2)}, u32[]{:S(2)}) collective-permute-start(bf16[272,128]{1,0:T(8,128)(2,1)S(1)} %dynamic_update_slice.115), channel_id=1, source_target_pairs={{0,4},{2,6},{4,0},{6,2},{8,12},{10,14},{12,8},{14,10},{16,20},{18,... | collective-permute-start | bytes 208904 | tf_op jit(solution)/shard_map/ppermute | solution.py:36
  175.5 20.4 %collective-permute-start.39 = (bf16[272,128]{1,0:T(8,128)(2,1)S(1)}, bf16[272,128]{1,0:T(8,128)(2,1)S(1)}, u32[]{:S(2)}, u32[]{:S(2)}) collective-permute-start(bf16[272,128]{1,0:T(8,128)(2,1)S(1)} %dynamic_update_slice.115), channel_id=1, source_target_pairs={{0,6},{2,4},{4,2},{6,0},{8,14},{10,12},{12,10},{14,8},{16,22},{18,... | collective-permute-start | bytes 208904 | tf_op jit(solution)/shard_map/ppermute | solution.py:36
  181.2 4.4 %collective-permute-start.49 = (bf16[272,128]{1,0:T(8,128)(2,1)S(1)}, bf16[272,128]{1,0:T(8,128)(2,1)S(1)}, u32[]{:S(2)}, u32[]{:S(2)}) collective-permute-start(bf16[272,128]{1,0:T(8,128)(2,1)S(1)} %dynamic_update_slice.123), channel_id=1, source_target_pairs={{0,2},{2,0},{4,6},{6,4},{8,10},{10,8},{12,14},{14,12},{16,18},{18,... | collective-permute-start | bytes 208904 | tf_op jit(solution)/shard_map/ppermute | solution.py:36
  183.2 4.3 %collective-permute-start.50 = (bf16[272,128]{1,0:T(8,128)(2,1)S(1)}, bf16[272,128]{1,0:T(8,128)(2,1)S(1)}, u32[]{:S(2)}, u32[]{:S(2)}) collective-permute-start(bf16[272,128]{1,0:T(8,128)(2,1)S(1)} %dynamic_update_slice.123), channel_id=1, source_target_pairs={{0,4},{2,6},{4,0},{6,2},{8,12},{10,14},{12,8},{14,10},{16,20},{18,... | collective-permute-start | bytes 208904 | tf_op jit(solution)/shard_map/ppermute | solution.py:36
  185.6 5.2 %collective-permute-start.51 = (bf16[272,128]{1,0:T(8,128)(2,1)S(1)}, bf16[272,128]{1,0:T(8,128)(2,1)S(1)}, u32[]{:S(2)}, u32[]{:S(2)}) collective-permute-start(bf16[272,128]{1,0:T(8,128)(2,1)S(1)} %dynamic_update_slice.123), channel_id=1, source_target_pairs={{0,6},{2,4},{4,2},{6,0},{8,14},{10,12},{12,10},{14,8},{16,22},{18,... | collective-permute-start | bytes 208904 | tf_op jit(solution)/shard_map/ppermute | solution.py:36
  190.8 5.1 %copy-start.6 = (bf16[3072,512]{1,0:T(8,128)(2,1)S(1)}, bf16[3072,512]{1,0:T(8,128)(2,1)}, u32[]{:S(2)}) copy-start(bf16[3072,512]{1,0:T(8,128)(2,1)} %gather_fusion) | copy-start | bytes 9437188
  196.0 4.2 %copy-start.4 = (bf16[128,3072]{1,0:T(8,128)(2,1)S(1)}, bf16[128,3072]{1,0:T(8,128)(2,1)}, u32[]{:S(2)}) copy-start(bf16[128,3072]{1,0:T(8,128)(2,1)} %copy-done.3) | copy-start | bytes 2359300
  197.7 2.5 %copy-start.2 = (bf16[256,3072]{1,0:T(8,128)(2,1)S(1)}, bf16[256,3072]{1,0:T(8,128)(2,1)}, u32[]{:S(2)}) copy-start(bf16[256,3072]{1,0:T(8,128)(2,1)} %copy-done.1) | copy-start | bytes 4718596
  197.8 2.4 %collective-permute-start.53 = (bf16[128,3072]{1,0:T(8,128)(2,1)S(1)}, bf16[128,3072]{1,0:T(8,128)(2,1)S(1)}, u32[]{:S(2)}, u32[]{:S(2)}) collective-permute-start(bf16[128,3072]{1,0:T(8,128)(2,1)S(1)} %slice.527), channel_id=1, source_target_pairs={{0,1},{1,0},{2,3},{3,2},{4,5},{5,4},{6,7},{7,6},{8,9},{9,8},{10,11... | collective-permute-start | bytes 2359304 | tf_op jit(solution)/shard_map/ppermute | solution.py:110
  198.2 2.0 collective-permute-start.52
  (6 other events, 10.9 us)

commit v5 on v3

--- a/solution.py
+++ b/solution.py
@@ -12,7 +12,7 @@
     me = lax.axis_index("vert")
     cur = x
     plan = []
-    for first, group in enumerate(rounds):
+    for group in rounds:
         n = 1 << len(group)
         digit = sum(((me >> b) & 1) << i for i, b in enumerate(group))
         masks = [sum(((t >> i) & 1) << b for i, b in enumerate(group)) for t in range(n)]
@@ -20,10 +20,8 @@
         total = lax.dynamic_slice_in_dim(cur, digit * width, width, axis=1)
         for t in range(1, n):
             send = lax.dynamic_slice_in_dim(cur, (digit ^ t) * width, width, axis=1)
-            if first == 0:
-                send = encode(send)
-            got = lax.ppermute(send, "vert", [(i, i ^ masks[t]) for i in range(n_vert)])
-            total = total + (decode(got) if first == 0 else got)
+            got = lax.ppermute(encode(send), "vert", [(i, i ^ masks[t]) for i in range(n_vert)])
+            total = total + decode(got)
         cur = total
         plan.append((n, digit, masks))
     cur = finish(cur)

time: 145 us -> 132 us (0.910)
  waiting for transfers between devices: 53.5 us -> 42.3 us
  starting transfers between devices: 36.7 us -> 35.1 us
    ppermute x12, waiting for transfers between devices: 32.1 us -> 22 us  [vert_sum(): lax.ppermute(encode(send), 'vert', [(i, i ^ masks[t]) for i in range(n_ve...]
    ppermute x12, starting transfers between devices: 17.9 us -> 16 us  [vert_sum(): got = lax.ppermute(cur, 'vert', [(i, i ^ masks[t]) for i in range(n_vert)])]
  transfers between devices with their start and end apart: 30 -> 30, of which waited for: 21 -> 21; matrix products, arithmetic and copies ran while one was open for 16% -> 18% of each run, Pallas kernels for 0% -> 0%
where the time goes in v5:
time: 132 us
  waiting for transfers between devices  42.3 us (32%)
  starting transfers between devices  35.1 us (27%)
  local copies, waits for them, and re-layouts  24.4 us (18%)
  matrix products  19.4 us (15%)
  other arithmetic  8.61 us (7%)
  between operations  2.14 us (2%)
    ppermute x12, waiting for transfers between devices, vert_sum(): lax.ppermute(encode(send), 'vert', [(i, i ^ masks[t]) for i in range(n_ve...  22 us
    gather x1, local copies, waits for them, and re-layouts, shards(): features = jnp.take(eig_table, obs_ids, axis=0)  18.7 us
    ppermute x12, starting transfers between devices, vert_sum(): lax.ppermute(encode(send), 'vert', [(i, i ^ masks[t]) for i in range(n_ve...  17.1 us
    ppermute x12, starting transfers between devices, vert_sum(): got = lax.ppermute(cur, 'vert', [(i, i ^ masks[t]) for i in range(n_vert)])  16 us
    ppermute x12, waiting for transfers between devices, vert_sum(): got = lax.ppermute(cur, 'vert', [(i, i ^ masks[t]) for i in range(n_vert)])  15.2 us
    dot_general x2, matrix products, operate(): coeff = jnp.dot(rows, features, preferred_element_type=jnp.float32)  9.83 us
    dot_general x2, matrix products, operate(): lax.dot_general(weights, features, (((1,), (1,)), ((), ())), preferred_el...  9.56 us
    dynamic_update_slice x12, local copies, waits for them, and re-layouts, vert_sum(): out = lax.dynamic_update_slice_in_dim(out, got, (digit ^ t) * width, axis=1)  3.73 us
  transfers between devices with their start and end apart: 30, of which 21 were waited for; matrix products, arithmetic and copies ran while one was open for 18% of the time, Pallas kernels for 0%

profile of v5, /device:TPU:0, one launch (start us, length us, event | category | flops | bytes accessed | tf_op | source)
XLA Modules:
  0.0 131.9 jit_solution(9105957025591861650)
XLA Ops:
  1.3 1.5 %select_convert_fusion = bf16[128,3072]{1,0:T(8,128)(2,1)S(1)} fusion(f32[128,3072]{1,0:T(8,128)} %param.19, pred[3072]{0:T(1024)(128)(4,1)S(1)} %iota_compare_fusion), kind=kLoop, calls=%fused_computation.35 | loop fusion | flops 393216 | bytes 2362368 | tf_op jit(solution)/shard_map/convert_element_type | solution.py:71
  2.9 0.6 collective-permute-start
  3.4 18.7 %gather_fusion = bf16[3072,1024]{1,0:T(8,128)(2,1)} fusion(bf16[2048,1024]{1,0:T(8,128)(2,1)} %param.14, s32[3072]{0:T(1024)S(1)} %fusion.41), kind=kCustom, calls=%fused_computation | custom fusion | bytes 12595200 | tf_op jit(solution)/shard_map/jit(_take)/gather | solution.py:49
  22.2 0.4 fusion
  22.6 0.2 scatter.15
  22.9 4.7 %fusion.16 = f32[256,1024]{1,0:T(8,128)S(1)} fusion(bf16[128,3072]{1,0:T(8,128)(2,1)S(1)} %collective-permute-done, bf16[128,3072]{1,0:T(8,128)(2,1)S(1)} %select_convert_fusion, f32[1024]{0:T(1024)S(1)} %power_multiply_fusion, bf16[3072,1024]{1,0:T(8,128)(2,1)} %gather_fusion, pred[3072]{0:T(1024)(128)(4,1)S(1)} %compare_and_fusion), kind=kOutput, calls=%fused_computation.34 | convolution fusion | flops 1617166336 | bytes 8920064 | tf_op jit(solution)/shard_map/dot_general | solution.py:76
  27.8 3.6 %collective-permute-start.3 = (bf16[272,256]{1,0:T(8,128)(2,1)S(1)}, bf16[272,256]{1,0:T(8,128)(2,1)S(1)}, u32[]{:S(2)}, u32[]{:S(2)}) collective-permute-start(bf16[272,256]{1,0:T(8,128)(2,1)S(1)} %pad_maximum_fusion.2), channel_id=1, source_target_pairs={{0,6},{2,4},{4,2},{6,0},{8,14},{10,12},{12,10},{14,8},{16,22},{18,... | collective-permute-start | bytes 417800 | tf_op jit(solution)/shard_map/ppermute | solution.py:23
  31.4 0.6 collective-permute-start.2
  32.1 3.7 %collective-permute-done.3 = bf16[272,256]{1,0:T(8,128)(2,1)S(1)} collective-permute-done((bf16[272,256]{1,0:T(8,128)(2,1)S(1)}, bf16[272,256]{1,0:T(8,128)(2,1)S(1)}, u32[]{:S(2)}, u32[]{:S(2)}) %collective-permute-start.3) | collective-permute-done | bytes 139296 | tf_op jit(solution)/shard_map/ppermute | solution.py:23
  35.8 2.8 %collective-permute-done.2 = bf16[272,256]{1,0:T(8,128)(2,1)S(1)} collective-permute-done((bf16[272,256]{1,0:T(8,128)(2,1)S(1)}, bf16[272,256]{1,0:T(8,128)(2,1)S(1)}, u32[]{:S(2)}, u32[]{:S(2)}) %collective-permute-start.2) | collective-permute-done | bytes 139296 | tf_op jit(solution)/shard_map/ppermute | solution.py:23
  38.7 0.3 collective-permute-done.1
  39.3 3.7 %collective-permute-start.6 = (bf16[272,64]{1,0:T(8,128)(2,1)S(1)}, bf16[272,64]{1,0:T(8,128)(2,1)S(1)}, u32[]{:S(2)}, u32[]{:S(2)}) collective-permute-start(bf16[272,64]{1,0:T(8,128)(2,1)S(1)} %pad_maximum_fusion.8), channel_id=1, source_target_pairs={{0,24},{2,26},{4,28},{6,30},{8,16},{10,18},{12,20},{14,22},{16,8},... | collective-permute-start | bytes 104456 | tf_op jit(solution)/shard_map/ppermute | solution.py:23
  43.1 0.8 collective-permute-start.4
  44.0 1.8 %collective-permute-done.6 = bf16[272,64]{1,0:T(8,128)(2,1)S(1)} collective-permute-done((bf16[272,64]{1,0:T(8,128)(2,1)S(1)}, bf16[272,64]{1,0:T(8,128)(2,1)S(1)}, u32[]{:S(2)}, u32[]{:S(2)}) %collective-permute-start.6) | collective-permute-done | bytes 34848 | tf_op jit(solution)/shard_map/ppermute | solution.py:23
  45.8 3.3 %collective-permute-done.5 = bf16[272,64]{1,0:T(8,128)(2,1)S(1)} collective-permute-done((bf16[272,64]{1,0:T(8,128)(2,1)S(1)}, bf16[272,64]{1,0:T(8,128)(2,1)S(1)}, u32[]{:S(2)}, u32[]{:S(2)}) %collective-permute-start.5) | collective-permute-done | bytes 34848 | tf_op jit(solution)/shard_map/ppermute | solution.py:23
  49.3 1.1 collective-permute-start.7
  50.4 2.2 %collective-permute-start.8 = (bf16[272,64]{1,0:T(8,128)(2,1)S(1)}, bf16[272,64]{1,0:T(8,128)(2,1)S(1)}, u32[]{:S(2)}, u32[]{:S(2)}) collective-permute-start(bf16[272,64]{1,0:T(8,128)(2,1)S(1)} %pad_maximum_fusion.9), channel_id=1, source_target_pairs={{0,16},{2,18},{4,20},{6,22},{8,24},{10,26},{12,28},{14,30},{16,0},... | collective-permute-start | bytes 104456 | tf_op jit(solution)/shard_map/ppermute | solution.py:33
  52.5 1.2 collective-permute-start.9
  53.8 0.3 dynamic_update_slice.48
  54.1 0.6 dynamic_update_slice.49
  54.8 2.5 %collective-permute-done.8 = bf16[272,64]{1,0:T(8,128)(2,1)S(1)} collective-permute-done((bf16[272,64]{1,0:T(8,128)(2,1)S(1)}, bf16[272,64]{1,0:T(8,128)(2,1)S(1)}, u32[]{:S(2)}, u32[]{:S(2)}) %collective-permute-start.8) | collective-permute-done | bytes 34848 | tf_op jit(solution)/shard_map/ppermute | solution.py:33
  57.3 0.3 dynamic_update_slice.50
  57.6 1.2 collective-permute-done.9
  58.8 0.5 dynamic_update_slice.51
  59.3 1.6 %collective-permute-start.10 = (bf16[272,256]{1,0:T(8,128)(2,1)S(1)}, bf16[272,256]{1,0:T(8,128)(2,1)S(1)}, u32[]{:S(2)}, u32[]{:S(2)}) collective-permute-start(bf16[272,256]{1,0:T(8,128)(2,1)S(1)} %dynamic_update_slice.51), channel_id=1, source_target_pairs={{0,2},{2,0},{4,6},{6,4},{8,10},{10,8},{12,14},{14,12},{16,18},{18,... | collective-permute-start | bytes 417800 | tf_op jit(solution)/shard_map/ppermute | solution.py:33
  60.9 0.3 collective-permute-start.11
  61.2 1.7 %collective-permute-start.12 = (bf16[272,256]{1,0:T(8,128)(2,1)S(1)}, bf16[272,256]{1,0:T(8,128)(2,1)S(1)}, u32[]{:S(2)}, u32[]{:S(2)}) collective-permute-start(bf16[272,256]{1,0:T(8,128)(2,1)S(1)} %dynamic_update_slice.51), channel_id=1, source_target_pairs={{0,6},{2,4},{4,2},{6,0},{8,14},{10,12},{12,10},{14,8},{16,22},{18,... | collective-permute-start | bytes 417800 | tf_op jit(solution)/shard_map/ppermute | solution.py:33
  63.0 2.3 %collective-permute-done.10 = bf16[272,256]{1,0:T(8,128)(2,1)S(1)} collective-permute-done((bf16[272,256]{1,0:T(8,128)(2,1)S(1)}, bf16[272,256]{1,0:T(8,128)(2,1)S(1)}, u32[]{:S(2)}, u32[]{:S(2)}) %collective-permute-start.10) | collective-permute-done | bytes 139296 | tf_op jit(solution)/shard_map/ppermute | solution.py:33
  65.2 2.2 %collective-permute-done.11 = bf16[272,256]{1,0:T(8,128)(2,1)S(1)} collective-permute-done((bf16[272,256]{1,0:T(8,128)(2,1)S(1)}, bf16[272,256]{1,0:T(8,128)(2,1)S(1)}, u32[]{:S(2)}, u32[]{:S(2)}) %collective-permute-start.11) | collective-permute-done | bytes 139296 | tf_op jit(solution)/shard_map/ppermute | solution.py:33
  67.5 4.7 %convolution_convert_fusion.1 = bf16[256,3072]{1,0:T(8,128)(2,1)S(1)} fusion(bf16[272,1024]{1,0:T(8,128)(2,1)S(1)} %constant_dynamic-update-slice_fusion.4, bf16[3072,1024]{1,0:T(8,128)(2,1)} %gather_fusion, pred[3072]{0:T(1024)(128)(4,1)S(1)} %compare_and_fusion), kind=kOutput, calls=%fused_computation.3 | convolution fusion | flops 1614544896 | bytes 8391680 | tf_op jit(solution)/shard_map/dot_general | solution.py:89
  72.6 0.6 collective-permute-start.13
  73.1 1.5 %collective-permute-done.13 = f32[128]{0:T(128)S(1)} collective-permute-done((f32[128]{0:T(128)S(1)}, f32[128]{0:T(128)S(1)}, u32[]{:S(2)}, u32[]{:S(2)}) %collective-permute-start.13) | collective-permute-done | bytes 544 | tf_op jit(solution)/shard_map/ppermute | solution.py:93
  74.7 0.9 fusion.1
  75.6 1.0 convert_element_type.336
  76.7 0.3 scatter.19
  77.1 2.2 %collective-permute-done.15 = bf16[128,3072]{1,0:T(8,128)(2,1)} collective-permute-done((bf16[128,3072]{1,0:T(8,128)(2,1)}, bf16[128,3072]{1,0:T(8,128)(2,1)}, u32[]{:S(2)}, u32[]{:S(2)}) %collective-permute-start.15) | collective-permute-done | bytes 786464 | tf_op jit(solution)/shard_map/ppermute | solution.py:73
  79.2 5.2 %fusion.13 = f32[256,1024]{1,0:T(8,128)S(1)} fusion(bf16[128,3072]{1,0:T(8,128)(2,1)} %collective-permute-done.15, bf16[128,3072]{1,0:T(8,128)(2,1)} %convert_element_type.336, f32[1024]{0:T(1024)S(1)} %power_multiply_fusion, bf16[3072,1024]{1,0:T(8,128)(2,1)} %gather_fusion, pred[3072]{0:T(1024)(128)(4,1)S(1)} %compare_and_fusion), kind=kOutput, calls=%fused_computation.33 | convolution fusion | flops 1617166336 | bytes 8920064 | tf_op jit(solution)/shard_map/dot_general | solution.py:76
  84.6 1.5 %collective-permute-start.18 = (bf16[272,256]{1,0:T(8,128)(2,1)S(1)}, bf16[272,256]{1,0:T(8,128)(2,1)S(1)}, u32[]{:S(2)}, u32[]{:S(2)}) collective-permute-start(bf16[272,256]{1,0:T(8,128)(2,1)S(1)} %pad_maximum_fusion.5), channel_id=1, source_target_pairs={{0,6},{2,4},{4,2},{6,0},{8,14},{10,12},{12,10},{14,8},{16,22},{18,... | collective-permute-start | bytes 417800 | tf_op jit(solution)/shard_map/ppermute | solution.py:23
  86.1 1.5 %collective-permute-start.17 = (bf16[272,256]{1,0:T(8,128)(2,1)S(1)}, bf16[272,256]{1,0:T(8,128)(2,1)S(1)}, u32[]{:S(2)}, u32[]{:S(2)}) collective-permute-start(bf16[272,256]{1,0:T(8,128)(2,1)S(1)} %pad_maximum_fusion.4), channel_id=1, source_target_pairs={{0,4},{2,6},{4,0},{6,2},{8,12},{10,14},{12,8},{14,10},{16,20},{18,... | collective-permute-start | bytes 417800 | tf_op jit(solution)/shard_map/ppermute | solution.py:23
  87.6 0.7 collective-permute-start.16
  88.3 3.8 %collective-permute-done.18 = bf16[272,256]{1,0:T(8,128)(2,1)S(1)} collective-permute-done((bf16[272,256]{1,0:T(8,128)(2,1)S(1)}, bf16[272,256]{1,0:T(8,128)(2,1)S(1)}, u32[]{:S(2)}, u32[]{:S(2)}) %collective-permute-start.18) | collective-permute-done | bytes 139296 | tf_op jit(solution)/shard_map/ppermute | solution.py:23
  92.2 2.1 %collective-permute-done.17 = bf16[272,256]{1,0:T(8,128)(2,1)S(1)} collective-permute-done((bf16[272,256]{1,0:T(8,128)(2,1)S(1)}, bf16[272,256]{1,0:T(8,128)(2,1)S(1)}, u32[]{:S(2)}, u32[]{:S(2)}) %collective-permute-start.17) | collective-permute-done | bytes 139296 | tf_op jit(solution)/shard_map/ppermute | solution.py:23
  94.7 1.7 %collective-permute-start.21 = (bf16[272,64]{1,0:T(8,128)(2,1)S(1)}, bf16[272,64]{1,0:T(8,128)(2,1)S(1)}, u32[]{:S(2)}, u32[]{:S(2)}) collective-permute-start(bf16[272,64]{1,0:T(8,128)(2,1)S(1)} %pad_maximum_fusion.12), channel_id=1, source_target_pairs={{0,24},{2,26},{4,28},{6,30},{8,16},{10,18},{12,20},{14,22},{16,8},... | collective-permute-start | bytes 104456 | tf_op jit(solution)/shard_map/ppermute | solution.py:23
  96.6 2.7 %collective-permute-start.19 = (bf16[272,64]{1,0:T(8,128)(2,1)S(1)}, bf16[272,64]{1,0:T(8,128)(2,1)S(1)}, u32[]{:S(2)}, u32[]{:S(2)}) collective-permute-start(bf16[272,64]{1,0:T(8,128)(2,1)S(1)} %pad_maximum_fusion.10), channel_id=1, source_target_pairs={{0,8},{2,10},{4,12},{6,14},{8,0},{10,2},{12,4},{14,6},{16,24},{18,... | collective-permute-start | bytes 104456 | tf_op jit(solution)/shard_map/ppermute | solution.py:23
  99.3 2.3 %collective-permute-done.21 = bf16[272,64]{1,0:T(8,128)(2,1)S(1)} collective-permute-done((bf16[272,64]{1,0:T(8,128)(2,1)S(1)}, bf16[272,64]{1,0:T(8,128)(2,1)S(1)}, u32[]{:S(2)}, u32[]{:S(2)}) %collective-permute-start.21) | collective-permute-done | bytes 34848 | tf_op jit(solution)/shard_map/ppermute | solution.py:23
  101.6 2.0 %collective-permute-done.20 = bf16[272,64]{1,0:T(8,128)(2,1)S(1)} collective-permute-done((bf16[272,64]{1,0:T(8,128)(2,1)S(1)}, bf16[272,64]{1,0:T(8,128)(2,1)S(1)}, u32[]{:S(2)}, u32[]{:S(2)}) %collective-permute-start.20) | collective-permute-done | bytes 34848 | tf_op jit(solution)/shard_map/ppermute | solution.py:23
  104.0 2.4 %collective-permute-start.23 = (bf16[272,64]{1,0:T(8,128)(2,1)S(1)}, bf16[272,64]{1,0:T(8,128)(2,1)S(1)}, u32[]{:S(2)}, u32[]{:S(2)}) collective-permute-start(bf16[272,64]{1,0:T(8,128)(2,1)S(1)} %pad_maximum_fusion.13), channel_id=1, source_target_pairs={{0,16},{2,18},{4,20},{6,22},{8,24},{10,26},{12,28},{14,30},{16,0},... | collective-permute-start | bytes 104456 | tf_op jit(solution)/shard_map/ppermute | solution.py:33
  106.4 1.9 %collective-permute-start.24 = (bf16[272,64]{1,0:T(8,128)(2,1)S(1)}, bf16[272,64]{1,0:T(8,128)(2,1)S(1)}, u32[]{:S(2)}, u32[]{:S(2)}) collective-permute-start(bf16[272,64]{1,0:T(8,128)(2,1)S(1)} %pad_maximum_fusion.13), channel_id=1, source_target_pairs={{0,24},{2,26},{4,28},{6,30},{8,16},{10,18},{12,20},{14,22},{16,8},... | collective-permute-start | bytes 104456 | tf_op jit(solution)/shard_map/ppermute | solution.py:33
  108.4 0.3 dynamic_update_slice.56
  108.7 0.5 collective-permute-done.22
  109.2 1.4 %dynamic_update_slice.57 = bf16[272,256]{1,0:T(8,128)(2,1)S(1)} dynamic-update-slice(bf16[272,256]{1,0:T(8,128)(2,1)S(1)} %dynamic_update_slice.56, bf16[272,64]{1,0:T(8,128)(2,1)} %collective-permute-done.22, s32[]{:T(128)} %constant.120.clone.1, s32[]{:T(128)S(6)} %select_n.75) | dynamic-update-slice | bytes 69636 | tf_op jit(solution)/shard_map/dynamic_update_slice | solution.py:34
  110.6 2.1 %collective-permute-done.23 = bf16[272,64]{1,0:T(8,128)(2,1)S(1)} collective-permute-done((bf16[272,64]{1,0:T(8,128)(2,1)S(1)}, bf16[272,64]{1,0:T(8,128)(2,1)S(1)}, u32[]{:S(2)}, u32[]{:S(2)}) %collective-permute-start.23) | collective-permute-done | bytes 34848 | tf_op jit(solution)/shard_map/ppermute | solution.py:33
  112.8 0.3 dynamic_update_slice.58
  113.0 0.6 dynamic_update_slice.59
  113.6 1.4 %collective-permute-start.25 = (bf16[272,256]{1,0:T(8,128)(2,1)S(1)}, bf16[272,256]{1,0:T(8,128)(2,1)S(1)}, u32[]{:S(2)}, u32[]{:S(2)}) collective-permute-start(bf16[272,256]{1,0:T(8,128)(2,1)S(1)} %dynamic_update_slice.59), channel_id=1, source_target_pairs={{0,2},{2,0},{4,6},{6,4},{8,10},{10,8},{12,14},{14,12},{16,18},{18,... | collective-permute-start | bytes 417800 | tf_op jit(solution)/shard_map/ppermute | solution.py:33
  115.1 0.6 collective-permute-start.26
  115.7 1.5 %collective-permute-start.27 = (bf16[272,256]{1,0:T(8,128)(2,1)S(1)}, bf16[272,256]{1,0:T(8,128)(2,1)S(1)}, u32[]{:S(2)}, u32[]{:S(2)}) collective-permute-start(bf16[272,256]{1,0:T(8,128)(2,1)S(1)} %dynamic_update_slice.59), channel_id=1, source_target_pairs={{0,6},{2,4},{4,2},{6,0},{8,14},{10,12},{12,10},{14,8},{16,22},{18,... | collective-permute-start | bytes 417800 | tf_op jit(solution)/shard_map/ppermute | solution.py:33
  117.3 2.4 %collective-permute-done.25 = bf16[272,256]{1,0:T(8,128)(2,1)S(1)} collective-permute-done((bf16[272,256]{1,0:T(8,128)(2,1)S(1)}, bf16[272,256]{1,0:T(8,128)(2,1)S(1)}, u32[]{:S(2)}, u32[]{:S(2)}) %collective-permute-start.25) | collective-permute-done | bytes 139296 | tf_op jit(solution)/shard_map/ppermute | solution.py:33
  119.7 0.4 collective-permute-done.26
  120.1 1.5 %collective-permute-done.27 = bf16[272,256]{1,0:T(8,128)(2,1)S(1)} collective-permute-done((bf16[272,256]{1,0:T(8,128)(2,1)S(1)}, bf16[272,256]{1,0:T(8,128)(2,1)S(1)}, u32[]{:S(2)}, u32[]{:S(2)}) %collective-permute-start.27) | collective-permute-done | bytes 139296 | tf_op jit(solution)/shard_map/ppermute | solution.py:33
  121.7 4.8 %convolution_convert_fusion = bf16[256,3072]{1,0:T(8,128)(2,1)S(1)} fusion(bf16[272,1024]{1,0:T(8,128)(2,1)S(1)} %constant_dynamic-update-slice_fusion, bf16[3072,1024]{1,0:T(8,128)(2,1)} %gather_fusion, pred[3072]{0:T(1024)(128)(4,1)} %copy-done.8), kind=kOutput, calls=%fused_computation.2 | convolution fusion | flops 1614544896 | bytes 8391680 | tf_op jit(solution)/shard_map/dot_general | solution.py:89
  126.9 0.6 collective-permute-start.28
  127.5 1.5 %collective-permute-done.28 = f32[128]{0:T(128)S(1)} collective-permute-done((f32[128]{0:T(128)S(1)}, f32[128]{0:T(128)S(1)}, u32[]{:S(2)}, u32[]{:S(2)}) %collective-permute-start.28) | collective-permute-done | bytes 544 | tf_op jit(solution)/shard_map/ppermute | solution.py:93
  129.0 2.9 %fusion.4 = (f32[128,3072]{1,0:T(8,128)}, f32[128,3072]{1,0:T(8,128)}) fusion(f32[128,3072]{1,0:T(8,128)S(1)} %get-tuple-element.70, bf16[128,3072]{1,0:T(8,128)(2,1)S(1)} %collective-permute-done.29, bf16[128,3072]{1,0:T(8,128)(2,1)S(1)} %copy-done.4, f32[128,3072]{1,0:T(8,128)S(1)} %copy-done, bf16[256,3072]{1,0:T(8,128)(2,1)S(1)} %convolution_convert_fusion, ...), kind=kLoop, calls=%fused_computation.20 | loop fusion | flops 8650752 | bytes 9454080 | tf_op jit(solution)/shard_map/sub | solution.py:114
  (130 shorter events, 3.4 us)
Async XLA Ops:
  0.6 2.8 %copy-start.6 = (s32[3072]{0:T(1024)S(1)}, s32[3072]{0:T(1024)}, u32[]{:S(2)}) copy-start(s32[3072]{0:T(1024)} %param.15) | copy-start | bytes 36868
  2.9 20.1 %collective-permute-start = (bf16[128,3072]{1,0:T(8,128)(2,1)S(1)}, bf16[128,3072]{1,0:T(8,128)(2,1)S(1)}, u32[]{:S(2)}, u32[]{:S(2)}) collective-permute-start(bf16[128,3072]{1,0:T(8,128)(2,1)S(1)} %select_convert_fusion), channel_id=1, source_target_pairs={{0,1},{1,0},{2,3},{3,2},{4,5},{5,4},{6,7},{7,6},{8,9},{9,8},{10,11... | collective-permute-start | bytes 2359304 | tf_op jit(solution)/shard_map/ppermute | solution.py:73
  3.4 18.7 %copy-start = (f32[128,3072]{1,0:T(8,128)S(1)}, f32[128,3072]{1,0:T(8,128)}, u32[]{:S(2)}) copy-start(f32[128,3072]{1,0:T(8,128)} %param.19) | copy-start | bytes 4718596
  3.4 18.7 %copy-start.5 = (f32[3072]{0:T(1024)S(1)}, f32[3072]{0:T(1024)}, u32[]{:S(2)}) copy-start(f32[3072]{0:T(1024)} %param.17) | copy-start | bytes 36868
  22.2 0.7 copy-start.7
  22.9 56.3 %copy-start.8 = (pred[3072]{0:T(1024)(128)(4,1)}, pred[3072]{0:T(1024)(128)(4,1)S(1)}, u32[]{:S(2)}) copy-start(pred[3072]{0:T(1024)(128)(4,1)S(1)} %compare_and_fusion) | copy-start | bytes 9220
  27.8 8.0 %collective-permute-start.3 = (bf16[272,256]{1,0:T(8,128)(2,1)S(1)}, bf16[272,256]{1,0:T(8,128)(2,1)S(1)}, u32[]{:S(2)}, u32[]{:S(2)}) collective-permute-start(bf16[272,256]{1,0:T(8,128)(2,1)S(1)} %pad_maximum_fusion.2), channel_id=1, source_target_pairs={{0,6},{2,4},{4,2},{6,0},{8,14},{10,12},{12,10},{14,8},{16,22},{18,... | collective-permute-start | bytes 417800 | tf_op jit(solution)/shard_map/ppermute | solution.py:23
  31.4 7.2 %collective-permute-start.2 = (bf16[272,256]{1,0:T(8,128)(2,1)S(1)}, bf16[272,256]{1,0:T(8,128)(2,1)S(1)}, u32[]{:S(2)}, u32[]{:S(2)}) collective-permute-start(bf16[272,256]{1,0:T(8,128)(2,1)S(1)} %pad_maximum_fusion.1), channel_id=1, source_target_pairs={{0,4},{2,6},{4,0},{6,2},{8,12},{10,14},{12,8},{14,10},{16,20},{18,... | collective-permute-start | bytes 417800 | tf_op jit(solution)/shard_map/ppermute | solution.py:23
  32.0 6.9 %collective-permute-start.1 = (bf16[272,256]{1,0:T(8,128)(2,1)S(1)}, bf16[272,256]{1,0:T(8,128)(2,1)S(1)}, u32[]{:S(2)}, u32[]{:S(2)}) collective-permute-start(bf16[272,256]{1,0:T(8,128)(2,1)S(1)} %pad_maximum_fusion), channel_id=1, source_target_pairs={{0,2},{2,0},{4,6},{6,4},{8,10},{10,8},{12,14},{14,12},{16,18},{18,... | collective-permute-start | bytes 417800 | tf_op jit(solution)/shard_map/ppermute | solution.py:23
  39.3 6.4 %collective-permute-start.6 = (bf16[272,64]{1,0:T(8,128)(2,1)S(1)}, bf16[272,64]{1,0:T(8,128)(2,1)S(1)}, u32[]{:S(2)}, u32[]{:S(2)}) collective-permute-start(bf16[272,64]{1,0:T(8,128)(2,1)S(1)} %pad_maximum_fusion.8), channel_id=1, source_target_pairs={{0,24},{2,26},{4,28},{6,30},{8,16},{10,18},{12,20},{14,22},{16,8},... | collective-permute-start | bytes 104456 | tf_op jit(solution)/shard_map/ppermute | solution.py:23
  43.0 6.0 %collective-permute-start.5 = (bf16[272,64]{1,0:T(8,128)(2,1)S(1)}, bf16[272,64]{1,0:T(8,128)(2,1)S(1)}, u32[]{:S(2)}, u32[]{:S(2)}) collective-permute-start(bf16[272,64]{1,0:T(8,128)(2,1)S(1)} %pad_maximum_fusion.7), channel_id=1, source_target_pairs={{0,16},{2,18},{4,20},{6,22},{8,24},{10,26},{12,28},{14,30},{16,0},... | collective-permute-start | bytes 104456 | tf_op jit(solution)/shard_map/ppermute | solution.py:23
  43.1 6.0 %collective-permute-start.4 = (bf16[272,64]{1,0:T(8,128)(2,1)S(1)}, bf16[272,64]{1,0:T(8,128)(2,1)S(1)}, u32[]{:S(2)}, u32[]{:S(2)}) collective-permute-start(bf16[272,64]{1,0:T(8,128)(2,1)S(1)} %pad_maximum_fusion.6), channel_id=1, source_target_pairs={{0,8},{2,10},{4,12},{6,14},{8,0},{10,2},{12,4},{14,6},{16,24},{18,... | collective-permute-start | bytes 104456 | tf_op jit(solution)/shard_map/ppermute | solution.py:23
  49.3 4.8 %collective-permute-start.7 = (bf16[272,64]{1,0:T(8,128)(2,1)S(1)}, bf16[272,64]{1,0:T(8,128)(2,1)S(1)}, u32[]{:S(2)}, u32[]{:S(2)}) collective-permute-start(bf16[272,64]{1,0:T(8,128)(2,1)S(1)} %pad_maximum_fusion.9), channel_id=1, source_target_pairs={{0,8},{2,10},{4,12},{6,14},{8,0},{10,2},{12,4},{14,6},{16,24},{18,... | collective-permute-start | bytes 104456 | tf_op jit(solution)/shard_map/ppermute | solution.py:33
  50.4 6.9 %collective-permute-start.8 = (bf16[272,64]{1,0:T(8,128)(2,1)S(1)}, bf16[272,64]{1,0:T(8,128)(2,1)S(1)}, u32[]{:S(2)}, u32[]{:S(2)}) collective-permute-start(bf16[272,64]{1,0:T(8,128)(2,1)S(1)} %pad_maximum_fusion.9), channel_id=1, source_target_pairs={{0,16},{2,18},{4,20},{6,22},{8,24},{10,26},{12,28},{14,30},{16,0},... | collective-permute-start | bytes 104456 | tf_op jit(solution)/shard_map/ppermute | solution.py:33
  52.5 6.2 %collective-permute-start.9 = (bf16[272,64]{1,0:T(8,128)(2,1)S(1)}, bf16[272,64]{1,0:T(8,128)(2,1)S(1)}, u32[]{:S(2)}, u32[]{:S(2)}) collective-permute-start(bf16[272,64]{1,0:T(8,128)(2,1)S(1)} %pad_maximum_fusion.9), channel_id=1, source_target_pairs={{0,24},{2,26},{4,28},{6,30},{8,16},{10,18},{12,20},{14,22},{16,8},... | collective-permute-start | bytes 104456 | tf_op jit(solution)/shard_map/ppermute | solution.py:33
  59.3 5.9 %collective-permute-start.10 = (bf16[272,256]{1,0:T(8,128)(2,1)S(1)}, bf16[272,256]{1,0:T(8,128)(2,1)S(1)}, u32[]{:S(2)}, u32[]{:S(2)}) collective-permute-start(bf16[272,256]{1,0:T(8,128)(2,1)S(1)} %dynamic_update_slice.51), channel_id=1, source_target_pairs={{0,2},{2,0},{4,6},{6,4},{8,10},{10,8},{12,14},{14,12},{16,18},{18,... | collective-permute-start | bytes 417800 | tf_op jit(solution)/shard_map/ppermute | solution.py:33
  60.9 6.5 %collective-permute-start.11 = (bf16[272,256]{1,0:T(8,128)(2,1)S(1)}, bf16[272,256]{1,0:T(8,128)(2,1)S(1)}, u32[]{:S(2)}, u32[]{:S(2)}) collective-permute-start(bf16[272,256]{1,0:T(8,128)(2,1)S(1)} %dynamic_update_slice.51), channel_id=1, source_target_pairs={{0,4},{2,6},{4,0},{6,2},{8,12},{10,14},{12,8},{14,10},{16,20},{18,... | collective-permute-start | bytes 417800 | tf_op jit(solution)/shard_map/ppermute | solution.py:33
  61.2 6.2 %collective-permute-start.12 = (bf16[272,256]{1,0:T(8,128)(2,1)S(1)}, bf16[272,256]{1,0:T(8,128)(2,1)S(1)}, u32[]{:S(2)}, u32[]{:S(2)}) collective-permute-start(bf16[272,256]{1,0:T(8,128)(2,1)S(1)} %dynamic_update_slice.51), channel_id=1, source_target_pairs={{0,6},{2,4},{4,2},{6,0},{8,14},{10,12},{12,10},{14,8},{16,22},{18,... | collective-permute-start | bytes 417800 | tf_op jit(solution)/shard_map/ppermute | solution.py:33
  72.2 3.4 %copy-start.1 = (bf16[256,3072]{1,0:T(8,128)(2,1)}, bf16[256,3072]{1,0:T(8,128)(2,1)S(1)}, u32[]{:S(2)}) copy-start(bf16[256,3072]{1,0:T(8,128)(2,1)S(1)} %convolution_convert_fusion.1) | copy-start | bytes 4718596
  72.3 2.4 %collective-permute-start.14 = (bf16[128,3072]{1,0:T(8,128)(2,1)S(1)}, bf16[128,3072]{1,0:T(8,128)(2,1)S(1)}, u32[]{:S(2)}, u32[]{:S(2)}) collective-permute-start(bf16[128,3072]{1,0:T(8,128)(2,1)S(1)} %slice.444), channel_id=1, source_target_pairs={{0,1},{1,0},{2,3},{3,2},{4,5},{5,4},{6,7},{7,6},{8,9},{9,8},{10,11... | collective-permute-start | bytes 2359304 | tf_op jit(solution)/shard_map/ppermute | solution.py:94
  72.6 2.0 %collective-permute-start.13 = (f32[128]{0:T(128)S(1)}, f32[128]{0:T(128)S(1)}, u32[]{:S(2)}, u32[]{:S(2)}) collective-permute-start(f32[128]{0:T(128)S(1)} %slice.366), channel_id=1, source_target_pairs={{0,1},{1,0},{2,3},{3,2},{4,5},{5,4},{6,7},{7,6},{8,9},{9,8},{10,11... | collective-permute-start | bytes 1544 | tf_op jit(solution)/shard_map/ppermute | solution.py:93
  74.6 1.0 copy-start.9
  74.6 1.0 copy-start.3
  76.6 2.6 %collective-permute-start.15 = (bf16[128,3072]{1,0:T(8,128)(2,1)}, bf16[128,3072]{1,0:T(8,128)(2,1)}, u32[]{:S(2)}, u32[]{:S(2)}) collective-permute-start(bf16[128,3072]{1,0:T(8,128)(2,1)} %convert_element_type.336), channel_id=1, source_target_pairs={{0,1},{1,0},{2,3},{3,2},{4,5},{5,4},{6,7},{7,6},{8,9},{9,8},{10,11... | collective-permute-start | bytes 2359304 | tf_op jit(solution)/shard_map/ppermute | solution.py:73
  84.6 7.5 %collective-permute-start.18 = (bf16[272,256]{1,0:T(8,128)(2,1)S(1)}, bf16[272,256]{1,0:T(8,128)(2,1)S(1)}, u32[]{:S(2)}, u32[]{:S(2)}) collective-permute-start(bf16[272,256]{1,0:T(8,128)(2,1)S(1)} %pad_maximum_fusion.5), channel_id=1, source_target_pairs={{0,6},{2,4},{4,2},{6,0},{8,14},{10,12},{12,10},{14,8},{16,22},{18,... | collective-permute-start | bytes 417800 | tf_op jit(solution)/shard_map/ppermute | solution.py:23
  86.1 8.2 %collective-permute-start.17 = (bf16[272,256]{1,0:T(8,128)(2,1)S(1)}, bf16[272,256]{1,0:T(8,128)(2,1)S(1)}, u32[]{:S(2)}, u32[]{:S(2)}) collective-permute-start(bf16[272,256]{1,0:T(8,128)(2,1)S(1)} %pad_maximum_fusion.4), channel_id=1, source_target_pairs={{0,4},{2,6},{4,0},{6,2},{8,12},{10,14},{12,8},{14,10},{16,20},{18,... | collective-permute-start | bytes 417800 | tf_op jit(solution)/shard_map/ppermute | solution.py:23
  87.6 6.7 %collective-permute-start.16 = (bf16[272,256]{1,0:T(8,128)(2,1)S(1)}, bf16[272,256]{1,0:T(8,128)(2,1)S(1)}, u32[]{:S(2)}, u32[]{:S(2)}) collective-permute-start(bf16[272,256]{1,0:T(8,128)(2,1)S(1)} %pad_maximum_fusion.3), channel_id=1, source_target_pairs={{0,2},{2,0},{4,6},{6,4},{8,10},{10,8},{12,14},{14,12},{16,18},{18,... | collective-permute-start | bytes 417800 | tf_op jit(solution)/shard_map/ppermute | solution.py:23
  94.7 6.9 %collective-permute-start.21 = (bf16[272,64]{1,0:T(8,128)(2,1)S(1)}, bf16[272,64]{1,0:T(8,128)(2,1)S(1)}, u32[]{:S(2)}, u32[]{:S(2)}) collective-permute-start(bf16[272,64]{1,0:T(8,128)(2,1)S(1)} %pad_maximum_fusion.12), channel_id=1, source_target_pairs={{0,24},{2,26},{4,28},{6,30},{8,16},{10,18},{12,20},{14,22},{16,8},... | collective-permute-start | bytes 104456 | tf_op jit(solution)/shard_map/ppermute | solution.py:23
  96.4 7.2 %collective-permute-start.20 = (bf16[272,64]{1,0:T(8,128)(2,1)S(1)}, bf16[272,64]{1,0:T(8,128)(2,1)S(1)}, u32[]{:S(2)}, u32[]{:S(2)}) collective-permute-start(bf16[272,64]{1,0:T(8,128)(2,1)S(1)} %pad_maximum_fusion.11), channel_id=1, source_target_pairs={{0,16},{2,18},{4,20},{6,22},{8,24},{10,26},{12,28},{14,30},{16,0},... | collective-permute-start | bytes 104456 | tf_op jit(solution)/shard_map/ppermute | solution.py:23
  96.6 7.0 %collective-permute-start.19 = (bf16[272,64]{1,0:T(8,128)(2,1)S(1)}, bf16[272,64]{1,0:T(8,128)(2,1)S(1)}, u32[]{:S(2)}, u32[]{:S(2)}) collective-permute-start(bf16[272,64]{1,0:T(8,128)(2,1)S(1)} %pad_maximum_fusion.10), channel_id=1, source_target_pairs={{0,8},{2,10},{4,12},{6,14},{8,0},{10,2},{12,4},{14,6},{16,24},{18,... | collective-permute-start | bytes 104456 | tf_op jit(solution)/shard_map/ppermute | solution.py:23
  103.9 5.4 %collective-permute-start.22 = (bf16[272,64]{1,0:T(8,128)(2,1)S(1)}, bf16[272,64]{1,0:T(8,128)(2,1)}, u32[]{:S(2)}, u32[]{:S(2)}) collective-permute-start(bf16[272,64]{1,0:T(8,128)(2,1)S(1)} %pad_maximum_fusion.13), channel_id=1, source_target_pairs={{0,8},{2,10},{4,12},{6,14},{8,0},{10,2},{12,4},{14,6},{16,24},{18,... | collective-permute-start | bytes 104456 | tf_op jit(solution)/shard_map/ppermute | solution.py:33
  104.0 8.8 %collective-permute-start.23 = (bf16[272,64]{1,0:T(8,128)(2,1)S(1)}, bf16[272,64]{1,0:T(8,128)(2,1)S(1)}, u32[]{:S(2)}, u32[]{:S(2)}) collective-permute-start(bf16[272,64]{1,0:T(8,128)(2,1)S(1)} %pad_maximum_fusion.13), channel_id=1, source_target_pairs={{0,16},{2,18},{4,20},{6,22},{8,24},{10,26},{12,28},{14,30},{16,0},... | collective-permute-start | bytes 104456 | tf_op jit(solution)/shard_map/ppermute | solution.py:33
  106.4 6.6 %collective-permute-start.24 = (bf16[272,64]{1,0:T(8,128)(2,1)S(1)}, bf16[272,64]{1,0:T(8,128)(2,1)S(1)}, u32[]{:S(2)}, u32[]{:S(2)}) collective-permute-start(bf16[272,64]{1,0:T(8,128)(2,1)S(1)} %pad_maximum_fusion.13), channel_id=1, source_target_pairs={{0,24},{2,26},{4,28},{6,30},{8,16},{10,18},{12,20},{14,22},{16,8},... | collective-permute-start | bytes 104456 | tf_op jit(solution)/shard_map/ppermute | solution.py:33
  113.6 6.0 %collective-permute-start.25 = (bf16[272,256]{1,0:T(8,128)(2,1)S(1)}, bf16[272,256]{1,0:T(8,128)(2,1)S(1)}, u32[]{:S(2)}, u32[]{:S(2)}) collective-permute-start(bf16[272,256]{1,0:T(8,128)(2,1)S(1)} %dynamic_update_slice.59), channel_id=1, source_target_pairs={{0,2},{2,0},{4,6},{6,4},{8,10},{10,8},{12,14},{14,12},{16,18},{18,... | collective-permute-start | bytes 417800 | tf_op jit(solution)/shard_map/ppermute | solution.py:33
  115.1 5.1 %collective-permute-start.26 = (bf16[272,256]{1,0:T(8,128)(2,1)S(1)}, bf16[272,256]{1,0:T(8,128)(2,1)S(1)}, u32[]{:S(2)}, u32[]{:S(2)}) collective-permute-start(bf16[272,256]{1,0:T(8,128)(2,1)S(1)} %dynamic_update_slice.59), channel_id=1, source_target_pairs={{0,4},{2,6},{4,0},{6,2},{8,12},{10,14},{12,8},{14,10},{16,20},{18,... | collective-permute-start | bytes 417800 | tf_op jit(solution)/shard_map/ppermute | solution.py:33
  115.7 6.0 %collective-permute-start.27 = (bf16[272,256]{1,0:T(8,128)(2,1)S(1)}, bf16[272,256]{1,0:T(8,128)(2,1)S(1)}, u32[]{:S(2)}, u32[]{:S(2)}) collective-permute-start(bf16[272,256]{1,0:T(8,128)(2,1)S(1)} %dynamic_update_slice.59), channel_id=1, source_target_pairs={{0,6},{2,4},{4,2},{6,0},{8,14},{10,12},{12,10},{14,8},{16,22},{18,... | collective-permute-start | bytes 417800 | tf_op jit(solution)/shard_map/ppermute | solution.py:33
  121.7 7.3 %copy-start.4 = (bf16[128,3072]{1,0:T(8,128)(2,1)S(1)}, bf16[128,3072]{1,0:T(8,128)(2,1)}, u32[]{:S(2)}) copy-start(bf16[128,3072]{1,0:T(8,128)(2,1)} %copy-done.3) | copy-start | bytes 2359300
  126.5 2.4 %copy-start.10 = (f32[128]{0:T(128)S(1)}, f32[128]{0:T(128)}, u32[]{:S(2)}) copy-start(f32[128]{0:T(128)} %copy-done.9) | copy-start | bytes 1540
  126.5 2.5 %copy-start.2 = (bf16[256,3072]{1,0:T(8,128)(2,1)S(1)}, bf16[256,3072]{1,0:T(8,128)(2,1)}, u32[]{:S(2)}) copy-start(bf16[256,3072]{1,0:T(8,128)(2,1)} %copy-done.1) | copy-start | bytes 4718596
  126.6 2.4 %collective-permute-start.29 = (bf16[128,3072]{1,0:T(8,128)(2,1)S(1)}, bf16[128,3072]{1,0:T(8,128)(2,1)S(1)}, u32[]{:S(2)}, u32[]{:S(2)}) collective-permute-start(bf16[128,3072]{1,0:T(8,128)(2,1)S(1)} %slice.477), channel_id=1, source_target_pairs={{0,1},{1,0},{2,3},{3,2},{4,5},{5,4},{6,7},{7,6},{8,9},{9,8},{10,11... | collective-permute-start | bytes 2359304 | tf_op jit(solution)/shard_map/ppermute | solution.py:94
  126.9 2.0 %collective-permute-start.28 = (f32[128]{0:T(128)S(1)}, f32[128]{0:T(128)S(1)}, u32[]{:S(2)}, u32[]{:S(2)}) collective-permute-start(f32[128]{0:T(128)S(1)} %slice.407), channel_id=1, source_target_pairs={{0,1},{1,0},{2,3},{3,2},{4,5},{5,4},{6,7},{7,6},{8,9},{9,8},{10,11... | collective-permute-start | bytes 1544 | tf_op jit(solution)/shard_map/ppermute | solution.py:93

commit v6 on v5

--- a/solution.py
+++ b/solution.py
@@ -46,7 +46,10 @@
         samples = own * n_eig
         group = eig_table.shape[1]
         filled = jnp.arange(capacity, dtype=jnp.int32) < counts[0]
-        features = jnp.take(eig_table, obs_ids, axis=0)
+        picker = (obs_ids[:, None] == jnp.arange(eig_table.shape[0], dtype=jnp.int32)[None, :]).astype(
+            jnp.bfloat16
+        )
+        features = jnp.dot(picker, eig_table, preferred_element_type=jnp.float32).astype(jnp.bfloat16)
         spectrum = 5.0 * jnp.power(3.0 + eigenvalues, -1.5)
         me_eig = lax.axis_index("eig")
 

time: 132 us -> 131 us (level)
  local copies, waits for them, and re-layouts: 24.4 us -> 6.46 us
  matrix products: 19.4 us -> 36.2 us
    gather x1 -> x0, local copies, waits for them, and re-layouts: 18.7 us -> none  [shards(): features = jnp.take(eig_table, obs_ids, axis=0)]
    dot_general x0 -> x1, matrix products: none -> 17.2 us  [shards(): jnp.dot(picker, eig_table, preferred_element_type=jnp.float32)]
  transfers between devices with their start and end apart: 30 -> 30, of which waited for: 21 -> 21; matrix products, arithmetic and copies ran while one was open for 18% -> 17% of each run, Pallas kernels for 0% -> 0%
where the time goes in v6:
time: 131 us
  waiting for transfers between devices  42.4 us (32%)
  matrix products  36.2 us (28%)
  starting transfers between devices  35.2 us (27%)
  other arithmetic  8.6 us (7%)
  local copies, waits for them, and re-layouts  6.46 us (5%)
  between operations  2.1 us (2%)
    ppermute x12, waiting for transfers between devices, vert_sum(): lax.ppermute(encode(send), 'vert', [(i, i ^ masks[t]) for i in range(n_ve...  21.9 us
    ppermute x12, starting transfers between devices, vert_sum(): lax.ppermute(encode(send), 'vert', [(i, i ^ masks[t]) for i in range(n_ve...  17.2 us
    dot_general x1, matrix products, shards(): jnp.dot(picker, eig_table, preferred_element_type=jnp.float32)  17.2 us
    ppermute x12, starting transfers between devices, vert_sum(): got = lax.ppermute(cur, 'vert', [(i, i ^ masks[t]) for i in range(n_vert)])  16 us
    ppermute x12, waiting for transfers between devices, vert_sum(): got = lax.ppermute(cur, 'vert', [(i, i ^ masks[t]) for i in range(n_vert)])  15.1 us
    dot_general x2, matrix products, operate(): coeff = jnp.dot(rows, features, preferred_element_type=jnp.float32)  9.7 us
    dot_general x2, matrix products, operate(): lax.dot_general(weights, features, (((1,), (1,)), ((), ())), preferred_el...  9.29 us
    dynamic_update_slice x12, local copies, waits for them, and re-layouts, vert_sum(): out = lax.dynamic_update_slice_in_dim(out, got, (digit ^ t) * width, axis=1)  4.13 us
  transfers between devices with their start and end apart: 30, of which 21 were waited for; matrix products, arithmetic and copies ran while one was open for 17% of the time, Pallas kernels for 0%

profile of v6, /device:TPU:0, one launch (start us, length us, event | category | flops | bytes accessed | tf_op | source)
XLA Modules:
  0.0 130.9 jit_solution(14663956806846217402)
XLA Ops:
  1.3 1.5 %select_convert_fusion = bf16[128,3072]{1,0:T(8,128)(2,1)S(1)} fusion(f32[128,3072]{1,0:T(8,128)} %param.19, pred[3072]{0:T(1024)(128)(4,1)S(1)} %iota_compare_fusion.4), kind=kLoop, calls=%fused_computation.37 | loop fusion | flops 393216 | bytes 2362368 | tf_op jit(solution)/shard_map/convert_element_type | solution.py:74
  2.9 0.6 collective-permute-start
  3.4 17.2 %fusion.2 = bf16[3072,1024]{1,0:T(8,128)(2,1)} fusion(bf16[2048,1024]{1,0:T(8,128)(2,1)} %param.14, s32[3072]{0:T(1024)S(1)} %copy-done.9), kind=kOutput, calls=%fused_computation.3 | convolution fusion | flops 12894339072 | bytes 10498048 | tf_op jit(solution)/shard_map/dot_general | solution.py:52
  20.6 0.4 fusion.3
  21.1 0.2 scatter.15
  21.4 4.6 %fusion.19 = f32[256,1024]{1,0:T(8,128)S(1)} fusion(bf16[3072,1024]{1,0:T(8,128)(2,1)} %fusion.2, bf16[128,3072]{1,0:T(8,128)(2,1)S(1)} %collective-permute-done, bf16[128,3072]{1,0:T(8,128)(2,1)S(1)} %select_convert_fusion, f32[1024]{0:T(1024)S(1)} %power_multiply_fusion), kind=kOutput, calls=%fused_computation.36 | convolution fusion | flops 1614020608 | bytes 8916992 | tf_op jit(solution)/shard_map/dot_general | solution.py:79
  26.2 3.6 %collective-permute-start.3 = (bf16[272,256]{1,0:T(8,128)(2,1)S(1)}, bf16[272,256]{1,0:T(8,128)(2,1)S(1)}, u32[]{:S(2)}, u32[]{:S(2)}) collective-permute-start(bf16[272,256]{1,0:T(8,128)(2,1)S(1)} %pad_maximum_fusion.2), channel_id=1, source_target_pairs={{0,6},{2,4},{4,2},{6,0},{8,14},{10,12},{12,10},{14,8},{16,22},{18,... | collective-permute-start | bytes 417800 | tf_op jit(solution)/shard_map/ppermute | solution.py:23
  29.9 0.6 collective-permute-start.2
  30.6 3.6 %collective-permute-done.3 = bf16[272,256]{1,0:T(8,128)(2,1)S(1)} collective-permute-done((bf16[272,256]{1,0:T(8,128)(2,1)S(1)}, bf16[272,256]{1,0:T(8,128)(2,1)S(1)}, u32[]{:S(2)}, u32[]{:S(2)}) %collective-permute-start.3) | collective-permute-done | bytes 139296 | tf_op jit(solution)/shard_map/ppermute | solution.py:23
  34.2 2.8 %collective-permute-done.2 = bf16[272,256]{1,0:T(8,128)(2,1)S(1)} collective-permute-done((bf16[272,256]{1,0:T(8,128)(2,1)S(1)}, bf16[272,256]{1,0:T(8,128)(2,1)S(1)}, u32[]{:S(2)}, u32[]{:S(2)}) %collective-permute-start.2) | collective-permute-done | bytes 139296 | tf_op jit(solution)/shard_map/ppermute | solution.py:23
  37.1 0.2 collective-permute-done.1
  37.7 3.7 %collective-permute-start.6 = (bf16[272,64]{1,0:T(8,128)(2,1)S(1)}, bf16[272,64]{1,0:T(8,128)(2,1)S(1)}, u32[]{:S(2)}, u32[]{:S(2)}) collective-permute-start(bf16[272,64]{1,0:T(8,128)(2,1)S(1)} %pad_maximum_fusion.8), channel_id=1, source_target_pairs={{0,24},{2,26},{4,28},{6,30},{8,16},{10,18},{12,20},{14,22},{16,8},... | collective-permute-start | bytes 104456 | tf_op jit(solution)/shard_map/ppermute | solution.py:23
  41.5 0.8 collective-permute-start.4
  42.4 1.8 %collective-permute-done.6 = bf16[272,64]{1,0:T(8,128)(2,1)S(1)} collective-permute-done((bf16[272,64]{1,0:T(8,128)(2,1)S(1)}, bf16[272,64]{1,0:T(8,128)(2,1)S(1)}, u32[]{:S(2)}, u32[]{:S(2)}) %collective-permute-start.6) | collective-permute-done | bytes 34848 | tf_op jit(solution)/shard_map/ppermute | solution.py:23
  44.2 3.3 %collective-permute-done.5 = bf16[272,64]{1,0:T(8,128)(2,1)S(1)} collective-permute-done((bf16[272,64]{1,0:T(8,128)(2,1)S(1)}, bf16[272,64]{1,0:T(8,128)(2,1)S(1)}, u32[]{:S(2)}, u32[]{:S(2)}) %collective-permute-start.5) | collective-permute-done | bytes 34848 | tf_op jit(solution)/shard_map/ppermute | solution.py:23
  47.7 1.1 collective-permute-start.7
  48.8 2.2 %collective-permute-start.8 = (bf16[272,64]{1,0:T(8,128)(2,1)S(1)}, bf16[272,64]{1,0:T(8,128)(2,1)S(1)}, u32[]{:S(2)}, u32[]{:S(2)}) collective-permute-start(bf16[272,64]{1,0:T(8,128)(2,1)S(1)} %pad_maximum_fusion.9), channel_id=1, source_target_pairs={{0,16},{2,18},{4,20},{6,22},{8,24},{10,26},{12,28},{14,30},{16,0},... | collective-permute-start | bytes 104456 | tf_op jit(solution)/shard_map/ppermute | solution.py:33
  50.9 1.2 collective-permute-start.9
  52.2 0.3 dynamic_update_slice.48
  52.5 0.6 dynamic_update_slice.49
  53.2 2.5 %collective-permute-done.8 = bf16[272,64]{1,0:T(8,128)(2,1)S(1)} collective-permute-done((bf16[272,64]{1,0:T(8,128)(2,1)S(1)}, bf16[272,64]{1,0:T(8,128)(2,1)S(1)}, u32[]{:S(2)}, u32[]{:S(2)}) %collective-permute-start.8) | collective-permute-done | bytes 34848 | tf_op jit(solution)/shard_map/ppermute | solution.py:33
  55.7 0.3 dynamic_update_slice.50
  56.0 1.2 collective-permute-done.9
  57.2 0.7 dynamic_update_slice.51
  57.9 1.5 %collective-permute-start.10 = (bf16[272,256]{1,0:T(8,128)(2,1)S(1)}, bf16[272,256]{1,0:T(8,128)(2,1)S(1)}, u32[]{:S(2)}, u32[]{:S(2)}) collective-permute-start(bf16[272,256]{1,0:T(8,128)(2,1)S(1)} %dynamic_update_slice.51), channel_id=1, source_target_pairs={{0,2},{2,0},{4,6},{6,4},{8,10},{10,8},{12,14},{14,12},{16,18},{18,... | collective-permute-start | bytes 417800 | tf_op jit(solution)/shard_map/ppermute | solution.py:33
  59.4 0.4 collective-permute-start.11
  59.8 1.7 %collective-permute-start.12 = (bf16[272,256]{1,0:T(8,128)(2,1)S(1)}, bf16[272,256]{1,0:T(8,128)(2,1)S(1)}, u32[]{:S(2)}, u32[]{:S(2)}) collective-permute-start(bf16[272,256]{1,0:T(8,128)(2,1)S(1)} %dynamic_update_slice.51), channel_id=1, source_target_pairs={{0,6},{2,4},{4,2},{6,0},{8,14},{10,12},{12,10},{14,8},{16,22},{18,... | collective-permute-start | bytes 417800 | tf_op jit(solution)/shard_map/ppermute | solution.py:33
  61.5 2.2 %collective-permute-done.10 = bf16[272,256]{1,0:T(8,128)(2,1)S(1)} collective-permute-done((bf16[272,256]{1,0:T(8,128)(2,1)S(1)}, bf16[272,256]{1,0:T(8,128)(2,1)S(1)}, u32[]{:S(2)}, u32[]{:S(2)}) %collective-permute-start.10) | collective-permute-done | bytes 139296 | tf_op jit(solution)/shard_map/ppermute | solution.py:33
  63.8 2.2 %collective-permute-done.11 = bf16[272,256]{1,0:T(8,128)(2,1)S(1)} collective-permute-done((bf16[272,256]{1,0:T(8,128)(2,1)S(1)}, bf16[272,256]{1,0:T(8,128)(2,1)S(1)}, u32[]{:S(2)}, u32[]{:S(2)}) %collective-permute-start.11) | collective-permute-done | bytes 139296 | tf_op jit(solution)/shard_map/ppermute | solution.py:33
  66.0 4.6 %convolution_convert_fusion.1 = bf16[256,3072]{1,0:T(8,128)(2,1)S(1)} fusion(bf16[3072,1024]{1,0:T(8,128)(2,1)} %fusion.2, bf16[272,1024]{1,0:T(8,128)(2,1)S(1)} %constant_dynamic-update-slice_fusion.4), kind=kOutput, calls=%fused_computation.5 | convolution fusion | flops 1611399168 | bytes 8388608 | tf_op jit(solution)/shard_map/dot_general | solution.py:92
  71.0 0.6 collective-permute-start.13
  71.6 1.5 %collective-permute-done.13 = f32[128]{0:T(128)S(1)} collective-permute-done((f32[128]{0:T(128)S(1)}, f32[128]{0:T(128)S(1)}, u32[]{:S(2)}, u32[]{:S(2)}) %collective-permute-start.13) | collective-permute-done | bytes 544 | tf_op jit(solution)/shard_map/ppermute | solution.py:96
  73.1 0.5 copy-done.7
  73.6 0.9 fusion.4
  74.6 1.0 convert_element_type.341
  75.9 2.3 %collective-permute-done.15 = bf16[128,3072]{1,0:T(8,128)(2,1)} collective-permute-done((bf16[128,3072]{1,0:T(8,128)(2,1)}, bf16[128,3072]{1,0:T(8,128)(2,1)}, u32[]{:S(2)}, u32[]{:S(2)}) %collective-permute-start.15) | collective-permute-done | bytes 786464 | tf_op jit(solution)/shard_map/ppermute | solution.py:76
  78.2 5.1 %fusion.16 = f32[256,1024]{1,0:T(8,128)S(1)} fusion(bf16[3072,1024]{1,0:T(8,128)(2,1)} %fusion.2, bf16[128,3072]{1,0:T(8,128)(2,1)} %collective-permute-done.15, bf16[128,3072]{1,0:T(8,128)(2,1)} %convert_element_type.341, f32[1024]{0:T(1024)S(1)} %power_multiply_fusion), kind=kOutput, calls=%fused_computation.35 | convolution fusion | flops 1614020608 | bytes 8916992 | tf_op jit(solution)/shard_map/dot_general | solution.py:79
  83.5 1.5 %collective-permute-start.18 = (bf16[272,256]{1,0:T(8,128)(2,1)S(1)}, bf16[272,256]{1,0:T(8,128)(2,1)S(1)}, u32[]{:S(2)}, u32[]{:S(2)}) collective-permute-start(bf16[272,256]{1,0:T(8,128)(2,1)S(1)} %pad_maximum_fusion.5), channel_id=1, source_target_pairs={{0,6},{2,4},{4,2},{6,0},{8,14},{10,12},{12,10},{14,8},{16,22},{18,... | collective-permute-start | bytes 417800 | tf_op jit(solution)/shard_map/ppermute | solution.py:23
  85.0 1.5 %collective-permute-start.17 = (bf16[272,256]{1,0:T(8,128)(2,1)S(1)}, bf16[272,256]{1,0:T(8,128)(2,1)S(1)}, u32[]{:S(2)}, u32[]{:S(2)}) collective-permute-start(bf16[272,256]{1,0:T(8,128)(2,1)S(1)} %pad_maximum_fusion.4), channel_id=1, source_target_pairs={{0,4},{2,6},{4,0},{6,2},{8,12},{10,14},{12,8},{14,10},{16,20},{18,... | collective-permute-start | bytes 417800 | tf_op jit(solution)/shard_map/ppermute | solution.py:23
  86.5 0.7 collective-permute-start.16
  87.2 3.8 %collective-permute-done.18 = bf16[272,256]{1,0:T(8,128)(2,1)S(1)} collective-permute-done((bf16[272,256]{1,0:T(8,128)(2,1)S(1)}, bf16[272,256]{1,0:T(8,128)(2,1)S(1)}, u32[]{:S(2)}, u32[]{:S(2)}) %collective-permute-start.18) | collective-permute-done | bytes 139296 | tf_op jit(solution)/shard_map/ppermute | solution.py:23
  91.0 2.1 %collective-permute-done.17 = bf16[272,256]{1,0:T(8,128)(2,1)S(1)} collective-permute-done((bf16[272,256]{1,0:T(8,128)(2,1)S(1)}, bf16[272,256]{1,0:T(8,128)(2,1)S(1)}, u32[]{:S(2)}, u32[]{:S(2)}) %collective-permute-start.17) | collective-permute-done | bytes 139296 | tf_op jit(solution)/shard_map/ppermute | solution.py:23
  93.6 1.7 %collective-permute-start.21 = (bf16[272,64]{1,0:T(8,128)(2,1)S(1)}, bf16[272,64]{1,0:T(8,128)(2,1)S(1)}, u32[]{:S(2)}, u32[]{:S(2)}) collective-permute-start(bf16[272,64]{1,0:T(8,128)(2,1)S(1)} %pad_maximum_fusion.12), channel_id=1, source_target_pairs={{0,24},{2,26},{4,28},{6,30},{8,16},{10,18},{12,20},{14,22},{16,8},... | collective-permute-start | bytes 104456 | tf_op jit(solution)/shard_map/ppermute | solution.py:23
  95.5 2.7 %collective-permute-start.19 = (bf16[272,64]{1,0:T(8,128)(2,1)S(1)}, bf16[272,64]{1,0:T(8,128)(2,1)S(1)}, u32[]{:S(2)}, u32[]{:S(2)}) collective-permute-start(bf16[272,64]{1,0:T(8,128)(2,1)S(1)} %pad_maximum_fusion.10), channel_id=1, source_target_pairs={{0,8},{2,10},{4,12},{6,14},{8,0},{10,2},{12,4},{14,6},{16,24},{18,... | collective-permute-start | bytes 104456 | tf_op jit(solution)/shard_map/ppermute | solution.py:23
  98.2 2.3 %collective-permute-done.21 = bf16[272,64]{1,0:T(8,128)(2,1)S(1)} collective-permute-done((bf16[272,64]{1,0:T(8,128)(2,1)S(1)}, bf16[272,64]{1,0:T(8,128)(2,1)S(1)}, u32[]{:S(2)}, u32[]{:S(2)}) %collective-permute-start.21) | collective-permute-done | bytes 34848 | tf_op jit(solution)/shard_map/ppermute | solution.py:23
  100.5 2.0 %collective-permute-done.20 = bf16[272,64]{1,0:T(8,128)(2,1)S(1)} collective-permute-done((bf16[272,64]{1,0:T(8,128)(2,1)S(1)}, bf16[272,64]{1,0:T(8,128)(2,1)S(1)}, u32[]{:S(2)}, u32[]{:S(2)}) %collective-permute-start.20) | collective-permute-done | bytes 34848 | tf_op jit(solution)/shard_map/ppermute | solution.py:23
  102.8 2.4 %collective-permute-start.23 = (bf16[272,64]{1,0:T(8,128)(2,1)S(1)}, bf16[272,64]{1,0:T(8,128)(2,1)S(1)}, u32[]{:S(2)}, u32[]{:S(2)}) collective-permute-start(bf16[272,64]{1,0:T(8,128)(2,1)S(1)} %pad_maximum_fusion.13), channel_id=1, source_target_pairs={{0,16},{2,18},{4,20},{6,22},{8,24},{10,26},{12,28},{14,30},{16,0},... | collective-permute-start | bytes 104456 | tf_op jit(solution)/shard_map/ppermute | solution.py:33
  105.3 2.0 %collective-permute-start.24 = (bf16[272,64]{1,0:T(8,128)(2,1)S(1)}, bf16[272,64]{1,0:T(8,128)(2,1)S(1)}, u32[]{:S(2)}, u32[]{:S(2)}) collective-permute-start(bf16[272,64]{1,0:T(8,128)(2,1)S(1)} %pad_maximum_fusion.13), channel_id=1, source_target_pairs={{0,24},{2,26},{4,28},{6,30},{8,16},{10,18},{12,20},{14,22},{16,8},... | collective-permute-start | bytes 104456 | tf_op jit(solution)/shard_map/ppermute | solution.py:33
  107.2 0.3 dynamic_update_slice.56
  107.6 0.5 collective-permute-done.22
  108.1 1.4 %dynamic_update_slice.57 = bf16[272,256]{1,0:T(8,128)(2,1)S(1)} dynamic-update-slice(bf16[272,256]{1,0:T(8,128)(2,1)S(1)} %dynamic_update_slice.56, bf16[272,64]{1,0:T(8,128)(2,1)} %collective-permute-done.22, s32[]{:T(128)} %constant.112.clone.1, s32[]{:T(128)S(6)} %select_n.32) | dynamic-update-slice | bytes 69636 | tf_op jit(solution)/shard_map/dynamic_update_slice | solution.py:34
  109.5 2.1 %collective-permute-done.23 = bf16[272,64]{1,0:T(8,128)(2,1)S(1)} collective-permute-done((bf16[272,64]{1,0:T(8,128)(2,1)S(1)}, bf16[272,64]{1,0:T(8,128)(2,1)S(1)}, u32[]{:S(2)}, u32[]{:S(2)}) %collective-permute-start.23) | collective-permute-done | bytes 34848 | tf_op jit(solution)/shard_map/ppermute | solution.py:33
  111.6 0.3 dynamic_update_slice.58
  111.9 0.8 dynamic_update_slice.59
  112.7 1.4 %collective-permute-start.25 = (bf16[272,256]{1,0:T(8,128)(2,1)S(1)}, bf16[272,256]{1,0:T(8,128)(2,1)S(1)}, u32[]{:S(2)}, u32[]{:S(2)}) collective-permute-start(bf16[272,256]{1,0:T(8,128)(2,1)S(1)} %dynamic_update_slice.59), channel_id=1, source_target_pairs={{0,2},{2,0},{4,6},{6,4},{8,10},{10,8},{12,14},{14,12},{16,18},{18,... | collective-permute-start | bytes 417800 | tf_op jit(solution)/shard_map/ppermute | solution.py:33
  114.2 0.6 collective-permute-start.26
  114.8 1.5 %collective-permute-start.27 = (bf16[272,256]{1,0:T(8,128)(2,1)S(1)}, bf16[272,256]{1,0:T(8,128)(2,1)S(1)}, u32[]{:S(2)}, u32[]{:S(2)}) collective-permute-start(bf16[272,256]{1,0:T(8,128)(2,1)S(1)} %dynamic_update_slice.59), channel_id=1, source_target_pairs={{0,6},{2,4},{4,2},{6,0},{8,14},{10,12},{12,10},{14,8},{16,22},{18,... | collective-permute-start | bytes 417800 | tf_op jit(solution)/shard_map/ppermute | solution.py:33
  116.4 2.4 %collective-permute-done.25 = bf16[272,256]{1,0:T(8,128)(2,1)S(1)} collective-permute-done((bf16[272,256]{1,0:T(8,128)(2,1)S(1)}, bf16[272,256]{1,0:T(8,128)(2,1)S(1)}, u32[]{:S(2)}, u32[]{:S(2)}) %collective-permute-start.25) | collective-permute-done | bytes 139296 | tf_op jit(solution)/shard_map/ppermute | solution.py:33
  118.8 0.4 collective-permute-done.26
  119.2 1.5 %collective-permute-done.27 = bf16[272,256]{1,0:T(8,128)(2,1)S(1)} collective-permute-done((bf16[272,256]{1,0:T(8,128)(2,1)S(1)}, bf16[272,256]{1,0:T(8,128)(2,1)S(1)}, u32[]{:S(2)}, u32[]{:S(2)}) %collective-permute-start.27) | collective-permute-done | bytes 139296 | tf_op jit(solution)/shard_map/ppermute | solution.py:33
  120.8 4.7 %convolution_convert_fusion = bf16[256,3072]{1,0:T(8,128)(2,1)S(1)} fusion(bf16[3072,1024]{1,0:T(8,128)(2,1)} %fusion.2, bf16[272,1024]{1,0:T(8,128)(2,1)S(1)} %constant_dynamic-update-slice_fusion), kind=kOutput, calls=%fused_computation.4 | convolution fusion | flops 1611399168 | bytes 8388608 | tf_op jit(solution)/shard_map/dot_general | solution.py:92
  125.8 0.6 collective-permute-start.28
  126.4 1.5 %collective-permute-done.28 = f32[128]{0:T(128)S(1)} collective-permute-done((f32[128]{0:T(128)S(1)}, f32[128]{0:T(128)S(1)}, u32[]{:S(2)}, u32[]{:S(2)}) %collective-permute-start.28) | collective-permute-done | bytes 544 | tf_op jit(solution)/shard_map/ppermute | solution.py:96
  127.9 2.9 %fusion.7 = (f32[128,3072]{1,0:T(8,128)}, f32[128,3072]{1,0:T(8,128)}) fusion(f32[128,3072]{1,0:T(8,128)S(1)} %get-tuple-element.70, bf16[128,3072]{1,0:T(8,128)(2,1)S(1)} %collective-permute-done.29, bf16[128,3072]{1,0:T(8,128)(2,1)S(1)} %copy-done.4, f32[128,3072]{1,0:T(8,128)S(1)} %copy-done, bf16[256,3072]{1,0:T(8,128)(2,1)S(1)} %convolution_convert_fusion, ...), kind=kLoop, calls=%fused_computation.22 | loop fusion | flops 8650752 | bytes 9454080 | tf_op jit(solution)/shard_map/sub | solution.py:117
  (126 shorter events, 3.5 us)
Async XLA Ops:
  0.6 2.8 %copy-start.9 = (s32[3072]{0:T(1024)S(1)}, s32[3072]{0:T(1024)}, u32[]{:S(2)}) copy-start(s32[3072]{0:T(1024)} %param.15) | copy-start | bytes 36868
  2.9 17.8 %copy-start = (f32[128,3072]{1,0:T(8,128)S(1)}, f32[128,3072]{1,0:T(8,128)}, u32[]{:S(2)}) copy-start(f32[128,3072]{1,0:T(8,128)} %param.19) | copy-start | bytes 4718596
  2.9 17.8 %copy-start.5 = (f32[3072]{0:T(1024)S(1)}, f32[3072]{0:T(1024)}, u32[]{:S(2)}) copy-start(f32[3072]{0:T(1024)} %param.17) | copy-start | bytes 36868
  2.9 18.5 %collective-permute-start = (bf16[128,3072]{1,0:T(8,128)(2,1)S(1)}, bf16[128,3072]{1,0:T(8,128)(2,1)S(1)}, u32[]{:S(2)}, u32[]{:S(2)}) collective-permute-start(bf16[128,3072]{1,0:T(8,128)(2,1)S(1)} %select_convert_fusion), channel_id=1, source_target_pairs={{0,1},{1,0},{2,3},{3,2},{4,5},{5,4},{6,7},{7,6},{8,9},{9,8},{10,11... | collective-permute-start | bytes 2359304 | tf_op jit(solution)/shard_map/ppermute | solution.py:76
  20.6 0.7 copy-start.6
  26.2 8.0 %collective-permute-start.3 = (bf16[272,256]{1,0:T(8,128)(2,1)S(1)}, bf16[272,256]{1,0:T(8,128)(2,1)S(1)}, u32[]{:S(2)}, u32[]{:S(2)}) collective-permute-start(bf16[272,256]{1,0:T(8,128)(2,1)S(1)} %pad_maximum_fusion.2), channel_id=1, source_target_pairs={{0,6},{2,4},{4,2},{6,0},{8,14},{10,12},{12,10},{14,8},{16,22},{18,... | collective-permute-start | bytes 417800 | tf_op jit(solution)/shard_map/ppermute | solution.py:23
  29.9 7.2 %collective-permute-start.2 = (bf16[272,256]{1,0:T(8,128)(2,1)S(1)}, bf16[272,256]{1,0:T(8,128)(2,1)S(1)}, u32[]{:S(2)}, u32[]{:S(2)}) collective-permute-start(bf16[272,256]{1,0:T(8,128)(2,1)S(1)} %pad_maximum_fusion.1), channel_id=1, source_target_pairs={{0,4},{2,6},{4,0},{6,2},{8,12},{10,14},{12,8},{14,10},{16,20},{18,... | collective-permute-start | bytes 417800 | tf_op jit(solution)/shard_map/ppermute | solution.py:23
  30.5 6.9 %collective-permute-start.1 = (bf16[272,256]{1,0:T(8,128)(2,1)S(1)}, bf16[272,256]{1,0:T(8,128)(2,1)S(1)}, u32[]{:S(2)}, u32[]{:S(2)}) collective-permute-start(bf16[272,256]{1,0:T(8,128)(2,1)S(1)} %pad_maximum_fusion), channel_id=1, source_target_pairs={{0,2},{2,0},{4,6},{6,4},{8,10},{10,8},{12,14},{14,12},{16,18},{18,... | collective-permute-start | bytes 417800 | tf_op jit(solution)/shard_map/ppermute | solution.py:23
  37.7 6.4 %collective-permute-start.6 = (bf16[272,64]{1,0:T(8,128)(2,1)S(1)}, bf16[272,64]{1,0:T(8,128)(2,1)S(1)}, u32[]{:S(2)}, u32[]{:S(2)}) collective-permute-start(bf16[272,64]{1,0:T(8,128)(2,1)S(1)} %pad_maximum_fusion.8), channel_id=1, source_target_pairs={{0,24},{2,26},{4,28},{6,30},{8,16},{10,18},{12,20},{14,22},{16,8},... | collective-permute-start | bytes 104456 | tf_op jit(solution)/shard_map/ppermute | solution.py:23
  41.4 6.1 %collective-permute-start.5 = (bf16[272,64]{1,0:T(8,128)(2,1)S(1)}, bf16[272,64]{1,0:T(8,128)(2,1)S(1)}, u32[]{:S(2)}, u32[]{:S(2)}) collective-permute-start(bf16[272,64]{1,0:T(8,128)(2,1)S(1)} %pad_maximum_fusion.7), channel_id=1, source_target_pairs={{0,16},{2,18},{4,20},{6,22},{8,24},{10,26},{12,28},{14,30},{16,0},... | collective-permute-start | bytes 104456 | tf_op jit(solution)/shard_map/ppermute | solution.py:23
  41.5 6.0 %collective-permute-start.4 = (bf16[272,64]{1,0:T(8,128)(2,1)S(1)}, bf16[272,64]{1,0:T(8,128)(2,1)S(1)}, u32[]{:S(2)}, u32[]{:S(2)}) collective-permute-start(bf16[272,64]{1,0:T(8,128)(2,1)S(1)} %pad_maximum_fusion.6), channel_id=1, source_target_pairs={{0,8},{2,10},{4,12},{6,14},{8,0},{10,2},{12,4},{14,6},{16,24},{18,... | collective-permute-start | bytes 104456 | tf_op jit(solution)/shard_map/ppermute | solution.py:23
  47.7 4.8 %collective-permute-start.7 = (bf16[272,64]{1,0:T(8,128)(2,1)S(1)}, bf16[272,64]{1,0:T(8,128)(2,1)S(1)}, u32[]{:S(2)}, u32[]{:S(2)}) collective-permute-start(bf16[272,64]{1,0:T(8,128)(2,1)S(1)} %pad_maximum_fusion.9), channel_id=1, source_target_pairs={{0,8},{2,10},{4,12},{6,14},{8,0},{10,2},{12,4},{14,6},{16,24},{18,... | collective-permute-start | bytes 104456 | tf_op jit(solution)/shard_map/ppermute | solution.py:33
  48.8 6.9 %collective-permute-start.8 = (bf16[272,64]{1,0:T(8,128)(2,1)S(1)}, bf16[272,64]{1,0:T(8,128)(2,1)S(1)}, u32[]{:S(2)}, u32[]{:S(2)}) collective-permute-start(bf16[272,64]{1,0:T(8,128)(2,1)S(1)} %pad_maximum_fusion.9), channel_id=1, source_target_pairs={{0,16},{2,18},{4,20},{6,22},{8,24},{10,26},{12,28},{14,30},{16,0},... | collective-permute-start | bytes 104456 | tf_op jit(solution)/shard_map/ppermute | solution.py:33
  50.9 6.2 %collective-permute-start.9 = (bf16[272,64]{1,0:T(8,128)(2,1)S(1)}, bf16[272,64]{1,0:T(8,128)(2,1)S(1)}, u32[]{:S(2)}, u32[]{:S(2)}) collective-permute-start(bf16[272,64]{1,0:T(8,128)(2,1)S(1)} %pad_maximum_fusion.9), channel_id=1, source_target_pairs={{0,24},{2,26},{4,28},{6,30},{8,16},{10,18},{12,20},{14,22},{16,8},... | collective-permute-start | bytes 104456 | tf_op jit(solution)/shard_map/ppermute | solution.py:33
  57.9 5.9 %collective-permute-start.10 = (bf16[272,256]{1,0:T(8,128)(2,1)S(1)}, bf16[272,256]{1,0:T(8,128)(2,1)S(1)}, u32[]{:S(2)}, u32[]{:S(2)}) collective-permute-start(bf16[272,256]{1,0:T(8,128)(2,1)S(1)} %dynamic_update_slice.51), channel_id=1, source_target_pairs={{0,2},{2,0},{4,6},{6,4},{8,10},{10,8},{12,14},{14,12},{16,18},{18,... | collective-permute-start | bytes 417800 | tf_op jit(solution)/shard_map/ppermute | solution.py:33
  59.4 6.5 %collective-permute-start.11 = (bf16[272,256]{1,0:T(8,128)(2,1)S(1)}, bf16[272,256]{1,0:T(8,128)(2,1)S(1)}, u32[]{:S(2)}, u32[]{:S(2)}) collective-permute-start(bf16[272,256]{1,0:T(8,128)(2,1)S(1)} %dynamic_update_slice.51), channel_id=1, source_target_pairs={{0,4},{2,6},{4,0},{6,2},{8,12},{10,14},{12,8},{14,10},{16,20},{18,... | collective-permute-start | bytes 417800 | tf_op jit(solution)/shard_map/ppermute | solution.py:33
  59.8 6.2 %collective-permute-start.12 = (bf16[272,256]{1,0:T(8,128)(2,1)S(1)}, bf16[272,256]{1,0:T(8,128)(2,1)S(1)}, u32[]{:S(2)}, u32[]{:S(2)}) collective-permute-start(bf16[272,256]{1,0:T(8,128)(2,1)S(1)} %dynamic_update_slice.51), channel_id=1, source_target_pairs={{0,6},{2,4},{4,2},{6,0},{8,14},{10,12},{12,10},{14,8},{16,22},{18,... | collective-permute-start | bytes 417800 | tf_op jit(solution)/shard_map/ppermute | solution.py:33
  70.7 3.9 %copy-start.1 = (bf16[256,3072]{1,0:T(8,128)(2,1)}, bf16[256,3072]{1,0:T(8,128)(2,1)S(1)}, u32[]{:S(2)}) copy-start(bf16[256,3072]{1,0:T(8,128)(2,1)S(1)} %convolution_convert_fusion.1) | copy-start | bytes 4718596
  70.7 2.9 %collective-permute-start.14 = (bf16[128,3072]{1,0:T(8,128)(2,1)S(1)}, bf16[128,3072]{1,0:T(8,128)(2,1)S(1)}, u32[]{:S(2)}, u32[]{:S(2)}) collective-permute-start(bf16[128,3072]{1,0:T(8,128)(2,1)S(1)} %slice.442), channel_id=1, source_target_pairs={{0,1},{1,0},{2,3},{3,2},{4,5},{5,4},{6,7},{7,6},{8,9},{9,8},{10,11... | collective-permute-start | bytes 2359304 | tf_op jit(solution)/shard_map/ppermute | solution.py:97
  71.0 2.0 %collective-permute-start.13 = (f32[128]{0:T(128)S(1)}, f32[128]{0:T(128)S(1)}, u32[]{:S(2)}, u32[]{:S(2)}) collective-permute-start(f32[128]{0:T(128)S(1)} %slice.366), channel_id=1, source_target_pairs={{0,1},{1,0},{2,3},{3,2},{4,5},{5,4},{6,7},{7,6},{8,9},{9,8},{10,11... | collective-permute-start | bytes 1544 | tf_op jit(solution)/shard_map/ppermute | solution.py:96
  73.1 0.5 copy-start.7
  73.6 0.9 copy-start.3
  75.6 2.6 %collective-permute-start.15 = (bf16[128,3072]{1,0:T(8,128)(2,1)}, bf16[128,3072]{1,0:T(8,128)(2,1)}, u32[]{:S(2)}, u32[]{:S(2)}) collective-permute-start(bf16[128,3072]{1,0:T(8,128)(2,1)} %convert_element_type.341), channel_id=1, source_target_pairs={{0,1},{1,0},{2,3},{3,2},{4,5},{5,4},{6,7},{7,6},{8,9},{9,8},{10,11... | collective-permute-start | bytes 2359304 | tf_op jit(solution)/shard_map/ppermute | solution.py:76
  83.5 7.5 %collective-permute-start.18 = (bf16[272,256]{1,0:T(8,128)(2,1)S(1)}, bf16[272,256]{1,0:T(8,128)(2,1)S(1)}, u32[]{:S(2)}, u32[]{:S(2)}) collective-permute-start(bf16[272,256]{1,0:T(8,128)(2,1)S(1)} %pad_maximum_fusion.5), channel_id=1, source_target_pairs={{0,6},{2,4},{4,2},{6,0},{8,14},{10,12},{12,10},{14,8},{16,22},{18,... | collective-permute-start | bytes 417800 | tf_op jit(solution)/shard_map/ppermute | solution.py:23
  85.0 8.1 %collective-permute-start.17 = (bf16[272,256]{1,0:T(8,128)(2,1)S(1)}, bf16[272,256]{1,0:T(8,128)(2,1)S(1)}, u32[]{:S(2)}, u32[]{:S(2)}) collective-permute-start(bf16[272,256]{1,0:T(8,128)(2,1)S(1)} %pad_maximum_fusion.4), channel_id=1, source_target_pairs={{0,4},{2,6},{4,0},{6,2},{8,12},{10,14},{12,8},{14,10},{16,20},{18,... | collective-permute-start | bytes 417800 | tf_op jit(solution)/shard_map/ppermute | solution.py:23
  86.5 6.7 %collective-permute-start.16 = (bf16[272,256]{1,0:T(8,128)(2,1)S(1)}, bf16[272,256]{1,0:T(8,128)(2,1)S(1)}, u32[]{:S(2)}, u32[]{:S(2)}) collective-permute-start(bf16[272,256]{1,0:T(8,128)(2,1)S(1)} %pad_maximum_fusion.3), channel_id=1, source_target_pairs={{0,2},{2,0},{4,6},{6,4},{8,10},{10,8},{12,14},{14,12},{16,18},{18,... | collective-permute-start | bytes 417800 | tf_op jit(solution)/shard_map/ppermute | solution.py:23
  93.6 6.9 %collective-permute-start.21 = (bf16[272,64]{1,0:T(8,128)(2,1)S(1)}, bf16[272,64]{1,0:T(8,128)(2,1)S(1)}, u32[]{:S(2)}, u32[]{:S(2)}) collective-permute-start(bf16[272,64]{1,0:T(8,128)(2,1)S(1)} %pad_maximum_fusion.12), channel_id=1, source_target_pairs={{0,24},{2,26},{4,28},{6,30},{8,16},{10,18},{12,20},{14,22},{16,8},... | collective-permute-start | bytes 104456 | tf_op jit(solution)/shard_map/ppermute | solution.py:23
  95.3 7.2 %collective-permute-start.20 = (bf16[272,64]{1,0:T(8,128)(2,1)S(1)}, bf16[272,64]{1,0:T(8,128)(2,1)S(1)}, u32[]{:S(2)}, u32[]{:S(2)}) collective-permute-start(bf16[272,64]{1,0:T(8,128)(2,1)S(1)} %pad_maximum_fusion.11), channel_id=1, source_target_pairs={{0,16},{2,18},{4,20},{6,22},{8,24},{10,26},{12,28},{14,30},{16,0},... | collective-permute-start | bytes 104456 | tf_op jit(solution)/shard_map/ppermute | solution.py:23
  95.5 7.0 %collective-permute-start.19 = (bf16[272,64]{1,0:T(8,128)(2,1)S(1)}, bf16[272,64]{1,0:T(8,128)(2,1)S(1)}, u32[]{:S(2)}, u32[]{:S(2)}) collective-permute-start(bf16[272,64]{1,0:T(8,128)(2,1)S(1)} %pad_maximum_fusion.10), channel_id=1, source_target_pairs={{0,8},{2,10},{4,12},{6,14},{8,0},{10,2},{12,4},{14,6},{16,24},{18,... | collective-permute-start | bytes 104456 | tf_op jit(solution)/shard_map/ppermute | solution.py:23
  102.8 5.4 %collective-permute-start.22 = (bf16[272,64]{1,0:T(8,128)(2,1)S(1)}, bf16[272,64]{1,0:T(8,128)(2,1)}, u32[]{:S(2)}, u32[]{:S(2)}) collective-permute-start(bf16[272,64]{1,0:T(8,128)(2,1)S(1)} %pad_maximum_fusion.13), channel_id=1, source_target_pairs={{0,8},{2,10},{4,12},{6,14},{8,0},{10,2},{12,4},{14,6},{16,24},{18,... | collective-permute-start | bytes 104456 | tf_op jit(solution)/shard_map/ppermute | solution.py:33
  102.8 8.8 %collective-permute-start.23 = (bf16[272,64]{1,0:T(8,128)(2,1)S(1)}, bf16[272,64]{1,0:T(8,128)(2,1)S(1)}, u32[]{:S(2)}, u32[]{:S(2)}) collective-permute-start(bf16[272,64]{1,0:T(8,128)(2,1)S(1)} %pad_maximum_fusion.13), channel_id=1, source_target_pairs={{0,16},{2,18},{4,20},{6,22},{8,24},{10,26},{12,28},{14,30},{16,0},... | collective-permute-start | bytes 104456 | tf_op jit(solution)/shard_map/ppermute | solution.py:33
  105.3 6.6 %collective-permute-start.24 = (bf16[272,64]{1,0:T(8,128)(2,1)S(1)}, bf16[272,64]{1,0:T(8,128)(2,1)S(1)}, u32[]{:S(2)}, u32[]{:S(2)}) collective-permute-start(bf16[272,64]{1,0:T(8,128)(2,1)S(1)} %pad_maximum_fusion.13), channel_id=1, source_target_pairs={{0,24},{2,26},{4,28},{6,30},{8,16},{10,18},{12,20},{14,22},{16,8},... | collective-permute-start | bytes 104456 | tf_op jit(solution)/shard_map/ppermute | solution.py:33
  112.7 6.0 %collective-permute-start.25 = (bf16[272,256]{1,0:T(8,128)(2,1)S(1)}, bf16[272,256]{1,0:T(8,128)(2,1)S(1)}, u32[]{:S(2)}, u32[]{:S(2)}) collective-permute-start(bf16[272,256]{1,0:T(8,128)(2,1)S(1)} %dynamic_update_slice.59), channel_id=1, source_target_pairs={{0,2},{2,0},{4,6},{6,4},{8,10},{10,8},{12,14},{14,12},{16,18},{18,... | collective-permute-start | bytes 417800 | tf_op jit(solution)/shard_map/ppermute | solution.py:33
  114.2 5.1 %collective-permute-start.26 = (bf16[272,256]{1,0:T(8,128)(2,1)S(1)}, bf16[272,256]{1,0:T(8,128)(2,1)S(1)}, u32[]{:S(2)}, u32[]{:S(2)}) collective-permute-start(bf16[272,256]{1,0:T(8,128)(2,1)S(1)} %dynamic_update_slice.59), channel_id=1, source_target_pairs={{0,4},{2,6},{4,0},{6,2},{8,12},{10,14},{12,8},{14,10},{16,20},{18,... | collective-permute-start | bytes 417800 | tf_op jit(solution)/shard_map/ppermute | solution.py:33
  114.8 6.0 %collective-permute-start.27 = (bf16[272,256]{1,0:T(8,128)(2,1)S(1)}, bf16[272,256]{1,0:T(8,128)(2,1)S(1)}, u32[]{:S(2)}, u32[]{:S(2)}) collective-permute-start(bf16[272,256]{1,0:T(8,128)(2,1)S(1)} %dynamic_update_slice.59), channel_id=1, source_target_pairs={{0,6},{2,4},{4,2},{6,0},{8,14},{10,12},{12,10},{14,8},{16,22},{18,... | collective-permute-start | bytes 417800 | tf_op jit(solution)/shard_map/ppermute | solution.py:33
  120.7 7.2 %copy-start.4 = (bf16[128,3072]{1,0:T(8,128)(2,1)S(1)}, bf16[128,3072]{1,0:T(8,128)(2,1)}, u32[]{:S(2)}) copy-start(bf16[128,3072]{1,0:T(8,128)(2,1)} %copy-done.3) | copy-start | bytes 2359300
  125.4 2.4 %copy-start.8 = (f32[128]{0:T(128)S(1)}, f32[128]{0:T(128)}, u32[]{:S(2)}) copy-start(f32[128]{0:T(128)} %copy-done.7) | copy-start | bytes 1540
  125.5 2.5 %copy-start.2 = (bf16[256,3072]{1,0:T(8,128)(2,1)S(1)}, bf16[256,3072]{1,0:T(8,128)(2,1)}, u32[]{:S(2)}) copy-start(bf16[256,3072]{1,0:T(8,128)(2,1)} %copy-done.1) | copy-start | bytes 4718596
  125.5 2.4 %collective-permute-start.29 = (bf16[128,3072]{1,0:T(8,128)(2,1)S(1)}, bf16[128,3072]{1,0:T(8,128)(2,1)S(1)}, u32[]{:S(2)}, u32[]{:S(2)}) collective-permute-start(bf16[128,3072]{1,0:T(8,128)(2,1)S(1)} %slice.475), channel_id=1, source_target_pairs={{0,1},{1,0},{2,3},{3,2},{4,5},{5,4},{6,7},{7,6},{8,9},{9,8},{10,11... | collective-permute-start | bytes 2359304 | tf_op jit(solution)/shard_map/ppermute | solution.py:97
  125.8 2.0 %collective-permute-start.28 = (f32[128]{0:T(128)S(1)}, f32[128]{0:T(128)S(1)}, u32[]{:S(2)}, u32[]{:S(2)}) collective-permute-start(f32[128]{0:T(128)S(1)} %slice.407), channel_id=1, source_target_pairs={{0,1},{1,0},{2,3},{3,2},{4,5},{5,4},{6,7},{7,6},{8,9},{9,8},{10,11... | collective-permute-start | bytes 1544 | tf_op jit(solution)/shard_map/ppermute | solution.py:96

commit v7 on v6

--- a/solution.py
+++ b/solution.py
@@ -49,7 +49,24 @@
         picker = (obs_ids[:, None] == jnp.arange(eig_table.shape[0], dtype=jnp.int32)[None, :]).astype(
             jnp.bfloat16
         )
-        features = jnp.dot(picker, eig_table, preferred_element_type=jnp.float32).astype(jnp.bfloat16)
+        piece = group // 4
+        features = jnp.concatenate(
+            [
+                jnp.dot(picker, eig_table[:, c * piece : (c + 1) * piece], preferred_element_type=jnp.float32)
+                .astype(jnp.bfloat16)
+                for c in range(4)
+            ],
+            1,
+        )
+
+        def coeff_from_table(rows):
+            summed = jnp.dot(rows, picker, preferred_element_type=jnp.float32)
+            high = summed.astype(jnp.bfloat16)
+            low = (summed - high.astype(jnp.float32)).astype(jnp.bfloat16)
+            both = jnp.dot(
+                jnp.concatenate([high, low], 0), eig_table, preferred_element_type=jnp.float32
+            )
+            return both[: rows.shape[0]] + both[rows.shape[0] :]
         spectrum = 5.0 * jnp.power(3.0 + eigenvalues, -1.5)
         me_eig = lax.axis_index("eig")
 
@@ -70,13 +87,16 @@
                 0,
             )
 
-        def operate(vector):
+        def operate(vector, first=False):
             lowered = vector.astype(jnp.bfloat16)
             if pair:
                 rows = jnp.concatenate([lowered, lax.ppermute(lowered, "eig", swap)], 0)
             else:
                 rows = lax.all_gather(lowered, "eig", axis=0, tiled=True)
-            coeff = jnp.dot(rows, features, preferred_element_type=jnp.float32)
+            if first:
+                coeff = coeff_from_table(rows)
+            else:
+                coeff = jnp.dot(rows, features, preferred_element_type=jnp.float32)
             sums = jnp.zeros((8, group), jnp.float32)
             sums = sums.at[0, :own].set(jnp.sum(vector * vector, axis=1))
             sums = sums.at[1, :own].set(jnp.sum(noise_var[None, :] * vector * vector, axis=1))
@@ -109,7 +129,7 @@
 
         residual = jnp.where(filled[None, :], rhs, jnp.zeros((), jnp.float32))
         solution = jnp.zeros_like(residual)
-        applied, norm_now, product = operate(residual)
+        applied, norm_now, product = operate(residual, first=True)
         step_size = norm_now / product
         direction, along = (residual, applied)
         for iteration in range(ITERS):

time: 131 us -> 143 us (1.092)
  matrix products: 36.2 us -> 50.4 us
  waiting for transfers between devices: 42.4 us -> 39.6 us
    dot_general x1 -> x6, matrix products: 17.2 us -> 37 us  [the longest x4 29.6 us: shards(): jnp.dot(picker, eig_table[:, c * piece:(c + 1) * piece], preferred_elemen...]
    dot_general x2, matrix products: 9.29 us -> 6.2 us  [operate(): lax.dot_general(weights, features, (((1,), (1,)), ((), ())), preferred_el...]
    ppermute x12, waiting for transfers between devices: 15.1 us -> 12.3 us  [vert_sum(): got = lax.ppermute(cur, 'vert', [(i, i ^ masks[t]) for i in range(n_vert)])]
    dot_general x2 -> x1, matrix products: 9.7 us -> 7.16 us  [operate(): coeff = jnp.dot(rows, features, preferred_element_type=jnp.float32)]
  transfers between devices with their start and end apart: 30 -> 30, of which waited for: 21 -> 18; matrix products, arithmetic and copies ran while one was open for 17% -> 24% of each run, Pallas kernels for 0% -> 0%
where the time goes in v7:
time: 143 us
  matrix products  50.4 us (35%)
  waiting for transfers between devices  39.6 us (28%)
  starting transfers between devices  35.1 us (25%)
  other arithmetic  8.72 us (6%)
  local copies, waits for them, and re-layouts  6.65 us (5%)
  between operations  2.35 us (2%)
    dot_general x4, matrix products, shards(): jnp.dot(picker, eig_table[:, c * piece:(c + 1) * piece], preferred_elemen...  29.6 us
    ppermute x12, waiting for transfers between devices, vert_sum(): lax.ppermute(encode(send), 'vert', [(i, i ^ masks[t]) for i in range(n_ve...  22 us
    ppermute x12, starting transfers between devices, vert_sum(): lax.ppermute(encode(send), 'vert', [(i, i ^ masks[t]) for i in range(n_ve...  17.1 us
    ppermute x12, starting transfers between devices, vert_sum(): got = lax.ppermute(cur, 'vert', [(i, i ^ masks[t]) for i in range(n_vert)])  16.1 us
    ppermute x12, waiting for transfers between devices, vert_sum(): got = lax.ppermute(cur, 'vert', [(i, i ^ masks[t]) for i in range(n_vert)])  12.3 us
    dot_general x1, matrix products, operate(): coeff = jnp.dot(rows, features, preferred_element_type=jnp.float32)  7.16 us
    dot_general x2, matrix products, operate(): lax.dot_general(weights, features, (((1,), (1,)), ((), ())), preferred_el...  6.2 us
    dot_general x1, matrix products, coeff_from_table(): summed = jnp.dot(rows, picker, preferred_element_type=jnp.float32)  5.09 us
  transfers between devices with their start and end apart: 30, of which 18 were waited for; matrix products, arithmetic and copies ran while one was open for 24% of the time, Pallas kernels for 0%

profile of v7, /device:TPU:0, one launch (start us, length us, event | category | flops | bytes accessed | tf_op | source)
XLA Modules:
  0.0 142.8 jit_solution(8961955394091718403)
XLA Ops:
  1.5 1.5 %select_convert_fusion = bf16[128,3072]{1,0:T(8,128)(2,1)S(1)} fusion(f32[128,3072]{1,0:T(8,128)} %param.19, pred[3072]{0:T(1024)(128)(4,1)S(1)} %iota_compare_fusion.14), kind=kLoop, calls=%fused_computation.52 | loop fusion | flops 393216 | bytes 2362368 | tf_op jit(solution)/shard_map/convert_element_type | solution.py:91
  3.0 0.6 collective-permute-start
  3.6 0.4 fusion.18
  4.3 8.4 %fusion.10 = bf16[3072,256]{0,1:T(8,128)(2,1)} fusion(s32[3072]{0:T(1024)S(1)} %copy-done.10, bf16[2048,1024]{1,0:T(8,128)(2,1)} %param.14), kind=kOutput, calls=%fused_computation.14 | convolution fusion | flops 3228303360 | bytes 2633728 | tf_op jit(solution)/shard_map/dot_general | solution.py:55
  12.7 7.0 %fusion.11 = bf16[3072,256]{0,1:T(8,128)(2,1)} fusion(s32[3072]{0:T(1024)S(1)} %copy-done.10, bf16[2048,1024]{1,0:T(8,128)(2,1)S(1)} %copy-done.9), kind=kOutput, calls=%fused_computation.15 | convolution fusion | flops 3228303360 | bytes 2633728 | tf_op jit(solution)/shard_map/dot_general | solution.py:55
  19.7 5.1 %subtract_convert_fusion = (bf16[256,2048]{1,0:T(8,128)(2,1)S(1)}, bf16[256,2048]{1,0:T(8,128)(2,1)S(1)}) fusion(s32[3072]{0:T(1024)S(1)} %copy-done.10, bf16[128,3072]{1,0:T(8,128)(2,1)S(1)} %collective-permute-done, bf16[128,3072]{1,0:T(8,128)(2,1)S(1)} %select_convert_fusion), kind=kOutput, calls=%fused_computation.34 | convolution fusion | flops 3232759808 | bytes 3682304 | tf_op jit(solution)/shard_map/dot_general | solution.py:63
  24.8 2.3 %fusion.14 = f32[512,1024]{1,0:T(8,128)S(1)} fusion(bf16[2048,1024]{1,0:T(8,128)(2,1)S(1)} %copy-done.9, bf16[256,2048]{1,0:T(8,128)(2,1)S(1)} %get-tuple-element.85, bf16[256,2048]{1,0:T(8,128)(2,1)S(1)} %get-tuple-element.86), kind=kOutput, calls=%fused_computation.30 | convolution fusion | flops 2151677952 | bytes 8388608 | tf_op jit(solution)/shard_map/dot_general | solution.py:66
  27.4 3.6 %collective-permute-start.3 = (bf16[272,256]{1,0:T(8,128)(2,1)S(1)}, bf16[272,256]{1,0:T(8,128)(2,1)S(1)}, u32[]{:S(2)}, u32[]{:S(2)}) collective-permute-start(bf16[272,256]{1,0:T(8,128)(2,1)S(1)} %pad_maximum_fusion.3), channel_id=1, source_target_pairs={{0,6},{2,4},{4,2},{6,0},{8,14},{10,12},{12,10},{14,8},{16,22},{18,... | collective-permute-start | bytes 417800 | tf_op jit(solution)/shard_map/ppermute | solution.py:23
  31.1 0.6 collective-permute-start.2
  31.8 3.7 %collective-permute-done.3 = bf16[272,256]{1,0:T(8,128)(2,1)S(1)} collective-permute-done((bf16[272,256]{1,0:T(8,128)(2,1)S(1)}, bf16[272,256]{1,0:T(8,128)(2,1)S(1)}, u32[]{:S(2)}, u32[]{:S(2)}) %collective-permute-start.3) | collective-permute-done | bytes 139296 | tf_op jit(solution)/shard_map/ppermute | solution.py:23
  35.5 2.8 %collective-permute-done.2 = bf16[272,256]{1,0:T(8,128)(2,1)S(1)} collective-permute-done((bf16[272,256]{1,0:T(8,128)(2,1)S(1)}, bf16[272,256]{1,0:T(8,128)(2,1)S(1)}, u32[]{:S(2)}, u32[]{:S(2)}) %collective-permute-start.2) | collective-permute-done | bytes 139296 | tf_op jit(solution)/shard_map/ppermute | solution.py:23
  39.0 3.7 %collective-permute-start.6 = (bf16[272,64]{1,0:T(8,128)(2,1)S(1)}, bf16[272,64]{1,0:T(8,128)(2,1)S(1)}, u32[]{:S(2)}, u32[]{:S(2)}) collective-permute-start(bf16[272,64]{1,0:T(8,128)(2,1)S(1)} %pad_maximum_fusion.9), channel_id=1, source_target_pairs={{0,24},{2,26},{4,28},{6,30},{8,16},{10,18},{12,20},{14,22},{16,8},... | collective-permute-start | bytes 104456 | tf_op jit(solution)/shard_map/ppermute | solution.py:23
  42.7 0.8 collective-permute-start.4
  43.6 1.8 %collective-permute-done.6 = bf16[272,64]{1,0:T(8,128)(2,1)S(1)} collective-permute-done((bf16[272,64]{1,0:T(8,128)(2,1)S(1)}, bf16[272,64]{1,0:T(8,128)(2,1)S(1)}, u32[]{:S(2)}, u32[]{:S(2)}) %collective-permute-start.6) | collective-permute-done | bytes 34848 | tf_op jit(solution)/shard_map/ppermute | solution.py:23
  45.4 3.3 %collective-permute-done.5 = bf16[272,64]{1,0:T(8,128)(2,1)S(1)} collective-permute-done((bf16[272,64]{1,0:T(8,128)(2,1)S(1)}, bf16[272,64]{1,0:T(8,128)(2,1)S(1)}, u32[]{:S(2)}, u32[]{:S(2)}) %collective-permute-start.5) | collective-permute-done | bytes 34848 | tf_op jit(solution)/shard_map/ppermute | solution.py:23
  48.9 1.1 collective-permute-start.7
  50.0 2.2 %collective-permute-start.8 = (bf16[272,64]{1,0:T(8,128)(2,1)S(1)}, bf16[272,64]{1,0:T(8,128)(2,1)S(1)}, u32[]{:S(2)}, u32[]{:S(2)}) collective-permute-start(bf16[272,64]{1,0:T(8,128)(2,1)S(1)} %pad_maximum_fusion.10), channel_id=1, source_target_pairs={{0,16},{2,18},{4,20},{6,22},{8,24},{10,26},{12,28},{14,30},{16,0},... | collective-permute-start | bytes 104456 | tf_op jit(solution)/shard_map/ppermute | solution.py:33
  52.2 1.2 collective-permute-start.9
  53.4 7.0 %fusion.12 = bf16[3072,256]{0,1:T(8,128)(2,1)} fusion(s32[3072]{0:T(1024)S(1)} %copy-done.10, bf16[2048,1024]{1,0:T(8,128)(2,1)S(1)} %copy-done.9), kind=kOutput, calls=%fused_computation.16 | convolution fusion | flops 3228303360 | bytes 2633728 | tf_op jit(solution)/shard_map/dot_general | solution.py:55
  60.4 0.3 dynamic_update_slice.48
  60.7 0.6 dynamic_update_slice.49
  61.4 0.3 dynamic_update_slice.50
  61.7 0.8 dynamic_update_slice.51
  62.5 1.6 %collective-permute-start.10 = (bf16[272,256]{1,0:T(8,128)(2,1)S(1)}, bf16[272,256]{1,0:T(8,128)(2,1)S(1)}, u32[]{:S(2)}, u32[]{:S(2)}) collective-permute-start(bf16[272,256]{1,0:T(8,128)(2,1)S(1)} %dynamic_update_slice.51), channel_id=1, source_target_pairs={{0,2},{2,0},{4,6},{6,4},{8,10},{10,8},{12,14},{14,12},{16,18},{18,... | collective-permute-start | bytes 417800 | tf_op jit(solution)/shard_map/ppermute | solution.py:33
  64.0 7.3 %fusion.13 = bf16[3072,256]{0,1:T(8,128)(2,1)S(1)} fusion(s32[3072]{0:T(1024)S(1)} %copy-done.10, bf16[2048,1024]{1,0:T(8,128)(2,1)} %param.14), kind=kOutput, calls=%fused_computation.17 | convolution fusion | flops 3228303360 | bytes 2633728 | tf_op jit(solution)/shard_map/dot_general | solution.py:55
  71.4 0.6 collective-permute-start.11
  72.0 1.5 %collective-permute-start.12 = (bf16[272,256]{1,0:T(8,128)(2,1)S(1)}, bf16[272,256]{1,0:T(8,128)(2,1)S(1)}, u32[]{:S(2)}, u32[]{:S(2)}) collective-permute-start(bf16[272,256]{1,0:T(8,128)(2,1)S(1)} %dynamic_update_slice.51), channel_id=1, source_target_pairs={{0,6},{2,4},{4,2},{6,0},{8,14},{10,12},{12,10},{14,8},{16,22},{18,... | collective-permute-start | bytes 417800 | tf_op jit(solution)/shard_map/ppermute | solution.py:33
  73.6 4.9 %collective-permute-done.11 = bf16[272,256]{1,0:T(8,128)(2,1)S(1)} collective-permute-done((bf16[272,256]{1,0:T(8,128)(2,1)S(1)}, bf16[272,256]{1,0:T(8,128)(2,1)S(1)}, u32[]{:S(2)}, u32[]{:S(2)}) %collective-permute-start.11) | collective-permute-done | bytes 139296 | tf_op jit(solution)/shard_map/ppermute | solution.py:33
  78.6 2.5 %convolution_convert_fusion.1 = bf16[256,3072]{1,0:T(8,128)(2,1)S(1)} fusion(bf16[272,1024]{1,0:T(8,128)(2,1)S(1)} %constant_dynamic-update-slice_fusion.4, bf16[3072,256]{0,1:T(8,128)(2,1)S(1)} %fusion.13, bf16[3072,256]{0,1:T(8,128)(2,1)S(1)} %copy-done.14, bf16[3072,256]{0,1:T(8,128)(2,1)S(1)} %copy-done.13, bf16[3072,256]{0,1:T(8,128)(2,1)S(1)} %copy-done.11), kind=kOutput, calls=%fused_computation.13 | convolution fusion | flops 1636564992 | bytes 8388608 | tf_op jit(solution)/shard_map/dot_general | solution.py:112
  81.4 0.6 collective-permute-start.13
  82.0 1.5 %collective-permute-done.13 = f32[128]{0:T(128)S(1)} collective-permute-done((f32[128]{0:T(128)S(1)}, f32[128]{0:T(128)S(1)}, u32[]{:S(2)}, u32[]{:S(2)}) %collective-permute-start.13) | collective-permute-done | bytes 544 | tf_op jit(solution)/shard_map/ppermute | solution.py:116
  83.5 0.6 copy-done.7
  84.0 0.9 fusion.19
  85.0 1.0 convert_element_type.365
  86.3 2.3 %collective-permute-done.15 = bf16[128,3072]{1,0:T(8,128)(2,1)} collective-permute-done((bf16[128,3072]{1,0:T(8,128)(2,1)}, bf16[128,3072]{1,0:T(8,128)(2,1)}, u32[]{:S(2)}, u32[]{:S(2)}) %collective-permute-start.15) | collective-permute-done | bytes 786464 | tf_op jit(solution)/shard_map/ppermute | solution.py:93
  88.6 7.2 %fusion.30 = f32[256,1024]{1,0:T(8,128)S(1)} fusion(bf16[128,3072]{1,0:T(8,128)(2,1)} %collective-permute-done.15, bf16[128,3072]{1,0:T(8,128)(2,1)} %convert_element_type.365, f32[1024]{0:T(1024)S(1)} %power_multiply_fusion, bf16[3072,256]{0,1:T(8,128)(2,1)} %copy-done.15, bf16[3072,256]{0,1:T(8,128)(2,1)} %fusion.12, bf16[3072,256]{0,1:T(8,128)(2,1)} %fusion.11, ...), kind=kOutput, calls=%fused_computation.51 | convolution fusion | flops 1639186432 | bytes 8916992 | tf_op jit(solution)/shard_map/dot_general | solution.py:99
  95.9 1.5 %collective-permute-start.18 = (bf16[272,256]{1,0:T(8,128)(2,1)S(1)}, bf16[272,256]{1,0:T(8,128)(2,1)S(1)}, u32[]{:S(2)}, u32[]{:S(2)}) collective-permute-start(bf16[272,256]{1,0:T(8,128)(2,1)S(1)} %pad_maximum_fusion.6), channel_id=1, source_target_pairs={{0,6},{2,4},{4,2},{6,0},{8,14},{10,12},{12,10},{14,8},{16,22},{18,... | collective-permute-start | bytes 417800 | tf_op jit(solution)/shard_map/ppermute | solution.py:23
  97.5 1.2 collective-permute-start.17
  98.8 0.9 collective-permute-start.16
  99.7 3.8 %collective-permute-done.18 = bf16[272,256]{1,0:T(8,128)(2,1)S(1)} collective-permute-done((bf16[272,256]{1,0:T(8,128)(2,1)S(1)}, bf16[272,256]{1,0:T(8,128)(2,1)S(1)}, u32[]{:S(2)}, u32[]{:S(2)}) %collective-permute-start.18) | collective-permute-done | bytes 139296 | tf_op jit(solution)/shard_map/ppermute | solution.py:23
  103.5 2.1 %collective-permute-done.17 = bf16[272,256]{1,0:T(8,128)(2,1)S(1)} collective-permute-done((bf16[272,256]{1,0:T(8,128)(2,1)S(1)}, bf16[272,256]{1,0:T(8,128)(2,1)S(1)}, u32[]{:S(2)}, u32[]{:S(2)}) %collective-permute-start.17) | collective-permute-done | bytes 139296 | tf_op jit(solution)/shard_map/ppermute | solution.py:23
  106.1 2.3 %collective-permute-start.21 = (bf16[272,64]{1,0:T(8,128)(2,1)S(1)}, bf16[272,64]{1,0:T(8,128)(2,1)S(1)}, u32[]{:S(2)}, u32[]{:S(2)}) collective-permute-start(bf16[272,64]{1,0:T(8,128)(2,1)S(1)} %pad_maximum_fusion.13), channel_id=1, source_target_pairs={{0,24},{2,26},{4,28},{6,30},{8,16},{10,18},{12,20},{14,22},{16,8},... | collective-permute-start | bytes 104456 | tf_op jit(solution)/shard_map/ppermute | solution.py:23
  108.5 2.2 %collective-permute-start.19 = (bf16[272,64]{1,0:T(8,128)(2,1)S(1)}, bf16[272,64]{1,0:T(8,128)(2,1)S(1)}, u32[]{:S(2)}, u32[]{:S(2)}) collective-permute-start(bf16[272,64]{1,0:T(8,128)(2,1)S(1)} %pad_maximum_fusion.11), channel_id=1, source_target_pairs={{0,8},{2,10},{4,12},{6,14},{8,0},{10,2},{12,4},{14,6},{16,24},{18,... | collective-permute-start | bytes 104456 | tf_op jit(solution)/shard_map/ppermute | solution.py:23
  110.7 2.2 %collective-permute-done.21 = bf16[272,64]{1,0:T(8,128)(2,1)S(1)} collective-permute-done((bf16[272,64]{1,0:T(8,128)(2,1)S(1)}, bf16[272,64]{1,0:T(8,128)(2,1)S(1)}, u32[]{:S(2)}, u32[]{:S(2)}) %collective-permute-start.21) | collective-permute-done | bytes 34848 | tf_op jit(solution)/shard_map/ppermute | solution.py:23
  112.9 2.1 %collective-permute-done.20 = bf16[272,64]{1,0:T(8,128)(2,1)S(1)} collective-permute-done((bf16[272,64]{1,0:T(8,128)(2,1)S(1)}, bf16[272,64]{1,0:T(8,128)(2,1)S(1)}, u32[]{:S(2)}, u32[]{:S(2)}) %collective-permute-start.20) | collective-permute-done | bytes 34848 | tf_op jit(solution)/shard_map/ppermute | solution.py:23
  115.3 0.5 collective-permute-start.22
  115.7 2.4 %collective-permute-start.23 = (bf16[272,64]{1,0:T(8,128)(2,1)S(1)}, bf16[272,64]{1,0:T(8,128)(2,1)S(1)}, u32[]{:S(2)}, u32[]{:S(2)}) collective-permute-start(bf16[272,64]{1,0:T(8,128)(2,1)S(1)} %pad_maximum_fusion.14), channel_id=1, source_target_pairs={{0,16},{2,18},{4,20},{6,22},{8,24},{10,26},{12,28},{14,30},{16,0},... | collective-permute-start | bytes 104456 | tf_op jit(solution)/shard_map/ppermute | solution.py:33
  118.1 1.6 %collective-permute-start.24 = (bf16[272,64]{1,0:T(8,128)(2,1)S(1)}, bf16[272,64]{1,0:T(8,128)(2,1)S(1)}, u32[]{:S(2)}, u32[]{:S(2)}) collective-permute-start(bf16[272,64]{1,0:T(8,128)(2,1)S(1)} %pad_maximum_fusion.14), channel_id=1, source_target_pairs={{0,24},{2,26},{4,28},{6,30},{8,16},{10,18},{12,20},{14,22},{16,8},... | collective-permute-start | bytes 104456 | tf_op jit(solution)/shard_map/ppermute | solution.py:33
  119.7 0.3 dynamic_update_slice.56
  120.1 0.4 collective-permute-done.22
  120.5 1.4 dynamic_update_slice.57
  121.9 2.6 %collective-permute-done.23 = bf16[272,64]{1,0:T(8,128)(2,1)S(1)} collective-permute-done((bf16[272,64]{1,0:T(8,128)(2,1)S(1)}, bf16[272,64]{1,0:T(8,128)(2,1)S(1)}, u32[]{:S(2)}, u32[]{:S(2)}) %collective-permute-start.23) | collective-permute-done | bytes 34848 | tf_op jit(solution)/shard_map/ppermute | solution.py:33
  124.4 0.3 dynamic_update_slice.58
  124.7 0.8 dynamic_update_slice.59
  125.6 1.3 collective-permute-start.25
  126.9 0.9 collective-permute-start.26
  127.7 1.4 collective-permute-start.27
  129.2 1.7 %collective-permute-done.25 = bf16[272,256]{1,0:T(8,128)(2,1)S(1)} collective-permute-done((bf16[272,256]{1,0:T(8,128)(2,1)S(1)}, bf16[272,256]{1,0:T(8,128)(2,1)S(1)}, u32[]{:S(2)}, u32[]{:S(2)}) %collective-permute-start.25) | collective-permute-done | bytes 139296 | tf_op jit(solution)/shard_map/ppermute | solution.py:33
  130.9 1.0 collective-permute-done.26
  131.9 1.7 %collective-permute-done.27 = bf16[272,256]{1,0:T(8,128)(2,1)S(1)} collective-permute-done((bf16[272,256]{1,0:T(8,128)(2,1)S(1)}, bf16[272,256]{1,0:T(8,128)(2,1)S(1)}, u32[]{:S(2)}, u32[]{:S(2)}) %collective-permute-start.27) | collective-permute-done | bytes 139296 | tf_op jit(solution)/shard_map/ppermute | solution.py:33
  133.7 3.7 %convolution_convert_fusion = bf16[256,3072]{1,0:T(8,128)(2,1)S(1)} fusion(bf16[272,1024]{1,0:T(8,128)(2,1)S(1)} %constant_dynamic-update-slice_fusion, bf16[3072,256]{0,1:T(8,128)(2,1)} %copy-done.15, bf16[3072,256]{0,1:T(8,128)(2,1)} %fusion.12, bf16[3072,256]{0,1:T(8,128)(2,1)} %fusion.11, bf16[3072,256]{0,1:T(8,128)(2,1)S(1)} %copy-done.12), kind=kOutput, calls=%fused_computation.12 | convolution fusion | flops 1636564992 | bytes 8388608 | tf_op jit(solution)/shard_map/dot_general | solution.py:112
  137.8 0.6 collective-permute-start.28
  138.4 1.5 %collective-permute-done.28 = f32[128]{0:T(128)S(1)} collective-permute-done((f32[128]{0:T(128)S(1)}, f32[128]{0:T(128)S(1)}, u32[]{:S(2)}, u32[]{:S(2)}) %collective-permute-start.28) | collective-permute-done | bytes 544 | tf_op jit(solution)/shard_map/ppermute | solution.py:116
  139.9 2.9 %fusion.22 = (f32[128,3072]{1,0:T(8,128)}, f32[128,3072]{1,0:T(8,128)}) fusion(f32[128,3072]{1,0:T(8,128)S(1)} %get-tuple-element.70, bf16[128,3072]{1,0:T(8,128)(2,1)S(1)} %collective-permute-done.29, bf16[128,3072]{1,0:T(8,128)(2,1)S(1)} %copy-done.4, f32[128,3072]{1,0:T(8,128)S(1)} %copy-done, bf16[256,3072]{1,0:T(8,128)(2,1)S(1)} %convolution_convert_fusion, ...), kind=kLoop, calls=%fused_computation.39 | loop fusion | flops 8650752 | bytes 9454080 | tf_op jit(solution)/shard_map/sub | solution.py:137
  (143 shorter events, 4.0 us)
Async XLA Ops:
  0.6 2.9 %copy-start = (f32[128,3072]{1,0:T(8,128)S(1)}, f32[128,3072]{1,0:T(8,128)}, u32[]{:S(2)}) copy-start(f32[128,3072]{1,0:T(8,128)} %param.19) | copy-start | bytes 4718596
  0.6 2.9 %copy-start.6 = (f32[1024]{0:T(1024)S(1)}, f32[1024]{0:T(1024)}, u32[]{:S(2)}) copy-start(f32[1024]{0:T(1024)} %param.18) | copy-start | bytes 12292
  0.7 2.9 %copy-start.5 = (f32[3072]{0:T(1024)S(1)}, f32[3072]{0:T(1024)}, u32[]{:S(2)}) copy-start(f32[3072]{0:T(1024)} %param.17) | copy-start | bytes 36868
  1.4 2.9 %copy-start.10 = (s32[3072]{0:T(1024)S(1)}, s32[3072]{0:T(1024)}, u32[]{:S(2)}) copy-start(s32[3072]{0:T(1024)} %param.15) | copy-start | bytes 36868
  3.0 16.7 %collective-permute-start = (bf16[128,3072]{1,0:T(8,128)(2,1)S(1)}, bf16[128,3072]{1,0:T(8,128)(2,1)S(1)}, u32[]{:S(2)}, u32[]{:S(2)}) collective-permute-start(bf16[128,3072]{1,0:T(8,128)(2,1)S(1)} %select_convert_fusion), channel_id=1, source_target_pairs={{0,1},{1,0},{2,3},{3,2},{4,5},{5,4},{6,7},{7,6},{8,9},{9,8},{10,11... | collective-permute-start | bytes 2359304 | tf_op jit(solution)/shard_map/ppermute | solution.py:93
  4.3 8.4 %copy-start.9 = (bf16[2048,1024]{1,0:T(8,128)(2,1)S(1)}, bf16[2048,1024]{1,0:T(8,128)(2,1)}, u32[]{:S(2)}) copy-start(bf16[2048,1024]{1,0:T(8,128)(2,1)} %param.14) | copy-start | bytes 12582916
  27.4 8.0 %collective-permute-start.3 = (bf16[272,256]{1,0:T(8,128)(2,1)S(1)}, bf16[272,256]{1,0:T(8,128)(2,1)S(1)}, u32[]{:S(2)}, u32[]{:S(2)}) collective-permute-start(bf16[272,256]{1,0:T(8,128)(2,1)S(1)} %pad_maximum_fusion.3), channel_id=1, source_target_pairs={{0,6},{2,4},{4,2},{6,0},{8,14},{10,12},{12,10},{14,8},{16,22},{18,... | collective-permute-start | bytes 417800 | tf_op jit(solution)/shard_map/ppermute | solution.py:23
  31.1 7.2 %collective-permute-start.2 = (bf16[272,256]{1,0:T(8,128)(2,1)S(1)}, bf16[272,256]{1,0:T(8,128)(2,1)S(1)}, u32[]{:S(2)}, u32[]{:S(2)}) collective-permute-start(bf16[272,256]{1,0:T(8,128)(2,1)S(1)} %pad_maximum_fusion.2), channel_id=1, source_target_pairs={{0,4},{2,6},{4,0},{6,2},{8,12},{10,14},{12,8},{14,10},{16,20},{18,... | collective-permute-start | bytes 417800 | tf_op jit(solution)/shard_map/ppermute | solution.py:23
  31.6 6.9 %collective-permute-start.1 = (bf16[272,256]{1,0:T(8,128)(2,1)S(1)}, bf16[272,256]{1,0:T(8,128)(2,1)S(1)}, u32[]{:S(2)}, u32[]{:S(2)}) collective-permute-start(bf16[272,256]{1,0:T(8,128)(2,1)S(1)} %pad_maximum_fusion.1), channel_id=1, source_target_pairs={{0,2},{2,0},{4,6},{6,4},{8,10},{10,8},{12,14},{14,12},{16,18},{18,... | collective-permute-start | bytes 417800 | tf_op jit(solution)/shard_map/ppermute | solution.py:23
  39.0 6.4 %collective-permute-start.6 = (bf16[272,64]{1,0:T(8,128)(2,1)S(1)}, bf16[272,64]{1,0:T(8,128)(2,1)S(1)}, u32[]{:S(2)}, u32[]{:S(2)}) collective-permute-start(bf16[272,64]{1,0:T(8,128)(2,1)S(1)} %pad_maximum_fusion.9), channel_id=1, source_target_pairs={{0,24},{2,26},{4,28},{6,30},{8,16},{10,18},{12,20},{14,22},{16,8},... | collective-permute-start | bytes 104456 | tf_op jit(solution)/shard_map/ppermute | solution.py:23
  42.6 6.0 %collective-permute-start.5 = (bf16[272,64]{1,0:T(8,128)(2,1)S(1)}, bf16[272,64]{1,0:T(8,128)(2,1)S(1)}, u32[]{:S(2)}, u32[]{:S(2)}) collective-permute-start(bf16[272,64]{1,0:T(8,128)(2,1)S(1)} %pad_maximum_fusion.8), channel_id=1, source_target_pairs={{0,16},{2,18},{4,20},{6,22},{8,24},{10,26},{12,28},{14,30},{16,0},... | collective-permute-start | bytes 104456 | tf_op jit(solution)/shard_map/ppermute | solution.py:23
  42.7 6.0 %collective-permute-start.4 = (bf16[272,64]{1,0:T(8,128)(2,1)S(1)}, bf16[272,64]{1,0:T(8,128)(2,1)S(1)}, u32[]{:S(2)}, u32[]{:S(2)}) collective-permute-start(bf16[272,64]{1,0:T(8,128)(2,1)S(1)} %pad_maximum_fusion.7), channel_id=1, source_target_pairs={{0,8},{2,10},{4,12},{6,14},{8,0},{10,2},{12,4},{14,6},{16,24},{18,... | collective-permute-start | bytes 104456 | tf_op jit(solution)/shard_map/ppermute | solution.py:23
  48.9 11.8 %collective-permute-start.7 = (bf16[272,64]{1,0:T(8,128)(2,1)S(1)}, bf16[272,64]{1,0:T(8,128)(2,1)S(1)}, u32[]{:S(2)}, u32[]{:S(2)}) collective-permute-start(bf16[272,64]{1,0:T(8,128)(2,1)S(1)} %pad_maximum_fusion.10), channel_id=1, source_target_pairs={{0,8},{2,10},{4,12},{6,14},{8,0},{10,2},{12,4},{14,6},{16,24},{18,... | collective-permute-start | bytes 104456 | tf_op jit(solution)/shard_map/ppermute | solution.py:33
  50.0 11.4 %collective-permute-start.8 = (bf16[272,64]{1,0:T(8,128)(2,1)S(1)}, bf16[272,64]{1,0:T(8,128)(2,1)S(1)}, u32[]{:S(2)}, u32[]{:S(2)}) collective-permute-start(bf16[272,64]{1,0:T(8,128)(2,1)S(1)} %pad_maximum_fusion.10), channel_id=1, source_target_pairs={{0,16},{2,18},{4,20},{6,22},{8,24},{10,26},{12,28},{14,30},{16,0},... | collective-permute-start | bytes 104456 | tf_op jit(solution)/shard_map/ppermute | solution.py:33
  52.2 9.5 %collective-permute-start.9 = (bf16[272,64]{1,0:T(8,128)(2,1)S(1)}, bf16[272,64]{1,0:T(8,128)(2,1)S(1)}, u32[]{:S(2)}, u32[]{:S(2)}) collective-permute-start(bf16[272,64]{1,0:T(8,128)(2,1)S(1)} %pad_maximum_fusion.10), channel_id=1, source_target_pairs={{0,24},{2,26},{4,28},{6,30},{8,16},{10,18},{12,20},{14,22},{16,8},... | collective-permute-start | bytes 104456 | tf_op jit(solution)/shard_map/ppermute | solution.py:33
  62.5 11.1 %collective-permute-start.10 = (bf16[272,256]{1,0:T(8,128)(2,1)S(1)}, bf16[272,256]{1,0:T(8,128)(2,1)S(1)}, u32[]{:S(2)}, u32[]{:S(2)}) collective-permute-start(bf16[272,256]{1,0:T(8,128)(2,1)S(1)} %dynamic_update_slice.51), channel_id=1, source_target_pairs={{0,2},{2,0},{4,6},{6,4},{8,10},{10,8},{12,14},{14,12},{16,18},{18,... | collective-permute-start | bytes 417800 | tf_op jit(solution)/shard_map/ppermute | solution.py:33
  64.0 14.5 %copy-start.13 = (bf16[3072,256]{0,1:T(8,128)(2,1)S(1)}, bf16[3072,256]{0,1:T(8,128)(2,1)}, u32[]{:S(2)}) copy-start(bf16[3072,256]{0,1:T(8,128)(2,1)} %fusion.11) | copy-start | bytes 4718596
  64.0 14.5 %copy-start.14 = (bf16[3072,256]{0,1:T(8,128)(2,1)S(1)}, bf16[3072,256]{0,1:T(8,128)(2,1)}, u32[]{:S(2)}) copy-start(bf16[3072,256]{0,1:T(8,128)(2,1)} %fusion.12) | copy-start | bytes 4718596
  71.4 9.6 %copy-start.15 = (bf16[3072,256]{0,1:T(8,128)(2,1)}, bf16[3072,256]{0,1:T(8,128)(2,1)S(1)}, u32[]{:S(2)}) copy-start(bf16[3072,256]{0,1:T(8,128)(2,1)S(1)} %fusion.13) | copy-start | bytes 4718596
  71.4 7.2 %copy-start.11 = (bf16[3072,256]{0,1:T(8,128)(2,1)S(1)}, bf16[3072,256]{0,1:T(8,128)(2,1)}, u32[]{:S(2)}) copy-start(bf16[3072,256]{0,1:T(8,128)(2,1)} %fusion.10) | copy-start | bytes 4718596
  71.4 7.1 %collective-permute-start.11 = (bf16[272,256]{1,0:T(8,128)(2,1)S(1)}, bf16[272,256]{1,0:T(8,128)(2,1)S(1)}, u32[]{:S(2)}, u32[]{:S(2)}) collective-permute-start(bf16[272,256]{1,0:T(8,128)(2,1)S(1)} %dynamic_update_slice.51), channel_id=1, source_target_pairs={{0,4},{2,6},{4,0},{6,2},{8,12},{10,14},{12,8},{14,10},{16,20},{18,... | collective-permute-start | bytes 417800 | tf_op jit(solution)/shard_map/ppermute | solution.py:33
  72.0 6.5 %collective-permute-start.12 = (bf16[272,256]{1,0:T(8,128)(2,1)S(1)}, bf16[272,256]{1,0:T(8,128)(2,1)S(1)}, u32[]{:S(2)}, u32[]{:S(2)}) collective-permute-start(bf16[272,256]{1,0:T(8,128)(2,1)S(1)} %dynamic_update_slice.51), channel_id=1, source_target_pairs={{0,6},{2,4},{4,2},{6,0},{8,14},{10,12},{12,10},{14,8},{16,22},{18,... | collective-permute-start | bytes 417800 | tf_op jit(solution)/shard_map/ppermute | solution.py:33
  81.0 3.9 %copy-start.1 = (bf16[256,3072]{1,0:T(8,128)(2,1)}, bf16[256,3072]{1,0:T(8,128)(2,1)S(1)}, u32[]{:S(2)}) copy-start(bf16[256,3072]{1,0:T(8,128)(2,1)S(1)} %convolution_convert_fusion.1) | copy-start | bytes 4718596
  81.1 2.9 %collective-permute-start.14 = (bf16[128,3072]{1,0:T(8,128)(2,1)S(1)}, bf16[128,3072]{1,0:T(8,128)(2,1)S(1)}, u32[]{:S(2)}, u32[]{:S(2)}) collective-permute-start(bf16[128,3072]{1,0:T(8,128)(2,1)S(1)} %slice.468), channel_id=1, source_target_pairs={{0,1},{1,0},{2,3},{3,2},{4,5},{5,4},{6,7},{7,6},{8,9},{9,8},{10,11... | collective-permute-start | bytes 2359304 | tf_op jit(solution)/shard_map/ppermute | solution.py:117
  81.4 2.0 %collective-permute-start.13 = (f32[128]{0:T(128)S(1)}, f32[128]{0:T(128)S(1)}, u32[]{:S(2)}, u32[]{:S(2)}) collective-permute-start(f32[128]{0:T(128)S(1)} %slice.386), channel_id=1, source_target_pairs={{0,1},{1,0},{2,3},{3,2},{4,5},{5,4},{6,7},{7,6},{8,9},{9,8},{10,11... | collective-permute-start | bytes 1544 | tf_op jit(solution)/shard_map/ppermute | solution.py:116
  83.5 0.6 copy-start.7
  84.0 0.9 copy-start.3
  86.0 2.6 %collective-permute-start.15 = (bf16[128,3072]{1,0:T(8,128)(2,1)}, bf16[128,3072]{1,0:T(8,128)(2,1)}, u32[]{:S(2)}, u32[]{:S(2)}) collective-permute-start(bf16[128,3072]{1,0:T(8,128)(2,1)} %convert_element_type.365), channel_id=1, source_target_pairs={{0,1},{1,0},{2,3},{3,2},{4,5},{5,4},{6,7},{7,6},{8,9},{9,8},{10,11... | collective-permute-start | bytes 2359304 | tf_op jit(solution)/shard_map/ppermute | solution.py:93
  95.9 7.5 %collective-permute-start.18 = (bf16[272,256]{1,0:T(8,128)(2,1)S(1)}, bf16[272,256]{1,0:T(8,128)(2,1)S(1)}, u32[]{:S(2)}, u32[]{:S(2)}) collective-permute-start(bf16[272,256]{1,0:T(8,128)(2,1)S(1)} %pad_maximum_fusion.6), channel_id=1, source_target_pairs={{0,6},{2,4},{4,2},{6,0},{8,14},{10,12},{12,10},{14,8},{16,22},{18,... | collective-permute-start | bytes 417800 | tf_op jit(solution)/shard_map/ppermute | solution.py:23
  97.5 8.1 %collective-permute-start.17 = (bf16[272,256]{1,0:T(8,128)(2,1)S(1)}, bf16[272,256]{1,0:T(8,128)(2,1)S(1)}, u32[]{:S(2)}, u32[]{:S(2)}) collective-permute-start(bf16[272,256]{1,0:T(8,128)(2,1)S(1)} %pad_maximum_fusion.5), channel_id=1, source_target_pairs={{0,4},{2,6},{4,0},{6,2},{8,12},{10,14},{12,8},{14,10},{16,20},{18,... | collective-permute-start | bytes 417800 | tf_op jit(solution)/shard_map/ppermute | solution.py:23
  98.8 6.9 %collective-permute-start.16 = (bf16[272,256]{1,0:T(8,128)(2,1)S(1)}, bf16[272,256]{1,0:T(8,128)(2,1)S(1)}, u32[]{:S(2)}, u32[]{:S(2)}) collective-permute-start(bf16[272,256]{1,0:T(8,128)(2,1)S(1)} %pad_maximum_fusion.4), channel_id=1, source_target_pairs={{0,2},{2,0},{4,6},{6,4},{8,10},{10,8},{12,14},{14,12},{16,18},{18,... | collective-permute-start | bytes 417800 | tf_op jit(solution)/shard_map/ppermute | solution.py:23
  106.1 6.8 %collective-permute-start.21 = (bf16[272,64]{1,0:T(8,128)(2,1)S(1)}, bf16[272,64]{1,0:T(8,128)(2,1)S(1)}, u32[]{:S(2)}, u32[]{:S(2)}) collective-permute-start(bf16[272,64]{1,0:T(8,128)(2,1)S(1)} %pad_maximum_fusion.13), channel_id=1, source_target_pairs={{0,24},{2,26},{4,28},{6,30},{8,16},{10,18},{12,20},{14,22},{16,8},... | collective-permute-start | bytes 104456 | tf_op jit(solution)/shard_map/ppermute | solution.py:23
  108.4 6.6 %collective-permute-start.20 = (bf16[272,64]{1,0:T(8,128)(2,1)S(1)}, bf16[272,64]{1,0:T(8,128)(2,1)S(1)}, u32[]{:S(2)}, u32[]{:S(2)}) collective-permute-start(bf16[272,64]{1,0:T(8,128)(2,1)S(1)} %pad_maximum_fusion.12), channel_id=1, source_target_pairs={{0,16},{2,18},{4,20},{6,22},{8,24},{10,26},{12,28},{14,30},{16,0},... | collective-permute-start | bytes 104456 | tf_op jit(solution)/shard_map/ppermute | solution.py:23
  108.5 6.6 %collective-permute-start.19 = (bf16[272,64]{1,0:T(8,128)(2,1)S(1)}, bf16[272,64]{1,0:T(8,128)(2,1)S(1)}, u32[]{:S(2)}, u32[]{:S(2)}) collective-permute-start(bf16[272,64]{1,0:T(8,128)(2,1)S(1)} %pad_maximum_fusion.11), channel_id=1, source_target_pairs={{0,8},{2,10},{4,12},{6,14},{8,0},{10,2},{12,4},{14,6},{16,24},{18,... | collective-permute-start | bytes 104456 | tf_op jit(solution)/shard_map/ppermute | solution.py:23
  115.3 5.2 %collective-permute-start.22 = (bf16[272,64]{1,0:T(8,128)(2,1)S(1)}, bf16[272,64]{1,0:T(8,128)(2,1)}, u32[]{:S(2)}, u32[]{:S(2)}) collective-permute-start(bf16[272,64]{1,0:T(8,128)(2,1)S(1)} %pad_maximum_fusion.14), channel_id=1, source_target_pairs={{0,8},{2,10},{4,12},{6,14},{8,0},{10,2},{12,4},{14,6},{16,24},{18,... | collective-permute-start | bytes 104456 | tf_op jit(solution)/shard_map/ppermute | solution.py:33
  115.7 8.7 %collective-permute-start.23 = (bf16[272,64]{1,0:T(8,128)(2,1)S(1)}, bf16[272,64]{1,0:T(8,128)(2,1)S(1)}, u32[]{:S(2)}, u32[]{:S(2)}) collective-permute-start(bf16[272,64]{1,0:T(8,128)(2,1)S(1)} %pad_maximum_fusion.14), channel_id=1, source_target_pairs={{0,16},{2,18},{4,20},{6,22},{8,24},{10,26},{12,28},{14,30},{16,0},... | collective-permute-start | bytes 104456 | tf_op jit(solution)/shard_map/ppermute | solution.py:33
  118.1 6.6 %collective-permute-start.24 = (bf16[272,64]{1,0:T(8,128)(2,1)S(1)}, bf16[272,64]{1,0:T(8,128)(2,1)S(1)}, u32[]{:S(2)}, u32[]{:S(2)}) collective-permute-start(bf16[272,64]{1,0:T(8,128)(2,1)S(1)} %pad_maximum_fusion.14), channel_id=1, source_target_pairs={{0,24},{2,26},{4,28},{6,30},{8,16},{10,18},{12,20},{14,22},{16,8},... | collective-permute-start | bytes 104456 | tf_op jit(solution)/shard_map/ppermute | solution.py:33
  125.6 8.1 %copy-start.12 = (bf16[3072,256]{0,1:T(8,128)(2,1)S(1)}, bf16[3072,256]{0,1:T(8,128)(2,1)}, u32[]{:S(2)}) copy-start(bf16[3072,256]{0,1:T(8,128)(2,1)} %fusion.10) | copy-start | bytes 4718596
  125.6 5.3 %collective-permute-start.25 = (bf16[272,256]{1,0:T(8,128)(2,1)S(1)}, bf16[272,256]{1,0:T(8,128)(2,1)S(1)}, u32[]{:S(2)}, u32[]{:S(2)}) collective-permute-start(bf16[272,256]{1,0:T(8,128)(2,1)S(1)} %dynamic_update_slice.59), channel_id=1, source_target_pairs={{0,2},{2,0},{4,6},{6,4},{8,10},{10,8},{12,14},{14,12},{16,18},{18,... | collective-permute-start | bytes 417800 | tf_op jit(solution)/shard_map/ppermute | solution.py:33
  126.9 5.1 %collective-permute-start.26 = (bf16[272,256]{1,0:T(8,128)(2,1)S(1)}, bf16[272,256]{1,0:T(8,128)(2,1)S(1)}, u32[]{:S(2)}, u32[]{:S(2)}) collective-permute-start(bf16[272,256]{1,0:T(8,128)(2,1)S(1)} %dynamic_update_slice.59), channel_id=1, source_target_pairs={{0,4},{2,6},{4,0},{6,2},{8,12},{10,14},{12,8},{14,10},{16,20},{18,... | collective-permute-start | bytes 417800 | tf_op jit(solution)/shard_map/ppermute | solution.py:33
  127.7 6.0 %collective-permute-start.27 = (bf16[272,256]{1,0:T(8,128)(2,1)S(1)}, bf16[272,256]{1,0:T(8,128)(2,1)S(1)}, u32[]{:S(2)}, u32[]{:S(2)}) collective-permute-start(bf16[272,256]{1,0:T(8,128)(2,1)S(1)} %dynamic_update_slice.59), channel_id=1, source_target_pairs={{0,6},{2,4},{4,2},{6,0},{8,14},{10,12},{12,10},{14,8},{16,22},{18,... | collective-permute-start | bytes 417800 | tf_op jit(solution)/shard_map/ppermute | solution.py:33
  133.7 6.2 %copy-start.4 = (bf16[128,3072]{1,0:T(8,128)(2,1)S(1)}, bf16[128,3072]{1,0:T(8,128)(2,1)}, u32[]{:S(2)}) copy-start(bf16[128,3072]{1,0:T(8,128)(2,1)} %copy-done.3) | copy-start | bytes 2359300
  137.5 2.4 %copy-start.8 = (f32[128]{0:T(128)S(1)}, f32[128]{0:T(128)}, u32[]{:S(2)}) copy-start(f32[128]{0:T(128)} %copy-done.7) | copy-start | bytes 1540
  137.5 2.5 %copy-start.2 = (bf16[256,3072]{1,0:T(8,128)(2,1)S(1)}, bf16[256,3072]{1,0:T(8,128)(2,1)}, u32[]{:S(2)}) copy-start(bf16[256,3072]{1,0:T(8,128)(2,1)} %copy-done.1) | copy-start | bytes 4718596
  137.5 2.4 %collective-permute-start.29 = (bf16[128,3072]{1,0:T(8,128)(2,1)S(1)}, bf16[128,3072]{1,0:T(8,128)(2,1)S(1)}, u32[]{:S(2)}, u32[]{:S(2)}) collective-permute-start(bf16[128,3072]{1,0:T(8,128)(2,1)S(1)} %slice.501), channel_id=1, source_target_pairs={{0,1},{1,0},{2,3},{3,2},{4,5},{5,4},{6,7},{7,6},{8,9},{9,8},{10,11... | collective-permute-start | bytes 2359304 | tf_op jit(solution)/shard_map/ppermute | solution.py:117
  137.8 2.0 %collective-permute-start.28 = (f32[128]{0:T(128)S(1)}, f32[128]{0:T(128)S(1)}, u32[]{:S(2)}, u32[]{:S(2)}) collective-permute-start(f32[128]{0:T(128)S(1)} %slice.431), channel_id=1, source_target_pairs={{0,1},{1,0},{2,3},{3,2},{4,5},{5,4},{6,7},{7,6},{8,9},{9,8},{10,11... | collective-permute-start | bytes 1544 | tf_op jit(solution)/shard_map/ppermute | solution.py:116

commit v8 on v7

--- a/solution.py
+++ b/solution.py
@@ -49,15 +49,7 @@
         picker = (obs_ids[:, None] == jnp.arange(eig_table.shape[0], dtype=jnp.int32)[None, :]).astype(
             jnp.bfloat16
         )
-        piece = group // 4
-        features = jnp.concatenate(
-            [
-                jnp.dot(picker, eig_table[:, c * piece : (c + 1) * piece], preferred_element_type=jnp.float32)
-                .astype(jnp.bfloat16)
-                for c in range(4)
-            ],
-            1,
-        )
+        features = jnp.dot(picker, eig_table, preferred_element_type=jnp.float32).astype(jnp.bfloat16)
 
         def coeff_from_table(rows):
             summed = jnp.dot(rows, picker, preferred_element_type=jnp.float32)

time: 143 us -> 132 us (0.923)
  matrix products: 50.4 us -> 35.7 us
  waiting for transfers between devices: 39.6 us -> 43.3 us
    dot_general x4 -> x1, matrix products: 29.6 us -> 16.7 us  [shards(): jnp.dot(picker, eig_table, preferred_element_type=jnp.float32)]
    ppermute x12, waiting for transfers between devices: 12.3 us -> 15.1 us  [vert_sum(): got = lax.ppermute(cur, 'vert', [(i, i ^ masks[t]) for i in range(n_vert)])]
    dot_general x1, matrix products: 7.16 us -> 5.07 us  [operate(): coeff = jnp.dot(rows, features, preferred_element_type=jnp.float32)]
  transfers between devices with their start and end apart: 30 -> 30, of which waited for: 18 -> 21; matrix products, arithmetic and copies ran while one was open for 24% -> 17% of each run, Pallas kernels for 0% -> 0%
where the time goes in v8:
time: 132 us; the launch traced here: 131 us
  waiting for transfers between devices  43.3 us (33%)
  matrix products  35.7 us (27%)
  starting transfers between devices  35.4 us (27%)
  other arithmetic  8.73 us (7%)
  local copies, waits for them, and re-layouts  6.04 us (5%)
  between operations  2.27 us (2%)
    ppermute x12, waiting for transfers between devices, vert_sum(): lax.ppermute(encode(send), 'vert', [(i, i ^ masks[t]) for i in range(n_ve...  21.7 us
    ppermute x12, starting transfers between devices, vert_sum(): lax.ppermute(encode(send), 'vert', [(i, i ^ masks[t]) for i in range(n_ve...  17.4 us
    dot_general x1, matrix products, shards(): jnp.dot(picker, eig_table, preferred_element_type=jnp.float32)  16.7 us
    ppermute x12, starting transfers between devices, vert_sum(): got = lax.ppermute(cur, 'vert', [(i, i ^ masks[t]) for i in range(n_vert)])  16.1 us
    ppermute x12, waiting for transfers between devices, vert_sum(): got = lax.ppermute(cur, 'vert', [(i, i ^ masks[t]) for i in range(n_vert)])  15.1 us
    dot_general x2, matrix products, operate(): lax.dot_general(weights, features, (((1,), (1,)), ((), ())), preferred_el...  6.52 us
    dot_general x1, matrix products, coeff_from_table(): summed = jnp.dot(rows, picker, preferred_element_type=jnp.float32)  5.09 us
    dot_general x1, matrix products, operate(): coeff = jnp.dot(rows, features, preferred_element_type=jnp.float32)  5.07 us
  transfers between devices with their start and end apart: 30, of which 21 were waited for; matrix products, arithmetic and copies ran while one was open for 17% of the time, Pallas kernels for 0%

profile of v8, /device:TPU:0, one launch (start us, length us, event | category | flops | bytes accessed | tf_op | source)
XLA Modules:
  0.0 131.5 jit_solution(4609651444579358707)
XLA Ops:
  1.5 1.5 %select_convert_fusion = bf16[128,3072]{1,0:T(8,128)(2,1)S(1)} fusion(f32[128,3072]{1,0:T(8,128)} %param.19, pred[3072]{0:T(1024)(128)(4,1)S(1)} %iota_compare_fusion.5), kind=kLoop, calls=%fused_computation.42 | loop fusion | flops 393216 | bytes 2362368 | tf_op jit(solution)/shard_map/convert_element_type | solution.py:83
  3.0 0.6 collective-permute-start
  3.6 0.4 fusion.9
  4.3 1.2 collective-permute-done
  5.5 5.1 %subtract_convert_fusion = (bf16[256,2048]{1,0:T(8,128)(2,1)S(1)}, bf16[256,2048]{1,0:T(8,128)(2,1)S(1)}) fusion(s32[3072]{0:T(1024)S(1)} %copy-done.10, bf16[128,3072]{1,0:T(8,128)(2,1)S(1)} %collective-permute-done, bf16[128,3072]{1,0:T(8,128)(2,1)S(1)} %select_convert_fusion), kind=kOutput, calls=%fused_computation.24 | convolution fusion | flops 3232759808 | bytes 3682304 | tf_op jit(solution)/shard_map/dot_general | solution.py:55
  10.6 2.3 %fusion.5 = f32[512,1024]{1,0:T(8,128)S(1)} fusion(bf16[2048,1024]{1,0:T(8,128)(2,1)S(1)} %copy-done.9, bf16[256,2048]{1,0:T(8,128)(2,1)S(1)} %get-tuple-element.85, bf16[256,2048]{1,0:T(8,128)(2,1)S(1)} %get-tuple-element.86), kind=kOutput, calls=%fused_computation.20 | convolution fusion | flops 2151677952 | bytes 8388608 | tf_op jit(solution)/shard_map/dot_general | solution.py:58
  13.3 3.9 %collective-permute-start.3 = (bf16[272,256]{1,0:T(8,128)(2,1)S(1)}, bf16[272,256]{1,0:T(8,128)(2,1)S(1)}, u32[]{:S(2)}, u32[]{:S(2)}) collective-permute-start(bf16[272,256]{1,0:T(8,128)(2,1)S(1)} %pad_maximum_fusion.2), channel_id=1, source_target_pairs={{0,6},{2,4},{4,2},{6,0},{8,14},{10,12},{12,10},{14,8},{16,22},{18,... | collective-permute-start | bytes 417800 | tf_op jit(solution)/shard_map/ppermute | solution.py:23
  17.2 0.6 collective-permute-start.2
  17.9 3.4 %collective-permute-done.3 = bf16[272,256]{1,0:T(8,128)(2,1)S(1)} collective-permute-done((bf16[272,256]{1,0:T(8,128)(2,1)S(1)}, bf16[272,256]{1,0:T(8,128)(2,1)S(1)}, u32[]{:S(2)}, u32[]{:S(2)}) %collective-permute-start.3) | collective-permute-done | bytes 139296 | tf_op jit(solution)/shard_map/ppermute | solution.py:23
  21.3 2.8 %collective-permute-done.2 = bf16[272,256]{1,0:T(8,128)(2,1)S(1)} collective-permute-done((bf16[272,256]{1,0:T(8,128)(2,1)S(1)}, bf16[272,256]{1,0:T(8,128)(2,1)S(1)}, u32[]{:S(2)}, u32[]{:S(2)}) %collective-permute-start.2) | collective-permute-done | bytes 139296 | tf_op jit(solution)/shard_map/ppermute | solution.py:23
  24.1 0.2 collective-permute-done.1
  24.8 3.7 %collective-permute-start.6 = (bf16[272,64]{1,0:T(8,128)(2,1)S(1)}, bf16[272,64]{1,0:T(8,128)(2,1)S(1)}, u32[]{:S(2)}, u32[]{:S(2)}) collective-permute-start(bf16[272,64]{1,0:T(8,128)(2,1)S(1)} %pad_maximum_fusion.8), channel_id=1, source_target_pairs={{0,24},{2,26},{4,28},{6,30},{8,16},{10,18},{12,20},{14,22},{16,8},... | collective-permute-start | bytes 104456 | tf_op jit(solution)/shard_map/ppermute | solution.py:23
  28.6 0.8 collective-permute-start.4
  29.4 1.8 %collective-permute-done.6 = bf16[272,64]{1,0:T(8,128)(2,1)S(1)} collective-permute-done((bf16[272,64]{1,0:T(8,128)(2,1)S(1)}, bf16[272,64]{1,0:T(8,128)(2,1)S(1)}, u32[]{:S(2)}, u32[]{:S(2)}) %collective-permute-start.6) | collective-permute-done | bytes 34848 | tf_op jit(solution)/shard_map/ppermute | solution.py:23
  31.2 3.3 %collective-permute-done.5 = bf16[272,64]{1,0:T(8,128)(2,1)S(1)} collective-permute-done((bf16[272,64]{1,0:T(8,128)(2,1)S(1)}, bf16[272,64]{1,0:T(8,128)(2,1)S(1)}, u32[]{:S(2)}, u32[]{:S(2)}) %collective-permute-start.5) | collective-permute-done | bytes 34848 | tf_op jit(solution)/shard_map/ppermute | solution.py:23
  34.7 1.1 collective-permute-start.7
  35.8 2.2 %collective-permute-start.8 = (bf16[272,64]{1,0:T(8,128)(2,1)S(1)}, bf16[272,64]{1,0:T(8,128)(2,1)S(1)}, u32[]{:S(2)}, u32[]{:S(2)}) collective-permute-start(bf16[272,64]{1,0:T(8,128)(2,1)S(1)} %pad_maximum_fusion.9), channel_id=1, source_target_pairs={{0,16},{2,18},{4,20},{6,22},{8,24},{10,26},{12,28},{14,30},{16,0},... | collective-permute-start | bytes 104456 | tf_op jit(solution)/shard_map/ppermute | solution.py:33
  38.0 1.2 collective-permute-start.9
  39.2 0.3 dynamic_update_slice.48
  39.6 0.6 dynamic_update_slice.49
  40.2 2.5 %collective-permute-done.8 = bf16[272,64]{1,0:T(8,128)(2,1)S(1)} collective-permute-done((bf16[272,64]{1,0:T(8,128)(2,1)S(1)}, bf16[272,64]{1,0:T(8,128)(2,1)S(1)}, u32[]{:S(2)}, u32[]{:S(2)}) %collective-permute-start.8) | collective-permute-done | bytes 34848 | tf_op jit(solution)/shard_map/ppermute | solution.py:33
  42.7 0.3 dynamic_update_slice.50
  43.0 1.2 collective-permute-done.9
  44.2 0.5 dynamic_update_slice.51
  44.8 1.5 %collective-permute-start.10 = (bf16[272,256]{1,0:T(8,128)(2,1)S(1)}, bf16[272,256]{1,0:T(8,128)(2,1)S(1)}, u32[]{:S(2)}, u32[]{:S(2)}) collective-permute-start(bf16[272,256]{1,0:T(8,128)(2,1)S(1)} %dynamic_update_slice.51), channel_id=1, source_target_pairs={{0,2},{2,0},{4,6},{6,4},{8,10},{10,8},{12,14},{14,12},{16,18},{18,... | collective-permute-start | bytes 417800 | tf_op jit(solution)/shard_map/ppermute | solution.py:33
  46.3 16.7 %fusion.4 = bf16[3072,1024]{1,0:T(8,128)(2,1)S(1)} fusion(bf16[2048,1024]{1,0:T(8,128)(2,1)} %param.14, s32[3072]{0:T(1024)S(1)} %copy-done.10), kind=kOutput, calls=%fused_computation.5 | convolution fusion | flops 12894339072 | bytes 10498048 | tf_op jit(solution)/shard_map/dot_general | solution.py:52
  63.0 0.4 collective-permute-start.11
  63.5 1.7 %collective-permute-start.12 = (bf16[272,256]{1,0:T(8,128)(2,1)S(1)}, bf16[272,256]{1,0:T(8,128)(2,1)S(1)}, u32[]{:S(2)}, u32[]{:S(2)}) collective-permute-start(bf16[272,256]{1,0:T(8,128)(2,1)S(1)} %dynamic_update_slice.51), channel_id=1, source_target_pairs={{0,6},{2,4},{4,2},{6,0},{8,14},{10,12},{12,10},{14,8},{16,22},{18,... | collective-permute-start | bytes 417800 | tf_op jit(solution)/shard_map/ppermute | solution.py:33
  65.2 4.4 %collective-permute-done.11 = bf16[272,256]{1,0:T(8,128)(2,1)S(1)} collective-permute-done((bf16[272,256]{1,0:T(8,128)(2,1)S(1)}, bf16[272,256]{1,0:T(8,128)(2,1)S(1)}, u32[]{:S(2)}, u32[]{:S(2)}) %collective-permute-start.11) | collective-permute-done | bytes 139296 | tf_op jit(solution)/shard_map/ppermute | solution.py:33
  69.7 1.8 %convolution_convert_fusion.1 = bf16[256,3072]{1,0:T(8,128)(2,1)S(1)} fusion(bf16[3072,1024]{1,0:T(8,128)(2,1)S(1)} %fusion.4, bf16[272,1024]{1,0:T(8,128)(2,1)S(1)} %constant_dynamic-update-slice_fusion.4), kind=kOutput, calls=%fused_computation.7 | convolution fusion | flops 1611399168 | bytes 8388608 | tf_op jit(solution)/shard_map/dot_general | solution.py:104
  71.9 0.6 collective-permute-start.13
  72.5 1.5 %collective-permute-done.13 = f32[128]{0:T(128)S(1)} collective-permute-done((f32[128]{0:T(128)S(1)}, f32[128]{0:T(128)S(1)}, u32[]{:S(2)}, u32[]{:S(2)}) %collective-permute-start.13) | collective-permute-done | bytes 544 | tf_op jit(solution)/shard_map/ppermute | solution.py:108
  74.0 0.5 copy-done.7
  74.5 0.9 fusion.10
  75.5 1.0 convert_element_type.353
  76.7 2.3 %collective-permute-done.15 = bf16[128,3072]{1,0:T(8,128)(2,1)} collective-permute-done((bf16[128,3072]{1,0:T(8,128)(2,1)}, bf16[128,3072]{1,0:T(8,128)(2,1)}, u32[]{:S(2)}, u32[]{:S(2)}) %collective-permute-start.15) | collective-permute-done | bytes 786464 | tf_op jit(solution)/shard_map/ppermute | solution.py:85
  79.1 5.1 %fusion.21 = f32[256,1024]{1,0:T(8,128)S(1)} fusion(bf16[3072,1024]{1,0:T(8,128)(2,1)} %copy-done.11, bf16[128,3072]{1,0:T(8,128)(2,1)} %collective-permute-done.15, bf16[128,3072]{1,0:T(8,128)(2,1)} %convert_element_type.353, f32[1024]{0:T(1024)S(1)} %power_multiply_fusion), kind=kOutput, calls=%fused_computation.41 | convolution fusion | flops 1614020608 | bytes 8916992 | tf_op jit(solution)/shard_map/dot_general | solution.py:91
  84.3 1.5 %collective-permute-start.18 = (bf16[272,256]{1,0:T(8,128)(2,1)S(1)}, bf16[272,256]{1,0:T(8,128)(2,1)S(1)}, u32[]{:S(2)}, u32[]{:S(2)}) collective-permute-start(bf16[272,256]{1,0:T(8,128)(2,1)S(1)} %pad_maximum_fusion.5), channel_id=1, source_target_pairs={{0,6},{2,4},{4,2},{6,0},{8,14},{10,12},{12,10},{14,8},{16,22},{18,... | collective-permute-start | bytes 417800 | tf_op jit(solution)/shard_map/ppermute | solution.py:23
  85.9 1.5 %collective-permute-start.17 = (bf16[272,256]{1,0:T(8,128)(2,1)S(1)}, bf16[272,256]{1,0:T(8,128)(2,1)S(1)}, u32[]{:S(2)}, u32[]{:S(2)}) collective-permute-start(bf16[272,256]{1,0:T(8,128)(2,1)S(1)} %pad_maximum_fusion.4), channel_id=1, source_target_pairs={{0,4},{2,6},{4,0},{6,2},{8,12},{10,14},{12,8},{14,10},{16,20},{18,... | collective-permute-start | bytes 417800 | tf_op jit(solution)/shard_map/ppermute | solution.py:23
  87.4 0.7 collective-permute-start.16
  88.1 3.8 %collective-permute-done.18 = bf16[272,256]{1,0:T(8,128)(2,1)S(1)} collective-permute-done((bf16[272,256]{1,0:T(8,128)(2,1)S(1)}, bf16[272,256]{1,0:T(8,128)(2,1)S(1)}, u32[]{:S(2)}, u32[]{:S(2)}) %collective-permute-start.18) | collective-permute-done | bytes 139296 | tf_op jit(solution)/shard_map/ppermute | solution.py:23
  91.9 2.1 %collective-permute-done.17 = bf16[272,256]{1,0:T(8,128)(2,1)S(1)} collective-permute-done((bf16[272,256]{1,0:T(8,128)(2,1)S(1)}, bf16[272,256]{1,0:T(8,128)(2,1)S(1)}, u32[]{:S(2)}, u32[]{:S(2)}) %collective-permute-start.17) | collective-permute-done | bytes 139296 | tf_op jit(solution)/shard_map/ppermute | solution.py:23
  94.4 1.7 %collective-permute-start.21 = (bf16[272,64]{1,0:T(8,128)(2,1)S(1)}, bf16[272,64]{1,0:T(8,128)(2,1)S(1)}, u32[]{:S(2)}, u32[]{:S(2)}) collective-permute-start(bf16[272,64]{1,0:T(8,128)(2,1)S(1)} %pad_maximum_fusion.12), channel_id=1, source_target_pairs={{0,24},{2,26},{4,28},{6,30},{8,16},{10,18},{12,20},{14,22},{16,8},... | collective-permute-start | bytes 104456 | tf_op jit(solution)/shard_map/ppermute | solution.py:23
  96.2 2.8 %collective-permute-start.19 = (bf16[272,64]{1,0:T(8,128)(2,1)S(1)}, bf16[272,64]{1,0:T(8,128)(2,1)S(1)}, u32[]{:S(2)}, u32[]{:S(2)}) collective-permute-start(bf16[272,64]{1,0:T(8,128)(2,1)S(1)} %pad_maximum_fusion.10), channel_id=1, source_target_pairs={{0,8},{2,10},{4,12},{6,14},{8,0},{10,2},{12,4},{14,6},{16,24},{18,... | collective-permute-start | bytes 104456 | tf_op jit(solution)/shard_map/ppermute | solution.py:23
  99.1 2.3 %collective-permute-done.21 = bf16[272,64]{1,0:T(8,128)(2,1)S(1)} collective-permute-done((bf16[272,64]{1,0:T(8,128)(2,1)S(1)}, bf16[272,64]{1,0:T(8,128)(2,1)S(1)}, u32[]{:S(2)}, u32[]{:S(2)}) %collective-permute-start.21) | collective-permute-done | bytes 34848 | tf_op jit(solution)/shard_map/ppermute | solution.py:23
  101.4 2.0 %collective-permute-done.20 = bf16[272,64]{1,0:T(8,128)(2,1)S(1)} collective-permute-done((bf16[272,64]{1,0:T(8,128)(2,1)S(1)}, bf16[272,64]{1,0:T(8,128)(2,1)S(1)}, u32[]{:S(2)}, u32[]{:S(2)}) %collective-permute-start.20) | collective-permute-done | bytes 34848 | tf_op jit(solution)/shard_map/ppermute | solution.py:23
  103.7 2.4 %collective-permute-start.23 = (bf16[272,64]{1,0:T(8,128)(2,1)S(1)}, bf16[272,64]{1,0:T(8,128)(2,1)S(1)}, u32[]{:S(2)}, u32[]{:S(2)}) collective-permute-start(bf16[272,64]{1,0:T(8,128)(2,1)S(1)} %pad_maximum_fusion.13), channel_id=1, source_target_pairs={{0,16},{2,18},{4,20},{6,22},{8,24},{10,26},{12,28},{14,30},{16,0},... | collective-permute-start | bytes 104456 | tf_op jit(solution)/shard_map/ppermute | solution.py:33
  106.1 2.0 %collective-permute-start.24 = (bf16[272,64]{1,0:T(8,128)(2,1)S(1)}, bf16[272,64]{1,0:T(8,128)(2,1)S(1)}, u32[]{:S(2)}, u32[]{:S(2)}) collective-permute-start(bf16[272,64]{1,0:T(8,128)(2,1)S(1)} %pad_maximum_fusion.13), channel_id=1, source_target_pairs={{0,24},{2,26},{4,28},{6,30},{8,16},{10,18},{12,20},{14,22},{16,8},... | collective-permute-start | bytes 104456 | tf_op jit(solution)/shard_map/ppermute | solution.py:33
  108.1 0.3 dynamic_update_slice.56
  108.5 0.5 collective-permute-done.22
  109.0 1.4 %dynamic_update_slice.57 = bf16[272,256]{1,0:T(8,128)(2,1)S(1)} dynamic-update-slice(bf16[272,256]{1,0:T(8,128)(2,1)S(1)} %dynamic_update_slice.56, bf16[272,64]{1,0:T(8,128)(2,1)} %collective-permute-done.22, s32[]{:T(128)} %constant.112.clone.1, s32[]{:T(128)S(6)} %select_n.32) | dynamic-update-slice | bytes 69636 | tf_op jit(solution)/shard_map/dynamic_update_slice | solution.py:34
  110.4 2.1 %collective-permute-done.23 = bf16[272,64]{1,0:T(8,128)(2,1)S(1)} collective-permute-done((bf16[272,64]{1,0:T(8,128)(2,1)S(1)}, bf16[272,64]{1,0:T(8,128)(2,1)S(1)}, u32[]{:S(2)}, u32[]{:S(2)}) %collective-permute-start.23) | collective-permute-done | bytes 34848 | tf_op jit(solution)/shard_map/ppermute | solution.py:33
  112.5 0.3 dynamic_update_slice.58
  112.8 0.6 dynamic_update_slice.59
  113.4 1.5 %collective-permute-start.25 = (bf16[272,256]{1,0:T(8,128)(2,1)S(1)}, bf16[272,256]{1,0:T(8,128)(2,1)S(1)}, u32[]{:S(2)}, u32[]{:S(2)}) collective-permute-start(bf16[272,256]{1,0:T(8,128)(2,1)S(1)} %dynamic_update_slice.59), channel_id=1, source_target_pairs={{0,2},{2,0},{4,6},{6,4},{8,10},{10,8},{12,14},{14,12},{16,18},{18,... | collective-permute-start | bytes 417800 | tf_op jit(solution)/shard_map/ppermute | solution.py:33
  114.8 0.6 collective-permute-start.26
  115.4 1.5 %collective-permute-start.27 = (bf16[272,256]{1,0:T(8,128)(2,1)S(1)}, bf16[272,256]{1,0:T(8,128)(2,1)S(1)}, u32[]{:S(2)}, u32[]{:S(2)}) collective-permute-start(bf16[272,256]{1,0:T(8,128)(2,1)S(1)} %dynamic_update_slice.59), channel_id=1, source_target_pairs={{0,6},{2,4},{4,2},{6,0},{8,14},{10,12},{12,10},{14,8},{16,22},{18,... | collective-permute-start | bytes 417800 | tf_op jit(solution)/shard_map/ppermute | solution.py:33
  117.0 2.4 %collective-permute-done.25 = bf16[272,256]{1,0:T(8,128)(2,1)S(1)} collective-permute-done((bf16[272,256]{1,0:T(8,128)(2,1)S(1)}, bf16[272,256]{1,0:T(8,128)(2,1)S(1)}, u32[]{:S(2)}, u32[]{:S(2)}) %collective-permute-start.25) | collective-permute-done | bytes 139296 | tf_op jit(solution)/shard_map/ppermute | solution.py:33
  119.5 0.4 collective-permute-done.26
  119.9 1.5 %collective-permute-done.27 = bf16[272,256]{1,0:T(8,128)(2,1)S(1)} collective-permute-done((bf16[272,256]{1,0:T(8,128)(2,1)S(1)}, bf16[272,256]{1,0:T(8,128)(2,1)S(1)}, u32[]{:S(2)}, u32[]{:S(2)}) %collective-permute-start.27) | collective-permute-done | bytes 139296 | tf_op jit(solution)/shard_map/ppermute | solution.py:33
  121.4 4.7 %convolution_convert_fusion = bf16[256,3072]{1,0:T(8,128)(2,1)S(1)} fusion(bf16[3072,1024]{1,0:T(8,128)(2,1)} %copy-done.11, bf16[272,1024]{1,0:T(8,128)(2,1)S(1)} %constant_dynamic-update-slice_fusion), kind=kOutput, calls=%fused_computation.6 | convolution fusion | flops 1611399168 | bytes 8388608 | tf_op jit(solution)/shard_map/dot_general | solution.py:104
  126.5 0.6 collective-permute-start.28
  127.1 1.5 %collective-permute-done.28 = f32[128]{0:T(128)S(1)} collective-permute-done((f32[128]{0:T(128)S(1)}, f32[128]{0:T(128)S(1)}, u32[]{:S(2)}, u32[]{:S(2)}) %collective-permute-start.28) | collective-permute-done | bytes 544 | tf_op jit(solution)/shard_map/ppermute | solution.py:108
  128.6 2.9 %fusion.13 = (f32[128,3072]{1,0:T(8,128)}, f32[128,3072]{1,0:T(8,128)}) fusion(f32[128,3072]{1,0:T(8,128)S(1)} %get-tuple-element.70, bf16[128,3072]{1,0:T(8,128)(2,1)S(1)} %collective-permute-done.29, bf16[128,3072]{1,0:T(8,128)(2,1)S(1)} %copy-done.4, f32[128,3072]{1,0:T(8,128)S(1)} %copy-done, bf16[256,3072]{1,0:T(8,128)(2,1)S(1)} %convolution_convert_fusion, ...), kind=kLoop, calls=%fused_computation.29 | loop fusion | flops 8650752 | bytes 9454080 | tf_op jit(solution)/shard_map/sub | solution.py:129
  (132 shorter events, 3.8 us)
Async XLA Ops:
  0.6 2.9 %copy-start = (f32[128,3072]{1,0:T(8,128)S(1)}, f32[128,3072]{1,0:T(8,128)}, u32[]{:S(2)}) copy-start(f32[128,3072]{1,0:T(8,128)} %param.19) | copy-start | bytes 4718596
  0.6 2.9 %copy-start.5 = (f32[3072]{0:T(1024)S(1)}, f32[3072]{0:T(1024)}, u32[]{:S(2)}) copy-start(f32[3072]{0:T(1024)} %param.17) | copy-start | bytes 36868
  1.4 2.8 %copy-start.6 = (f32[1024]{0:T(1024)S(1)}, f32[1024]{0:T(1024)}, u32[]{:S(2)}) copy-start(f32[1024]{0:T(1024)} %param.18) | copy-start | bytes 12292
  1.4 4.0 %copy-start.10 = (s32[3072]{0:T(1024)S(1)}, s32[3072]{0:T(1024)}, u32[]{:S(2)}) copy-start(s32[3072]{0:T(1024)} %param.15) | copy-start | bytes 36868
  3.0 2.5 %collective-permute-start = (bf16[128,3072]{1,0:T(8,128)(2,1)S(1)}, bf16[128,3072]{1,0:T(8,128)(2,1)S(1)}, u32[]{:S(2)}, u32[]{:S(2)}) collective-permute-start(bf16[128,3072]{1,0:T(8,128)(2,1)S(1)} %select_convert_fusion), channel_id=1, source_target_pairs={{0,1},{1,0},{2,3},{3,2},{4,5},{5,4},{6,7},{7,6},{8,9},{9,8},{10,11... | collective-permute-start | bytes 2359304 | tf_op jit(solution)/shard_map/ppermute | solution.py:85
  4.3 6.3 %copy-start.9 = (bf16[2048,1024]{1,0:T(8,128)(2,1)S(1)}, bf16[2048,1024]{1,0:T(8,128)(2,1)}, u32[]{:S(2)}) copy-start(bf16[2048,1024]{1,0:T(8,128)(2,1)} %param.14) | copy-start | bytes 12582916
  13.3 8.0 %collective-permute-start.3 = (bf16[272,256]{1,0:T(8,128)(2,1)S(1)}, bf16[272,256]{1,0:T(8,128)(2,1)S(1)}, u32[]{:S(2)}, u32[]{:S(2)}) collective-permute-start(bf16[272,256]{1,0:T(8,128)(2,1)S(1)} %pad_maximum_fusion.2), channel_id=1, source_target_pairs={{0,6},{2,4},{4,2},{6,0},{8,14},{10,12},{12,10},{14,8},{16,22},{18,... | collective-permute-start | bytes 417800 | tf_op jit(solution)/shard_map/ppermute | solution.py:23
  17.2 6.9 %collective-permute-start.2 = (bf16[272,256]{1,0:T(8,128)(2,1)S(1)}, bf16[272,256]{1,0:T(8,128)(2,1)S(1)}, u32[]{:S(2)}, u32[]{:S(2)}) collective-permute-start(bf16[272,256]{1,0:T(8,128)(2,1)S(1)} %pad_maximum_fusion.1), channel_id=1, source_target_pairs={{0,4},{2,6},{4,0},{6,2},{8,12},{10,14},{12,8},{14,10},{16,20},{18,... | collective-permute-start | bytes 417800 | tf_op jit(solution)/shard_map/ppermute | solution.py:23
  17.8 6.6 %collective-permute-start.1 = (bf16[272,256]{1,0:T(8,128)(2,1)S(1)}, bf16[272,256]{1,0:T(8,128)(2,1)S(1)}, u32[]{:S(2)}, u32[]{:S(2)}) collective-permute-start(bf16[272,256]{1,0:T(8,128)(2,1)S(1)} %pad_maximum_fusion), channel_id=1, source_target_pairs={{0,2},{2,0},{4,6},{6,4},{8,10},{10,8},{12,14},{14,12},{16,18},{18,... | collective-permute-start | bytes 417800 | tf_op jit(solution)/shard_map/ppermute | solution.py:23
  24.8 6.4 %collective-permute-start.6 = (bf16[272,64]{1,0:T(8,128)(2,1)S(1)}, bf16[272,64]{1,0:T(8,128)(2,1)S(1)}, u32[]{:S(2)}, u32[]{:S(2)}) collective-permute-start(bf16[272,64]{1,0:T(8,128)(2,1)S(1)} %pad_maximum_fusion.8), channel_id=1, source_target_pairs={{0,24},{2,26},{4,28},{6,30},{8,16},{10,18},{12,20},{14,22},{16,8},... | collective-permute-start | bytes 104456 | tf_op jit(solution)/shard_map/ppermute | solution.py:23
  28.5 6.0 %collective-permute-start.5 = (bf16[272,64]{1,0:T(8,128)(2,1)S(1)}, bf16[272,64]{1,0:T(8,128)(2,1)S(1)}, u32[]{:S(2)}, u32[]{:S(2)}) collective-permute-start(bf16[272,64]{1,0:T(8,128)(2,1)S(1)} %pad_maximum_fusion.7), channel_id=1, source_target_pairs={{0,16},{2,18},{4,20},{6,22},{8,24},{10,26},{12,28},{14,30},{16,0},... | collective-permute-start | bytes 104456 | tf_op jit(solution)/shard_map/ppermute | solution.py:23
  28.6 6.0 %collective-permute-start.4 = (bf16[272,64]{1,0:T(8,128)(2,1)S(1)}, bf16[272,64]{1,0:T(8,128)(2,1)S(1)}, u32[]{:S(2)}, u32[]{:S(2)}) collective-permute-start(bf16[272,64]{1,0:T(8,128)(2,1)S(1)} %pad_maximum_fusion.6), channel_id=1, source_target_pairs={{0,8},{2,10},{4,12},{6,14},{8,0},{10,2},{12,4},{14,6},{16,24},{18,... | collective-permute-start | bytes 104456 | tf_op jit(solution)/shard_map/ppermute | solution.py:23
  34.7 4.8 %collective-permute-start.7 = (bf16[272,64]{1,0:T(8,128)(2,1)S(1)}, bf16[272,64]{1,0:T(8,128)(2,1)S(1)}, u32[]{:S(2)}, u32[]{:S(2)}) collective-permute-start(bf16[272,64]{1,0:T(8,128)(2,1)S(1)} %pad_maximum_fusion.9), channel_id=1, source_target_pairs={{0,8},{2,10},{4,12},{6,14},{8,0},{10,2},{12,4},{14,6},{16,24},{18,... | collective-permute-start | bytes 104456 | tf_op jit(solution)/shard_map/ppermute | solution.py:33
  35.8 6.9 %collective-permute-start.8 = (bf16[272,64]{1,0:T(8,128)(2,1)S(1)}, bf16[272,64]{1,0:T(8,128)(2,1)S(1)}, u32[]{:S(2)}, u32[]{:S(2)}) collective-permute-start(bf16[272,64]{1,0:T(8,128)(2,1)S(1)} %pad_maximum_fusion.9), channel_id=1, source_target_pairs={{0,16},{2,18},{4,20},{6,22},{8,24},{10,26},{12,28},{14,30},{16,0},... | collective-permute-start | bytes 104456 | tf_op jit(solution)/shard_map/ppermute | solution.py:33
  38.0 6.2 %collective-permute-start.9 = (bf16[272,64]{1,0:T(8,128)(2,1)S(1)}, bf16[272,64]{1,0:T(8,128)(2,1)S(1)}, u32[]{:S(2)}, u32[]{:S(2)}) collective-permute-start(bf16[272,64]{1,0:T(8,128)(2,1)S(1)} %pad_maximum_fusion.9), channel_id=1, source_target_pairs={{0,24},{2,26},{4,28},{6,30},{8,16},{10,18},{12,20},{14,22},{16,8},... | collective-permute-start | bytes 104456 | tf_op jit(solution)/shard_map/ppermute | solution.py:33
  44.8 20.5 %collective-permute-start.10 = (bf16[272,256]{1,0:T(8,128)(2,1)S(1)}, bf16[272,256]{1,0:T(8,128)(2,1)S(1)}, u32[]{:S(2)}, u32[]{:S(2)}) collective-permute-start(bf16[272,256]{1,0:T(8,128)(2,1)S(1)} %dynamic_update_slice.51), channel_id=1, source_target_pairs={{0,2},{2,0},{4,6},{6,4},{8,10},{10,8},{12,14},{14,12},{16,18},{18,... | collective-permute-start | bytes 417800 | tf_op jit(solution)/shard_map/ppermute | solution.py:33
  63.0 8.5 %copy-start.11 = (bf16[3072,1024]{1,0:T(8,128)(2,1)}, bf16[3072,1024]{1,0:T(8,128)(2,1)S(1)}, u32[]{:S(2)}) copy-start(bf16[3072,1024]{1,0:T(8,128)(2,1)S(1)} %fusion.4) | copy-start | bytes 18874372
  63.0 6.6 %collective-permute-start.11 = (bf16[272,256]{1,0:T(8,128)(2,1)S(1)}, bf16[272,256]{1,0:T(8,128)(2,1)S(1)}, u32[]{:S(2)}, u32[]{:S(2)}) collective-permute-start(bf16[272,256]{1,0:T(8,128)(2,1)S(1)} %dynamic_update_slice.51), channel_id=1, source_target_pairs={{0,4},{2,6},{4,0},{6,2},{8,12},{10,14},{12,8},{14,10},{16,20},{18,... | collective-permute-start | bytes 417800 | tf_op jit(solution)/shard_map/ppermute | solution.py:33
  63.5 6.2 %collective-permute-start.12 = (bf16[272,256]{1,0:T(8,128)(2,1)S(1)}, bf16[272,256]{1,0:T(8,128)(2,1)S(1)}, u32[]{:S(2)}, u32[]{:S(2)}) collective-permute-start(bf16[272,256]{1,0:T(8,128)(2,1)S(1)} %dynamic_update_slice.51), channel_id=1, source_target_pairs={{0,6},{2,4},{4,2},{6,0},{8,14},{10,12},{12,10},{14,8},{16,22},{18,... | collective-permute-start | bytes 417800 | tf_op jit(solution)/shard_map/ppermute | solution.py:33
  71.6 3.9 %copy-start.1 = (bf16[256,3072]{1,0:T(8,128)(2,1)}, bf16[256,3072]{1,0:T(8,128)(2,1)S(1)}, u32[]{:S(2)}) copy-start(bf16[256,3072]{1,0:T(8,128)(2,1)S(1)} %convolution_convert_fusion.1) | copy-start | bytes 4718596
  71.6 2.9 %collective-permute-start.14 = (bf16[128,3072]{1,0:T(8,128)(2,1)S(1)}, bf16[128,3072]{1,0:T(8,128)(2,1)S(1)}, u32[]{:S(2)}, u32[]{:S(2)}) collective-permute-start(bf16[128,3072]{1,0:T(8,128)(2,1)S(1)} %slice.452), channel_id=1, source_target_pairs={{0,1},{1,0},{2,3},{3,2},{4,5},{5,4},{6,7},{7,6},{8,9},{9,8},{10,11... | collective-permute-start | bytes 2359304 | tf_op jit(solution)/shard_map/ppermute | solution.py:109
  71.9 2.0 %collective-permute-start.13 = (f32[128]{0:T(128)S(1)}, f32[128]{0:T(128)S(1)}, u32[]{:S(2)}, u32[]{:S(2)}) collective-permute-start(f32[128]{0:T(128)S(1)} %slice.374), channel_id=1, source_target_pairs={{0,1},{1,0},{2,3},{3,2},{4,5},{5,4},{6,7},{7,6},{8,9},{9,8},{10,11... | collective-permute-start | bytes 1544 | tf_op jit(solution)/shard_map/ppermute | solution.py:108
  74.0 0.5 copy-start.7
  74.5 0.9 copy-start.3
  76.4 2.6 %collective-permute-start.15 = (bf16[128,3072]{1,0:T(8,128)(2,1)}, bf16[128,3072]{1,0:T(8,128)(2,1)}, u32[]{:S(2)}, u32[]{:S(2)}) collective-permute-start(bf16[128,3072]{1,0:T(8,128)(2,1)} %convert_element_type.353), channel_id=1, source_target_pairs={{0,1},{1,0},{2,3},{3,2},{4,5},{5,4},{6,7},{7,6},{8,9},{9,8},{10,11... | collective-permute-start | bytes 2359304 | tf_op jit(solution)/shard_map/ppermute | solution.py:85
  84.3 7.5 %collective-permute-start.18 = (bf16[272,256]{1,0:T(8,128)(2,1)S(1)}, bf16[272,256]{1,0:T(8,128)(2,1)S(1)}, u32[]{:S(2)}, u32[]{:S(2)}) collective-permute-start(bf16[272,256]{1,0:T(8,128)(2,1)S(1)} %pad_maximum_fusion.5), channel_id=1, source_target_pairs={{0,6},{2,4},{4,2},{6,0},{8,14},{10,12},{12,10},{14,8},{16,22},{18,... | collective-permute-start | bytes 417800 | tf_op jit(solution)/shard_map/ppermute | solution.py:23
  85.9 8.1 %collective-permute-start.17 = (bf16[272,256]{1,0:T(8,128)(2,1)S(1)}, bf16[272,256]{1,0:T(8,128)(2,1)S(1)}, u32[]{:S(2)}, u32[]{:S(2)}) collective-permute-start(bf16[272,256]{1,0:T(8,128)(2,1)S(1)} %pad_maximum_fusion.4), channel_id=1, source_target_pairs={{0,4},{2,6},{4,0},{6,2},{8,12},{10,14},{12,8},{14,10},{16,20},{18,... | collective-permute-start | bytes 417800 | tf_op jit(solution)/shard_map/ppermute | solution.py:23
  87.4 6.7 %collective-permute-start.16 = (bf16[272,256]{1,0:T(8,128)(2,1)S(1)}, bf16[272,256]{1,0:T(8,128)(2,1)S(1)}, u32[]{:S(2)}, u32[]{:S(2)}) collective-permute-start(bf16[272,256]{1,0:T(8,128)(2,1)S(1)} %pad_maximum_fusion.3), channel_id=1, source_target_pairs={{0,2},{2,0},{4,6},{6,4},{8,10},{10,8},{12,14},{14,12},{16,18},{18,... | collective-permute-start | bytes 417800 | tf_op jit(solution)/shard_map/ppermute | solution.py:23
  94.4 6.9 %collective-permute-start.21 = (bf16[272,64]{1,0:T(8,128)(2,1)S(1)}, bf16[272,64]{1,0:T(8,128)(2,1)S(1)}, u32[]{:S(2)}, u32[]{:S(2)}) collective-permute-start(bf16[272,64]{1,0:T(8,128)(2,1)S(1)} %pad_maximum_fusion.12), channel_id=1, source_target_pairs={{0,24},{2,26},{4,28},{6,30},{8,16},{10,18},{12,20},{14,22},{16,8},... | collective-permute-start | bytes 104456 | tf_op jit(solution)/shard_map/ppermute | solution.py:23
  96.1 7.3 %collective-permute-start.20 = (bf16[272,64]{1,0:T(8,128)(2,1)S(1)}, bf16[272,64]{1,0:T(8,128)(2,1)S(1)}, u32[]{:S(2)}, u32[]{:S(2)}) collective-permute-start(bf16[272,64]{1,0:T(8,128)(2,1)S(1)} %pad_maximum_fusion.11), channel_id=1, source_target_pairs={{0,16},{2,18},{4,20},{6,22},{8,24},{10,26},{12,28},{14,30},{16,0},... | collective-permute-start | bytes 104456 | tf_op jit(solution)/shard_map/ppermute | solution.py:23
  96.2 7.2 %collective-permute-start.19 = (bf16[272,64]{1,0:T(8,128)(2,1)S(1)}, bf16[272,64]{1,0:T(8,128)(2,1)S(1)}, u32[]{:S(2)}, u32[]{:S(2)}) collective-permute-start(bf16[272,64]{1,0:T(8,128)(2,1)S(1)} %pad_maximum_fusion.10), channel_id=1, source_target_pairs={{0,8},{2,10},{4,12},{6,14},{8,0},{10,2},{12,4},{14,6},{16,24},{18,... | collective-permute-start | bytes 104456 | tf_op jit(solution)/shard_map/ppermute | solution.py:23
  103.6 5.4 %collective-permute-start.22 = (bf16[272,64]{1,0:T(8,128)(2,1)S(1)}, bf16[272,64]{1,0:T(8,128)(2,1)}, u32[]{:S(2)}, u32[]{:S(2)}) collective-permute-start(bf16[272,64]{1,0:T(8,128)(2,1)S(1)} %pad_maximum_fusion.13), channel_id=1, source_target_pairs={{0,8},{2,10},{4,12},{6,14},{8,0},{10,2},{12,4},{14,6},{16,24},{18,... | collective-permute-start | bytes 104456 | tf_op jit(solution)/shard_map/ppermute | solution.py:33
  103.7 8.8 %collective-permute-start.23 = (bf16[272,64]{1,0:T(8,128)(2,1)S(1)}, bf16[272,64]{1,0:T(8,128)(2,1)S(1)}, u32[]{:S(2)}, u32[]{:S(2)}) collective-permute-start(bf16[272,64]{1,0:T(8,128)(2,1)S(1)} %pad_maximum_fusion.13), channel_id=1, source_target_pairs={{0,16},{2,18},{4,20},{6,22},{8,24},{10,26},{12,28},{14,30},{16,0},... | collective-permute-start | bytes 104456 | tf_op jit(solution)/shard_map/ppermute | solution.py:33
  106.1 6.7 %collective-permute-start.24 = (bf16[272,64]{1,0:T(8,128)(2,1)S(1)}, bf16[272,64]{1,0:T(8,128)(2,1)S(1)}, u32[]{:S(2)}, u32[]{:S(2)}) collective-permute-start(bf16[272,64]{1,0:T(8,128)(2,1)S(1)} %pad_maximum_fusion.13), channel_id=1, source_target_pairs={{0,24},{2,26},{4,28},{6,30},{8,16},{10,18},{12,20},{14,22},{16,8},... | collective-permute-start | bytes 104456 | tf_op jit(solution)/shard_map/ppermute | solution.py:33
  113.4 6.1 %collective-permute-start.25 = (bf16[272,256]{1,0:T(8,128)(2,1)S(1)}, bf16[272,256]{1,0:T(8,128)(2,1)S(1)}, u32[]{:S(2)}, u32[]{:S(2)}) collective-permute-start(bf16[272,256]{1,0:T(8,128)(2,1)S(1)} %dynamic_update_slice.59), channel_id=1, source_target_pairs={{0,2},{2,0},{4,6},{6,4},{8,10},{10,8},{12,14},{14,12},{16,18},{18,... | collective-permute-start | bytes 417800 | tf_op jit(solution)/shard_map/ppermute | solution.py:33
  114.8 5.1 %collective-permute-start.26 = (bf16[272,256]{1,0:T(8,128)(2,1)S(1)}, bf16[272,256]{1,0:T(8,128)(2,1)S(1)}, u32[]{:S(2)}, u32[]{:S(2)}) collective-permute-start(bf16[272,256]{1,0:T(8,128)(2,1)S(1)} %dynamic_update_slice.59), channel_id=1, source_target_pairs={{0,4},{2,6},{4,0},{6,2},{8,12},{10,14},{12,8},{14,10},{16,20},{18,... | collective-permute-start | bytes 417800 | tf_op jit(solution)/shard_map/ppermute | solution.py:33
  115.4 6.0 %collective-permute-start.27 = (bf16[272,256]{1,0:T(8,128)(2,1)S(1)}, bf16[272,256]{1,0:T(8,128)(2,1)S(1)}, u32[]{:S(2)}, u32[]{:S(2)}) collective-permute-start(bf16[272,256]{1,0:T(8,128)(2,1)S(1)} %dynamic_update_slice.59), channel_id=1, source_target_pairs={{0,6},{2,4},{4,2},{6,0},{8,14},{10,12},{12,10},{14,8},{16,22},{18,... | collective-permute-start | bytes 417800 | tf_op jit(solution)/shard_map/ppermute | solution.py:33
  121.4 7.2 %copy-start.4 = (bf16[128,3072]{1,0:T(8,128)(2,1)S(1)}, bf16[128,3072]{1,0:T(8,128)(2,1)}, u32[]{:S(2)}) copy-start(bf16[128,3072]{1,0:T(8,128)(2,1)} %copy-done.3) | copy-start | bytes 2359300
  126.1 2.4 %copy-start.8 = (f32[128]{0:T(128)S(1)}, f32[128]{0:T(128)}, u32[]{:S(2)}) copy-start(f32[128]{0:T(128)} %copy-done.7) | copy-start | bytes 1540
  126.1 2.5 %copy-start.2 = (bf16[256,3072]{1,0:T(8,128)(2,1)S(1)}, bf16[256,3072]{1,0:T(8,128)(2,1)}, u32[]{:S(2)}) copy-start(bf16[256,3072]{1,0:T(8,128)(2,1)} %copy-done.1) | copy-start | bytes 4718596
  126.2 2.4 %collective-permute-start.29 = (bf16[128,3072]{1,0:T(8,128)(2,1)S(1)}, bf16[128,3072]{1,0:T(8,128)(2,1)S(1)}, u32[]{:S(2)}, u32[]{:S(2)}) collective-permute-start(bf16[128,3072]{1,0:T(8,128)(2,1)S(1)} %slice.485), channel_id=1, source_target_pairs={{0,1},{1,0},{2,3},{3,2},{4,5},{5,4},{6,7},{7,6},{8,9},{9,8},{10,11... | collective-permute-start | bytes 2359304 | tf_op jit(solution)/shard_map/ppermute | solution.py:109
  126.5 2.0 %collective-permute-start.28 = (f32[128]{0:T(128)S(1)}, f32[128]{0:T(128)S(1)}, u32[]{:S(2)}, u32[]{:S(2)}) collective-permute-start(f32[128]{0:T(128)S(1)} %slice.415), channel_id=1, source_target_pairs={{0,1},{1,0},{2,3},{3,2},{4,5},{5,4},{6,7},{7,6},{8,9},{9,8},{10,11... | collective-permute-start | bytes 1544 | tf_op jit(solution)/shard_map/ppermute | solution.py:108
